TPU v7x, 256 devices: a whole 4x4x8 slice. The times are simulated.
256 devices in a mesh: ctx: 32 (over z, y), dp: 8 (over x, core).
Axes of the slice: x: 4, y: 4, z: 8, core: 2. Of those that a mesh axis runs over, the one named last changes fastest.
Arguments:
- query: bfloat16 [65536, 128], P(('dp', 'ctx')), parts along dimension 0, may hold values from -6 to 6
- key: bfloat16 [65536, 128], P(('dp', 'ctx')), parts along dimension 0, may hold values from -6 to 6
- value_in: bfloat16 [65536, 1024], P(('dp', 'ctx')), parts along dimension 0, may hold values from -6 to 6
- gate: bfloat16 [65536, 1024], P(('dp', 'ctx')), parts along dimension 0, may hold values from -6 to 6
- conv_weight: bfloat16 [3, 1024], replicated, may hold values from -3 to 3
- doc_lengths: int32 [256], P('dp'), parts along dimension 0, may hold values from 1 to 4096, 8192 in all
- d_out: bfloat16 [65536, 1024], P(('dp', 'ctx')), parts along dimension 0, may hold values from -6 to 6
Outputs:
- mixed: bfloat16 [65536, 1024], P(('dp', 'ctx')), parts along dimension 0
- grad_query: bfloat16 [65536, 128], P(('dp', 'ctx')), parts along dimension 0
- grad_key: bfloat16 [65536, 128], P(('dp', 'ctx')), parts along dimension 0
- grad_value: bfloat16 [65536, 1024], P(('dp', 'ctx')), parts along dimension 0
- grad_gate: bfloat16 [65536, 1024], P(('dp', 'ctx')), parts along dimension 0
There are 8 independent parts, one for each index of `dp`. A program takes and returns all parts, laid end to end along the dimension named above; an argument that names none is the same for every part. Nothing has to cross between parts.
Inputs may be any that keep to these rules, and one draw needn't show every extreme that they name: `doc_lengths`: the 32 lengths sum to 8192; the longest is exactly 4096.
All inputs are finite; a program needn't handle non-finite values.
Results may differ from a plain program's by a relative error of at most 0.005.
Values may be sent and summed in bfloat16 or wider, within the bound.
No kernel may reach another device: no remote copies, remote signals or barrier semaphores. Data moves between devices by JAX's collectives and lax.ppermute only.
A program may use at most 128 MiB of HBM per device.

v0:
```python
import math

import jax
import numpy as np
import jax.numpy as jnp
from jax import lax
from jax.sharding import PartitionSpec as P

HEADS = 8
KD = 16
VD = 128
CONV = 3


highest = lax.Precision.HIGHEST
quad_scale = 1.0 / (4.0 * math.sqrt(2.0))


def shifted(block, axis, distance):
    devices = range(lax.axis_size(axis))
    route = [(i - distance, i) for i in devices if i - distance in devices]
    return lax.ppermute(block, axis, route)


def document_ids(lengths, positions):
    ends = jnp.cumsum(lengths, dtype=jnp.int32)
    counted = jnp.sum((ends[None, :] <= positions[:, None]).astype(jnp.int32), axis=1)
    return jnp.where(positions < 0, jnp.int32(-1), counted)


def pair_tables(width):
    rows, cols = np.triu_indices(width)
    weight = np.where(rows == cols, quad_scale, quad_scale * math.sqrt(2.0)).astype(np.float32)
    place = np.zeros((width, width), np.int32)
    place[rows, cols] = np.arange(rows.size)
    place[cols, rows] = np.arange(rows.size)
    spread_weight = np.where(np.eye(width, dtype=bool), 2.0, 1.0) * weight[place]
    return rows, cols, weight, place.reshape(-1), spread_weight.astype(np.float32).reshape(-1)


def feature_rows(values):
    spread = jnp.transpose(values, (1, 2, 0))
    head_count, width, token_count = spread.shape
    rows, cols, weight, _, _ = pair_tables(width)
    ones_row = jnp.ones((head_count, 1, token_count), jnp.float32)
    pieces = []
    for i in range(width):
        pieces.append(spread[:, i : i + 1, :] * spread[:, i:, :])
    outer = jnp.concatenate(pieces, axis=1) * jnp.asarray(weight)[None, :, None]
    return (jnp.concatenate([ones_row, 0.5 * spread, outer], axis=1), spread)


def feature_grad(grad_phi, spread):
    head_count, width, token_count = spread.shape
    _, _, _, place, spread_weight = pair_tables(width)
    linear = 0.5 * grad_phi[:, 1 : 1 + width]
    quad = grad_phi[:, 1 + width :]
    paired = jnp.take(quad, jnp.asarray(place), axis=1) * jnp.asarray(spread_weight)[None, :, None]
    paired = paired.reshape(head_count, width, width, token_count)
    return linear + jnp.einsum("hijt,hjt->hit", paired, spread, precision=highest)


def block_flags(doc_lengths, devices, rows):
    firsts = jnp.arange(devices, dtype=jnp.int32) * rows
    prev_docs = document_ids(doc_lengths, firsts - 1)
    first_docs = document_ids(doc_lengths, firsts)
    last_docs = document_ids(doc_lengths, firsts + rows - 1)
    next_docs = document_ids(doc_lengths, firsts + rows)
    return (last_docs != prev_docs).astype(jnp.int32), (first_docs != next_docs).astype(jnp.int32)


def scan_masks(restart, closes):
    devices = restart.shape[0]
    order = jnp.arange(devices, dtype=jnp.int32)
    target = order[:, None]
    source = order[None, :]
    restarts_upto = jnp.cumsum(restart)
    closes_upto = jnp.cumsum(closes)
    gap_fwd = restarts_upto[jnp.maximum(target - 1, 0)] - restarts_upto[source]
    forward = (source < target) & (gap_fwd == 0)
    gap_bwd = closes_upto[jnp.maximum(source - 1, 0)] - closes_upto[target]
    backward = (source > target) & (gap_bwd == 0)
    return forward.astype(jnp.float32), backward.astype(jnp.float32)


def state_scan(local_state, local_norm, mask):
    devices = mask.shape[0]
    heads, feats, width = local_state.shape
    state_rows = heads * feats
    norm_rows = -(-(heads * feats) // width)
    total_rows = -(-(state_rows + norm_rows) // devices) * devices
    flat_norm = jnp.pad(local_norm.reshape(-1), (0, norm_rows * width - heads * feats))
    packed = jnp.concatenate(
        [
            local_state.reshape(state_rows, width),
            flat_norm.reshape(norm_rows, width),
            jnp.zeros((total_rows - state_rows - norm_rows, width), jnp.float32),
        ],
        axis=0,
    ).reshape(devices, total_rows // devices, width)
    chunks = lax.all_to_all(packed, "ctx", 0, 0, tiled=True)
    summed = jnp.einsum("ij,jrc->irc", mask, chunks, precision=highest)
    back = lax.all_to_all(summed, "ctx", 0, 0, tiled=True).reshape(total_rows, width)
    state_in = back[:state_rows].reshape(heads, feats, width)
    norm_in = back[state_rows : state_rows + norm_rows].reshape(-1)[: heads * feats]
    return (state_in, norm_in.reshape(heads, feats))


def local(query, key, value_in, gate, conv_weight, doc_lengths, d_out):
    tok_rows = query.shape[0]
    channels = value_in.shape[1]
    dev_index = lax.axis_index("ctx")
    first_pos = dev_index * tok_rows
    local_pos = jnp.arange(tok_rows, dtype=jnp.int32)
    doc_ids = document_ids(doc_lengths, first_pos + local_pos)
    edge_docs = document_ids(doc_lengths, first_pos + jnp.array([-1, tok_rows], jnp.int32))
    prev_doc = edge_docs[0]
    next_doc = edge_docs[1]
    before_ids = document_ids(
        doc_lengths, first_pos - (CONV - 1) + jnp.arange(CONV - 1, dtype=jnp.int32)
    )
    after_ids = document_ids(
        doc_lengths, first_pos + tok_rows + jnp.arange(CONV - 1, dtype=jnp.int32)
    )
    taps = conv_weight.astype(jnp.float32)
    earlier = shifted(value_in[tok_rows - (CONV - 1) :], "ctx", 1)
    extended = jnp.concatenate([earlier, value_in], axis=0)
    extended_ids = jnp.concatenate([before_ids, doc_ids], axis=0)
    convolved = jnp.zeros((tok_rows, channels), jnp.float32)
    for offset in range(CONV):
        lower_row = CONV - 1 - offset
        keep = (extended_ids[lower_row : lower_row + tok_rows] == doc_ids).astype(jnp.float32)
        convolved = (
            convolved
            + taps[offset][None, :]
            * extended[lower_row : lower_row + tok_rows].astype(jnp.float32)
            * keep[:, None]
        )
    opening = jax.nn.sigmoid(gate.astype(jnp.float32))
    value_rows = (convolved * opening).astype(jnp.bfloat16)
    q_float = query.astype(jnp.float32).reshape(tok_rows, HEADS, KD)
    k_float = key.astype(jnp.float32).reshape(tok_rows, HEADS, KD)
    v_float = value_rows.astype(jnp.float32).reshape(tok_rows, HEADS, VD)
    scores = jnp.einsum("thd,shd->hts", q_float, k_float, precision=highest) * 0.25
    kernel = 1.0 + scores + 0.5 * scores * scores
    allowed = (local_pos[:, None] >= local_pos[None, :]) & (doc_ids[:, None] == doc_ids[None, :])
    weights = jnp.where(allowed[None], kernel, 0.0)
    numerator = jnp.einsum("hts,shv->thv", weights, v_float, precision=highest)
    denominator = jnp.transpose(jnp.sum(weights, axis=2), (1, 0))
    phi_query, spread_query = feature_rows(q_float)
    phi_key, spread_key = feature_rows(k_float)
    last_mask = (doc_ids == doc_ids[tok_rows - 1]).astype(jnp.float32)
    masked_key = phi_key * last_mask[None, None, :]
    local_state = jnp.einsum("hft,thv->hfv", masked_key, v_float, precision=highest)
    local_norm = jnp.sum(masked_key, axis=2)
    restart_all, closes_all = block_flags(doc_lengths, lax.axis_size("ctx"), tok_rows)
    forward_mask, backward_mask = scan_masks(restart_all, closes_all)
    state_in, norm_in = state_scan(local_state, local_norm, forward_mask)
    inside = (doc_ids == prev_doc).astype(jnp.float32)
    numerator = numerator + inside[:, None, None] * jnp.einsum(
        "hft,hfv->thv", phi_query, state_in, precision=highest
    )
    denominator = denominator + inside[:, None] * jnp.einsum(
        "hft,hf->th", phi_query, norm_in, precision=highest
    )
    attended = numerator / denominator[:, :, None]
    mixed = attended.reshape(tok_rows, HEADS * VD).astype(jnp.bfloat16)
    upstream = d_out.astype(jnp.float32).reshape(tok_rows, HEADS, VD)
    grad_num = upstream / denominator[:, :, None]
    grad_den = -jnp.sum(upstream * attended, axis=2) / denominator
    first_mask = (doc_ids == doc_ids[0]).astype(jnp.float32)
    masked_query = phi_query * first_mask[None, None, :]
    back_state = jnp.einsum("hft,thv->hfv", masked_query, grad_num, precision=highest)
    back_norm = jnp.einsum("hft,th->hf", masked_query, grad_den, precision=highest)
    grad_state_in, grad_norm_in = state_scan(back_state, back_norm, backward_mask)
    outside = (doc_ids == next_doc).astype(jnp.float32)
    grad_v = jnp.einsum("hts,thv->shv", weights, grad_num, precision=highest)
    grad_v = grad_v + outside[:, None, None] * jnp.einsum(
        "hfs,hfv->shv", phi_key, grad_state_in, precision=highest
    )
    grad_weights = (
        jnp.einsum("thv,shv->hts", grad_num, v_float, precision=highest)
        + jnp.transpose(grad_den, (1, 0))[:, :, None]
    )
    grad_scores = jnp.where(allowed[None], grad_weights * (1.0 + scores), 0.0)
    grad_q = jnp.einsum("hts,shd->thd", grad_scores, k_float, precision=highest) * 0.25
    grad_k = jnp.einsum("hts,thd->shd", grad_scores, q_float, precision=highest) * 0.25
    grad_phi_query = inside[None, None, :] * (
        jnp.einsum("hfv,thv->hft", state_in, grad_num, precision=highest)
        + norm_in[:, :, None] * jnp.transpose(grad_den, (1, 0))[:, None, :]
    )
    grad_phi_key = outside[None, None, :] * (
        jnp.einsum("hfv,shv->hfs", grad_state_in, v_float, precision=highest)
        + grad_norm_in[:, :, None]
    )
    grad_q = grad_q + jnp.transpose(feature_grad(grad_phi_query, spread_query), (2, 0, 1))
    grad_k = grad_k + jnp.transpose(feature_grad(grad_phi_key, spread_key), (2, 0, 1))
    grad_query = grad_q.reshape(tok_rows, HEADS * KD).astype(jnp.bfloat16)
    grad_key = grad_k.reshape(tok_rows, HEADS * KD).astype(jnp.bfloat16)
    grad_core = grad_v.reshape(tok_rows, channels)
    grad_gate = (grad_core * convolved * opening * (1.0 - opening)).astype(jnp.bfloat16)
    grad_conv = grad_core * opening
    later_rows = shifted(grad_conv[: CONV - 1], "ctx", -1)
    ahead = jnp.concatenate([grad_conv, later_rows], axis=0)
    ahead_ids = jnp.concatenate([doc_ids, after_ids], axis=0)
    grad_value = jnp.zeros((tok_rows, channels), jnp.float32)
    for offset in range(CONV):
        keep = (ahead_ids[offset : offset + tok_rows] == doc_ids).astype(jnp.float32)
        grad_value = (
            grad_value + taps[offset][None, :] * ahead[offset : offset + tok_rows] * keep[:, None]
        )
    return (mixed, grad_query, grad_key, grad_value.astype(jnp.bfloat16), grad_gate)


def solution(mesh):
    placed = (
        P(("dp", "ctx"), None),
        P(("dp", "ctx"), None),
        P(("dp", "ctx"), None),
        P(("dp", "ctx"), None),
        P(),
        P("dp"),
        P(("dp", "ctx"), None),
    )
    return jax.shard_map(
        local,
        mesh=mesh,
        in_specs=placed,
        out_specs=(
            P(("dp", "ctx"), None),
            P(("dp", "ctx"), None),
            P(("dp", "ctx"), None),
            P(("dp", "ctx"), None),
            P(("dp", "ctx"), None),
        ),
        check_vma=False,
    )
```

profile of v0, /device:TPU:32, one launch (start us, length us, event | category | flops | bytes accessed | tf_op | source)
XLA Modules:
  0.0 193.4 jit_solution(7439477420320445533)
XLA Ops:
  0.6 1.3 slice.268
  2.0 3.5 %collective-permute-start = (bf16[2,1024]{1,0:T(2,128)(2,1)}, bf16[2,1024]{1,0:T(2,128)(2,1)}, u32[]{:S(2)}, u32[]{:S(2)}) collective-permute-start(bf16[2,1024]{1,0:T(2,128)(2,1)} %slice.268), channel_id=1, source_target_pairs={{0,8},{8,16},{16,24},{24,32},{32,40},{40,48},{48,56},{56,64},{64,7... | collective-permute-start | bytes 12296 | tf_op jit(solution)/shard_map/ppermute | solution.py:22
  5.4 0.9 copy.102
  6.5 0.9 copy.101
  8.2 0.8 fusion.87
  9.1 0.7 copy.100
  11.6 1.2 compare_convert_fusion.5
  17.3 0.7 slice_multiply_fusion.15
  21.4 0.7 convert_multiply_fusion
  22.1 0.7 broadcast_multiply_fusion.4
  24.0 4.0 %concatenate.35 = f32[8,136,256]{2,1,0:T(8,128)S(1)} concatenate(f32[8,16,256]{2,1,0:T(8,128)S(1)} %get-tuple-element.40, f32[8,15,256]{2,1,0:T(8,128)S(1)} %slice_multiply_fusion.8, f32[8,14,256]{2,1,0:T(8,128)S(1)} %slice_multiply_fusion.7, f32[8,13,256]{2,1,0:T(8,128)S(1)} %slice_multiply_fusion.6, f32[8,12,256]{2,1,0:T(8,128)S(1)} %slice_multiply_fusion.5, ...), dimensions={1} | concatenate | bytes 2228224 | tf_op jit(solution)/shard_map/concatenate | solution.py:49
  28.1 5.8 %concatenate.32 = f32[8,136,256]{2,1,0:T(8,128)S(1)} concatenate(f32[8,16,256]{2,1,0:T(8,128)} %get-tuple-element.57, f32[8,15,256]{2,1,0:T(8,128)S(1)} %copy-done.21, f32[8,14,256]{2,1,0:T(8,128)S(1)} %slice_multiply_fusion.14, f32[8,13,256]{2,1,0:T(8,128)S(1)} %slice_multiply_fusion.13, f32[8,12,256]{2,1,0:T(8,128)S(1)} %slice_multiply_fusion.12, ...), dimensions={1} | concatenate | bytes 2228224 | tf_op jit(solution)/shard_map/concatenate | solution.py:49
  33.9 2.0 %broadcast_multiply_fusion = (f32[8,136,256]{2,1,0:T(8,128)}, f32[8,136,256]{2,1,0:T(8,128)S(1)}) fusion(f32[8,136,256]{2,1,0:T(8,128)S(1)} %concatenate.35, f32[136]{0:T(256)} %constant.85.clone, f32[8,136,256]{2,1,0:T(8,128)S(1)} %concatenate.32), kind=kLoop, calls=%fused_computation.64 | loop fusion | flops 557056 | bytes 4456992 | tf_op jit(solution)/shard_map/mul | solution.py:49
  35.9 2.4 %compare_convert_fusion.1 = (f32[256]{0:T(256)}, f32[256]{0:T(256)}, f32[256]{0:T(256)S(1)}, f32[256]{0:T(256)S(1)}, f32[256]{0:T(256)S(1)}, /*index=5*/f32[256]{0:T(256)S(1)}, f32[256]{0:T(256)S(1)}) fusion(s32[256]{0:T(256)S(1)} %get-tuple-element.34, s32[258]{0:T(512)S(1)} %copy-done.32, s32[]{:T(128)} %bitcast.42, s32[]{:T(128)} %bitcast.16, ...), kind=kLoop, calls=%fused_computation.192 | loop fusion | flops 3584 | bytes 12300 | tf_op jit(solution)/shard_map/convert_element_type | solution.py:208
  39.0 1.5 fusion.39
  40.5 1.8 fusion.10
  42.3 1.1 reshape.395
  43.8 0.9 reshape.398
  44.7 11.1 %all-to-all-start = ((f32[32,39,128]{2,1,0:T(8,128)}), f32[32,39,128]{2,1,0:T(8,128)S(1)}, u32[]{:S(2)}, u32[]{:S(2)}) async-start(f32[32,39,128]{2,1,0:T(8,128)} %reshape.398), calls=%async_computation | async-start | bytes 1310720 | tf_op jit(solution)/shard_map/all_to_all | solution.py:101
  56.3 0.7 gather_fusion.1
  57.0 0.7 gather_fusion
  57.7 17.5 %all-to-all-done = f32[32,39,128]{2,1,0:T(8,128)S(1)} async-done(((f32[32,39,128]{2,1,0:T(8,128)}), f32[32,39,128]{2,1,0:T(8,128)S(1)}, u32[]{:S(2)}, u32[]{:S(2)}) %all-to-all-start) | async-done | bytes 639008 | tf_op jit(solution)/shard_map/all_to_all | solution.py:101
  75.7 1.2 copy.108
  76.9 5.6 %all-to-all-start.1 = ((f32[32,39,128]{2,1,0:T(8,128)}), f32[32,39,128]{2,1,0:T(8,128)S(1)}, u32[]{:S(2)}, u32[]{:S(2)}) async-start(f32[32,39,128]{2,1,0:T(8,128)} %copy.108), calls=%async_computation.1 | async-start | bytes 1310720 | tf_op jit(solution)/shard_map/all_to_all | solution.py:103
  82.5 1.2 copy.109
  83.8 0.8 fusion.36
  84.6 1.3 copy-done.40
  86.0 2.4 %fusion.37 = f32[8,128,256]{2,1,0:T(8,128)} fusion(f32[8,256,256]{1,2,0:T(8,128)S(1)} %get-tuple-element.96, pred[256,256]{0,1:T(8,128)(4,1)S(1)} %fusion.48, bf16[32,8,8,128]{3,2,1,0:T(8,128)(2,1)S(1)} %fusion.39), kind=kOutput, calls=%fused_computation.68 | convolution fusion | flops 808452096 | bytes 3735552 | tf_op jit(solution)/shard_map/hts,shv->thv/dot_general | solution.py:148
  88.4 12.9 %all-to-all-done.1 = f32[32,39,128]{2,1,0:T(8,128)S(1)} async-done(((f32[32,39,128]{2,1,0:T(8,128)}), f32[32,39,128]{2,1,0:T(8,128)S(1)}, u32[]{:S(2)}, u32[]{:S(2)}) %all-to-all-start.1) | async-done | bytes 639008 | tf_op jit(solution)/shard_map/all_to_all | solution.py:103
  101.5 0.9 reshape.400
  102.4 2.2 %fusion.84 = f32[8,1,256]{2,1,0:T(1,128)S(1)} fusion(f32[8,153,1]{1,2,0:T(1,128)S(1)} %reshape.485, f32[8,136,256]{2,1,0:T(8,128)} %get-tuple-element.91, f32[8,16,256]{2,1,0:T(8,128)S(1)} %copy-done.24, f32[153]{0:T(256)S(1)} %copy-done.30), kind=kOutput, calls=%fused_computation.239 | convolution fusion | flops 4386816 | bytes 1258884 | tf_op jit(solution)/shard_map/hft,hf->th/dot_general | solution.py:163
  104.7 2.4 %fusion.8 = f32[8,153,128]{2,1,0:T(8,128)} fusion(f32[256]{0:T(256)S(1)} %get-tuple-element.80, f32[8,136,256]{2,1,0:T(8,128)S(1)} %copy-done.15, f32[8,16,256]{2,1,0:T(8,128)S(1)} %copy-done.24, f32[153]{0:T(256)S(1)} %copy-done.30, f32[256,8,128]{0,2,1:T(8,128)S(1)} %bitcast.212, f32[256,8]{0,1:T(8,128)S(1)} %fusion.67), kind=kOutput, calls=%fused_computation.26 | convolution fusion | flops 482498560 | bytes 2930276 | tf_op jit(solution)/shard_map/hft,thv->hfv/dot_general | solution.py:173
  107.1 1.1 reshape.407
  108.2 4.2 %multiply_reduce_fusion.3 = (f32[256,8]{0,1:T(8,128)S(1)}, bf16[256,8,128]{0,2,1:T(8,128)(2,1)S(1)}) fusion(f32[256,1024]{0,1:T(8,128)} %copy.109, f32[256,8]{0,1:T(8,128)S(1)} %fusion.67, f32[8,128,256]{2,1,0:T(8,128)} %fusion.37, f32[8,153,128]{2,1,0:T(8,128)} %reshape.400, f32[8,136,256]{2,1,0:T(8,128)} %get-tuple-element.91, ...), kind=kOutput, calls=%fused_computation.51 | convolution fusion | flops 483493888 | bytes 4511332 | tf_op jit(solution)/shard_map/hft,hfv->thv/dot_general | solution.py:160
  112.5 1.4 fusion.6
  114.3 0.9 reshape.410
  115.2 5.5 %all-to-all-start.2 = ((f32[32,39,128]{2,1,0:T(8,128)}), f32[32,39,128]{2,1,0:T(8,128)S(1)}, u32[]{:S(2)}, u32[]{:S(2)}) async-start(f32[32,39,128]{2,1,0:T(8,128)} %reshape.410), calls=%async_computation.2 | async-start | bytes 1310720 | tf_op jit(solution)/shard_map/all_to_all | solution.py:101
  121.0 0.7 gather_fusion.3
  121.7 0.7 gather_fusion.2
  122.4 0.7 copy.190
  123.1 0.7 copy.189
  123.9 1.0 copy.126
  124.9 14.6 %all-to-all-done.2 = f32[32,39,128]{2,1,0:T(8,128)S(1)} async-done(((f32[32,39,128]{2,1,0:T(8,128)}), f32[32,39,128]{2,1,0:T(8,128)S(1)}, u32[]{:S(2)}, u32[]{:S(2)}) %all-to-all-start.2) | async-done | bytes 639008 | tf_op jit(solution)/shard_map/all_to_all | solution.py:101
  140.0 1.3 copy.120
  141.3 5.5 %all-to-all-start.3 = ((f32[32,39,128]{2,1,0:T(8,128)}), f32[32,39,128]{2,1,0:T(8,128)S(1)}, u32[]{:S(2)}, u32[]{:S(2)}) async-start(f32[32,39,128]{2,1,0:T(8,128)} %copy.120), calls=%async_computation.3 | async-start | bytes 1310720 | tf_op jit(solution)/shard_map/all_to_all | solution.py:103
  146.8 2.4 %fusion = f32[8,153,256]{2,1,0:T(8,128)S(1)} fusion(f32[8,153,128]{2,1,0:T(8,128)} %reshape.400, f32[8,256]{1,0:T(8,128)S(1)} %bitcast_divide_fusion, f32[8,153]{1,0:T(8,128)S(1)} %reshape.402, f32[256]{0:T(256)S(1)} %get-tuple-element.82, f32[256,8,128]{0,2,1:T(8,128)S(1)} %bitcast.213, f32[256,8]{0,1:T(8,128)S(1)} %fusion.67), kind=kOutput, calls=%fused_computation.13 | convolution fusion | flops 482498560 | bytes 2950944 | tf_op jit(solution)/shard_map/hfv,thv->hft/dot_general | solution.py:189
  149.2 1.1 copy-done.12
  150.8 2.3 %gather_fusion.4 = f32[256,8,256]{2,1,0:T(8,128)} fusion(f32[8,136,256]{2,0,1:T(8,128)S(1)} %copy.115, s32[1024]{0:T(1024)S(1)} %pad_clamp_fusion.1), kind=kCustom, calls=%fused_computation.clone | custom fusion | bytes 4195328 | tf_op jit(solution)/shard_map/jit(_take)/gather | solution.py:58
  153.1 5.7 %fusion.35 = f32[8,128,256]{2,1,0:T(8,128)} fusion(f32[8,256,256]{1,2,0:T(8,128)} %copy-done.40, pred[256,256]{0,1:T(8,128)(4,1)S(1)} %fusion.48, f32[256,8,128]{0,2,1:T(8,128)} %bitcast.211, f32[256,8]{0,1:T(8,128)S(1)} %fusion.67), kind=kOutput, calls=%fused_computation.66 | convolution fusion | flops 808714240 | bytes 4268032 | tf_op jit(solution)/shard_map/hts,thv->shv/dot_general | solution.py:177
  158.8 2.7 %multiply_select_fusion = f32[8,256,256]{1,2,0:T(8,128)} fusion(f32[8,256,256]{1,2,0:T(8,128)S(1)} %copy-done.41, f32[8,256]{1,0:T(8,128)S(1)} %bitcast_divide_fusion, pred[256,256]{0,1:T(8,128)(4,1)S(1)} %fusion.48, bf16[32,8,8,128]{3,2,1,0:T(8,128)(2,1)S(1)} %copy-done.10, f32[256,8,128]{0,2,1:T(8,128)S(1)} %bitcast.214, f32[256,8]{0,1:T(8,128)S(1)} %fusion.67), kind=kOutput, calls=%fused_computation.10 | convolution fusion | flops 808189952 | bytes 5849088 | tf_op jit(solution)/shard_map/thv,shv->hts/dot_general | solution.py:182
  161.5 3.9 %all-to-all-done.3 = f32[32,39,128]{2,1,0:T(8,128)S(1)} async-done(((f32[32,39,128]{2,1,0:T(8,128)}), f32[32,39,128]{2,1,0:T(8,128)S(1)}, u32[]{:S(2)}, u32[]{:S(2)}) %all-to-all-start.3) | async-done | bytes 639008 | tf_op jit(solution)/shard_map/all_to_all | solution.py:103
  166.1 4.2 %fusion.2 = f32[8,128,256]{2,1,0:T(8,128)} fusion(f32[8,128,256]{2,1,0:T(8,128)} %fusion.35, f32[8,153,128]{2,1,0:T(8,128)S(1)} %reshape.412, f32[8,136,256]{2,1,0:T(8,128)S(1)} %get-tuple-element.92, f32[8,16,256]{2,1,0:T(8,128)S(1)} %copy-done.14, f32[153]{0:T(256)S(1)} %copy-done.30, f32[256]{0:T(256)S(1)} %copy-done.31), kind=kOutput, calls=%fused_computation.17 | convolution fusion | flops 482447360 | bytes 3970660 | tf_op jit(solution)/shard_map/hfs,hfv->shv/dot_general | solution.py:178
  170.3 1.6 copy.124
  172.0 0.7 fusion.1
  173.1 2.4 %multiply_convert_fusion = (bf16[256,1024]{1,0:T(8,128)(2,1)}, f32[256,1024]{1,0:T(8,128)S(1)}) fusion(f32[256,1024]{1,0:T(8,128)S(1)} %copy.124, bf16[256,1024]{1,0:T(8,128)(2,1)S(1)} %copy-done.8, f32[256]{0:T(256)S(1)} %copy-done.26, bf16[256,1024]{1,0:T(8,128)(2,1)S(1)} %copy-done.6, bf16[2,1024]{1,0:T(2,128)(2,1)} %collective-permute-done, ...), kind=kLoop, calls=%fused_computation.50 | loop fusion | flops 6815744 | bytes 3688448 | tf_op jit(solution)/shard_map/convert_element_type | solution.py:201
  175.5 4.6 %collective-permute-start.1 = (f32[2,1024]{1,0:T(2,128)S(1)}, f32[2,1024]{1,0:T(2,128)S(1)}, u32[]{:S(2)}, u32[]{:S(2)}) collective-permute-start(f32[2,1024]{1,0:T(2,128)S(1)} %slice.440), channel_id=1, source_target_pairs={{8,0},{16,8},{24,16},{32,24},{40,32},{48,40},{56,48},{64,56},{72,6... | collective-permute-start | bytes 24584 | tf_op jit(solution)/shard_map/ppermute | solution.py:22
  180.7 2.4 %gather_fusion.5 = f32[256,8,256]{2,1,0:T(8,128)} fusion(f32[8,136,256]{2,0,1:T(8,128)S(1)} %copy.122, s32[1024]{0:T(1024)S(1)} %pad_clamp_fusion.1), kind=kCustom, calls=%fused_computation.1.clone | custom fusion | bytes 4195328 | tf_op jit(solution)/shard_map/jit(_take)/gather | solution.py:58
  183.1 2.0 %bitcast_multiply_fusion = (f32[8,256,256]{2,0,1:T(8,128)S(1)}, f32[8,256,256]{2,0,1:T(8,128)S(1)}) fusion(f32[256,8,256]{2,1,0:T(8,128)} %gather_fusion.5, f32[256]{0:T(256)S(1)} %copy-done.38, f32[256,8,256]{2,1,0:T(8,128)S(1)} %copy-done), kind=kLoop, calls=%fused_computation.6 | loop fusion | flops 1048576 | bytes 8389632 | tf_op jit(solution)/shard_map/mul | solution.py:58
  185.2 1.4 copy-done.1
  186.6 2.0 %fusion.17 = bf16[256,8,16]{0,2,1:T(8,128)(2,1)S(1)} fusion(f32[8,256,256]{1,2,0:T(8,128)S(1)} %copy-done.1, bf16[256,8,16]{0,2,1:T(8,128)(2,1)S(1)} %bitcast.210, f32[8,153,256]{2,1,0:T(8,128)} %copy-done.2, f32[8,256,16]{1,0,2:T(8,128)S(1)} %multiply_reduce_fusion), kind=kOutput, calls=%fused_computation.38 | convolution fusion | flops 100827136 | bytes 2490368 | tf_op jit(solution)/shard_map/hts,thd->shd/dot_general | solution.py:187
  188.8 1.8 fusion.16
  190.7 0.7 copy.128
  191.4 0.7 copy.127
  192.1 1.2 fusion.23
  (197 shorter events, 17.5 us)
Async XLA Ops:
  2.0 37.0 %collective-permute-start = (bf16[2,1024]{1,0:T(2,128)(2,1)}, bf16[2,1024]{1,0:T(2,128)(2,1)}, u32[]{:S(2)}, u32[]{:S(2)}) collective-permute-start(bf16[2,1024]{1,0:T(2,128)(2,1)} %slice.268), channel_id=1, source_target_pairs={{0,8},{8,16},{16,24},{24,32},{32,40},{40,48},{48,56},{56,64},{64,7... | collective-permute-start | bytes 12296 | tf_op jit(solution)/shard_map/ppermute | solution.py:22
  10.0 5.9 %copy-start.34 = (s32[32]{0:T(128)}, s32[32]{0:T(128)S(1)}, u32[]{:S(2)}) copy-start(s32[32]{0:T(128)S(1)} %reduce.2) | copy-start | bytes 388
  22.8 5.2 %copy-start.21 = (f32[8,15,256]{2,1,0:T(8,128)S(1)}, f32[8,15,256]{2,1,0:T(8,128)}, u32[]{:S(2)}) copy-start(f32[8,15,256]{2,1,0:T(8,128)} %slice_multiply_fusion.15) | copy-start | bytes 368644
  33.9 2.0 %copy-start.32 = (s32[258]{0:T(512)S(1)}, s32[258]{0:T(512)}, u32[]{:S(2)}) copy-start(s32[258]{0:T(512)} %get-tuple-element.85) | copy-start | bytes 3100
  33.9 2.0 %copy-start.33 = (s32[258]{0:T(512)S(1)}, s32[258]{0:T(512)}, u32[]{:S(2)}) copy-start(s32[258]{0:T(512)} %get-tuple-element.86) | copy-start | bytes 3100
  33.9 4.5 %copy-start.13 = (f32[8,16,256]{2,1,0:T(8,128)S(1)}, f32[8,16,256]{2,1,0:T(8,128)}, u32[]{:S(2)}) copy-start(f32[8,16,256]{2,1,0:T(8,128)} %get-tuple-element.56) | copy-start | bytes 393220
  33.9 4.5 %copy-start.29 = (f32[153]{0:T(256)S(1)}, f32[153]{0:T(256)}, u32[]{:S(2)}) copy-start(f32[153]{0:T(256)} %pad.16.clone) | copy-start | bytes 1840
  35.9 3.1 %copy-start.5 = (bf16[256,1024]{1,0:T(8,128)(2,1)S(1)}, bf16[256,1024]{1,0:T(8,128)(2,1)}, u32[]{:S(2)}) copy-start(bf16[256,1024]{1,0:T(8,128)(2,1)} %param.18) | copy-start | bytes 1572868
  35.9 3.1 %copy-start.7 = (bf16[256,1024]{1,0:T(8,128)(2,1)S(1)}, bf16[256,1024]{1,0:T(8,128)(2,1)}, u32[]{:S(2)}) copy-start(bf16[256,1024]{1,0:T(8,128)(2,1)} %param.19) | copy-start | bytes 1572868
  38.3 2.2 %copy-start.25 = (f32[256]{0:T(256)}, f32[256]{0:T(256)S(1)}, u32[]{:S(2)}) copy-start(f32[256]{0:T(256)S(1)} %get-tuple-element.83) | copy-start | bytes 3076
  38.3 2.2 %copy-start.27 = (f32[256]{0:T(256)}, f32[256]{0:T(256)S(1)}, u32[]{:S(2)}) copy-start(f32[256]{0:T(256)S(1)} %get-tuple-element.84) | copy-start | bytes 3076
  38.4 2.2 %copy-start.14 = (f32[8,16,256]{2,1,0:T(8,128)S(1)}, f32[8,16,256]{2,1,0:T(8,128)}, u32[]{:S(2)}) copy-start(f32[8,16,256]{2,1,0:T(8,128)} %get-tuple-element.56) | copy-start | bytes 393220
  40.5 44.1 %copy-start.9 = (bf16[32,8,8,128]{3,2,1,0:T(8,128)(2,1)}, bf16[32,8,8,128]{3,2,1,0:T(8,128)(2,1)S(1)}, u32[]{:S(2)}) copy-start(bf16[32,8,8,128]{3,2,1,0:T(8,128)(2,1)S(1)} %fusion.39) | copy-start | bytes 1572868
  43.8 12.0 %copy-start.35 = (s32[32]{0:T(128)S(1)}, s32[32]{0:T(128)}, u32[]{:S(2)}) copy-start(s32[32]{0:T(128)} %copy-done.34) | copy-start | bytes 388
  44.7 30.6 %all-to-all-start = ((f32[32,39,128]{2,1,0:T(8,128)}), f32[32,39,128]{2,1,0:T(8,128)S(1)}, u32[]{:S(2)}, u32[]{:S(2)}) async-start(f32[32,39,128]{2,1,0:T(8,128)} %reshape.398), calls=%async_computation | async-start | bytes 1310720 | tf_op jit(solution)/shard_map/all_to_all | solution.py:101
  76.9 5.6 %copy-start.20 = (bf16[256,1024]{1,0:T(8,128)(2,1)S(1)}, bf16[256,1024]{1,0:T(8,128)(2,1)}, u32[]{:S(2)}) copy-start(bf16[256,1024]{1,0:T(8,128)(2,1)} %param.22) | copy-start | bytes 1572868
  76.9 24.4 %all-to-all-start.1 = ((f32[32,39,128]{2,1,0:T(8,128)}), f32[32,39,128]{2,1,0:T(8,128)S(1)}, u32[]{:S(2)}, u32[]{:S(2)}) async-start(f32[32,39,128]{2,1,0:T(8,128)} %copy.108), calls=%async_computation.1 | async-start | bytes 1310720 | tf_op jit(solution)/shard_map/all_to_all | solution.py:103
  84.6 1.3 copy-start.40
  101.4 1.1 copy-start.24
  101.4 1.1 copy-start.30
  101.4 3.2 %copy-start.15 = (f32[8,136,256]{2,1,0:T(8,128)S(1)}, f32[8,136,256]{2,1,0:T(8,128)}, u32[]{:S(2)}) copy-start(f32[8,136,256]{2,1,0:T(8,128)} %get-tuple-element.91) | copy-start | bytes 3342340
  102.4 2.3 %copy-start.17 = (f32[256,1024]{0,1:T(8,128)S(1)}, f32[256,1024]{0,1:T(8,128)}, u32[]{:S(2)}) copy-start(f32[256,1024]{0,1:T(8,128)} %copy.109) | copy-start | bytes 3145732
  108.2 4.2 %copy-start.16 = (f32[8,136,256]{2,1,0:T(8,128)S(1)}, f32[8,136,256]{2,1,0:T(8,128)}, u32[]{:S(2)}) copy-start(f32[8,136,256]{2,1,0:T(8,128)} %get-tuple-element.91) | copy-start | bytes 3342340
  115.2 8.6 %copy-start.39 = (s32[256]{0:T(256)S(1)}, s32[256]{0:T(256)}, u32[]{:S(2)}) copy-start(s32[256]{0:T(256)} %constant.110) | copy-start | bytes 3076
  115.2 24.3 %all-to-all-start.2 = ((f32[32,39,128]{2,1,0:T(8,128)}), f32[32,39,128]{2,1,0:T(8,128)S(1)}, u32[]{:S(2)}, u32[]{:S(2)}) async-start(f32[32,39,128]{2,1,0:T(8,128)} %reshape.410), calls=%async_computation.2 | async-start | bytes 1310720 | tf_op jit(solution)/shard_map/all_to_all | solution.py:101
  141.3 5.5 %copy-start.18 = (f32[256,1024]{0,1:T(8,128)S(1)}, f32[256,1024]{0,1:T(8,128)}, u32[]{:S(2)}) copy-start(f32[256,1024]{0,1:T(8,128)} %copy.109) | copy-start | bytes 3145732
  141.3 24.1 %all-to-all-start.3 = ((f32[32,39,128]{2,1,0:T(8,128)}), f32[32,39,128]{2,1,0:T(8,128)S(1)}, u32[]{:S(2)}, u32[]{:S(2)}) async-start(f32[32,39,128]{2,1,0:T(8,128)} %copy.120), calls=%async_computation.3 | async-start | bytes 1310720 | tf_op jit(solution)/shard_map/all_to_all | solution.py:103
  149.2 1.1 copy-start.12
  153.1 5.7 %copy-start.10 = (bf16[32,8,8,128]{3,2,1,0:T(8,128)(2,1)S(1)}, bf16[32,8,8,128]{3,2,1,0:T(8,128)(2,1)}, u32[]{:S(2)}) copy-start(bf16[32,8,8,128]{3,2,1,0:T(8,128)(2,1)} %copy-done.9) | copy-start | bytes 1572868
  153.1 5.7 %copy-start.19 = (f32[256,1024]{0,1:T(8,128)S(1)}, f32[256,1024]{0,1:T(8,128)}, u32[]{:S(2)}) copy-start(f32[256,1024]{0,1:T(8,128)} %copy.109) | copy-start | bytes 3145732
  153.1 5.7 %copy-start.41 = (f32[8,256,256]{1,2,0:T(8,128)S(1)}, f32[8,256,256]{1,2,0:T(8,128)}, u32[]{:S(2)}) copy-start(f32[8,256,256]{1,2,0:T(8,128)} %copy-done.40) | copy-start | bytes 6291460
  165.4 0.7 copy-start.31
  170.3 1.6 copy-start.11
  171.9 1.0 copy-start.6
  171.9 1.2 copy-start.8
  171.9 1.2 copy-start.26
  172.0 1.2 copy-start.28
  173.1 7.1 %copy-start.2 = (f32[8,153,256]{2,1,0:T(8,128)}, f32[8,153,256]{2,1,0:T(8,128)S(1)}, u32[]{:S(2)}) copy-start(f32[8,153,256]{2,1,0:T(8,128)S(1)} %fusion.1) | copy-start | bytes 3760132
  175.5 4.7 %copy-start.3 = (f32[256,1024]{1,0:T(8,128)}, f32[256,1024]{1,0:T(8,128)S(1)}, u32[]{:S(2)}) copy-start(f32[256,1024]{1,0:T(8,128)S(1)} %get-tuple-element.36) | copy-start | bytes 3145732
  175.5 16.6 %collective-permute-start.1 = (f32[2,1024]{1,0:T(2,128)S(1)}, f32[2,1024]{1,0:T(2,128)S(1)}, u32[]{:S(2)}, u32[]{:S(2)}) collective-permute-start(f32[2,1024]{1,0:T(2,128)S(1)} %slice.440), channel_id=1, source_target_pairs={{8,0},{16,8},{24,16},{32,24},{40,32},{48,40},{56,48},{64,56},{72,6... | collective-permute-start | bytes 24584 | tf_op jit(solution)/shard_map/ppermute | solution.py:22
  180.7 2.4 %copy-start = (f32[256,8,256]{2,1,0:T(8,128)S(1)}, f32[256,8,256]{2,1,0:T(8,128)}, u32[]{:S(2)}) copy-start(f32[256,8,256]{2,1,0:T(8,128)} %gather_fusion.4) | copy-start | bytes 6291460
  180.7 2.4 %copy-start.38 = (f32[256]{0:T(256)S(1)}, f32[256]{0:T(256)}, u32[]{:S(2)}) copy-start(f32[256]{0:T(256)} %constant.87.clone) | copy-start | bytes 3076
  183.1 2.0 %copy-start.23 = (f32[8,256,16]{1,0,2:T(8,128)S(1)}, f32[8,256,16]{1,0,2:T(8,128)}, u32[]{:S(2)}) copy-start(f32[8,256,16]{1,0,2:T(8,128)} %copy.190) | copy-start | bytes 393220
  185.0 1.6 copy-start.1
  186.6 2.0 %copy-start.22 = (f32[8,256,16]{1,0,2:T(8,128)S(1)}, f32[8,256,16]{1,0,2:T(8,128)}, u32[]{:S(2)}) copy-start(f32[8,256,16]{1,0,2:T(8,128)} %copy.189) | copy-start | bytes 393220
  188.8 3.3 %copy-start.4 = (f32[256,1024]{1,0:T(8,128)S(1)}, f32[256,1024]{1,0:T(8,128)}, u32[]{:S(2)}) copy-start(f32[256,1024]{1,0:T(8,128)} %copy-done.3) | copy-start | bytes 3145732
  188.8 3.3 %copy-start.36 = (f32[256]{0:T(256)S(1)}, f32[256]{0:T(256)}, u32[]{:S(2)}) copy-start(f32[256]{0:T(256)} %get-tuple-element.76) | copy-start | bytes 3076
  188.8 3.3 %copy-start.37 = (f32[256]{0:T(256)S(1)}, f32[256]{0:T(256)}, u32[]{:S(2)}) copy-start(f32[256]{0:T(256)} %get-tuple-element.77) | copy-start | bytes 3076
where the time goes:
time: 195 us; the launch traced here: 193 us
  waiting for transfers between devices  49 us (25%)
  local copies, waits for them, and re-layouts  45.2 us (23%)
  starting transfers between devices  35.8 us (18%)
  matrix products  35.8 us (18%)
  other arithmetic  26 us (13%)
    all_to_all x2, waiting for transfers between devices, state_scan(): chunks = lax.all_to_all(packed, 'ctx', 0, 0, tiled=True)  32.1 us
    all_to_all x2, waiting for transfers between devices, state_scan(): lax.all_to_all(summed, 'ctx', 0, 0, tiled=True).reshape(total_rows, width)  16.8 us
    all_to_all x2, starting transfers between devices, state_scan(): chunks = lax.all_to_all(packed, 'ctx', 0, 0, tiled=True)  16.6 us
    all_to_all x2, starting transfers between devices, state_scan(): lax.all_to_all(summed, 'ctx', 0, 0, tiled=True).reshape(total_rows, width)  11.1 us
    unnamed x107, local copies, waits for them, and re-layouts  10.6 us
    concatenate x2, local copies, waits for them, and re-layouts, feature_rows(): outer = jnp.concatenate(pieces, axis=1) * jnp.asarray(weight)[None, :, None]  9.82 us
    ppermute x2, starting transfers between devices, shifted(): return lax.ppermute(block, axis, route)  8.12 us
    mul x30, other arithmetic, feature_rows(): pieces.append(spread[:, i:i + 1, :] * spread[:, i:, :])  7.86 us
  transfers between devices with their start and end apart: 6, of which 4 were waited for; matrix products, arithmetic and copies ran while one was open for 35% of the time, Pallas kernels for 0%

commit v1 on v0

--- a/solution.py
+++ b/solution.py
@@ -13,6 +13,7 @@
 
 
 highest = lax.Precision.HIGHEST
+high = lax.Precision.HIGH
 quad_scale = 1.0 / (4.0 * math.sqrt(2.0))
 
 
@@ -57,7 +58,7 @@
     quad = grad_phi[:, 1 + width :]
     paired = jnp.take(quad, jnp.asarray(place), axis=1) * jnp.asarray(spread_weight)[None, :, None]
     paired = paired.reshape(head_count, width, width, token_count)
-    return linear + jnp.einsum("hijt,hjt->hit", paired, spread, precision=highest)
+    return linear + jnp.einsum("hijt,hjt->hit", paired, spread, precision=high)
 
 
 def block_flags(doc_lengths, devices, rows):
@@ -86,24 +87,23 @@
 def state_scan(local_state, local_norm, mask):
     devices = mask.shape[0]
     heads, feats, width = local_state.shape
-    state_rows = heads * feats
-    norm_rows = -(-(heads * feats) // width)
-    total_rows = -(-(state_rows + norm_rows) // devices) * devices
-    flat_norm = jnp.pad(local_norm.reshape(-1), (0, norm_rows * width - heads * feats))
+    norm_rows = -(-feats // width)
+    head_rows = feats + norm_rows
+    spare = (-heads * head_rows) % devices
+    flat_norm = jnp.pad(local_norm, ((0, 0), (0, norm_rows * width - feats)))
     packed = jnp.concatenate(
-        [
-            local_state.reshape(state_rows, width),
-            flat_norm.reshape(norm_rows, width),
-            jnp.zeros((total_rows - state_rows - norm_rows, width), jnp.float32),
-        ],
-        axis=0,
-    ).reshape(devices, total_rows // devices, width)
+        [local_state, flat_norm.reshape(heads, norm_rows, width)], axis=1
+    ).reshape(heads * head_rows, width)
+    if spare:
+        packed = jnp.pad(packed, ((0, spare), (0, 0)))
+    packed = packed.reshape(devices, -1, width)
     chunks = lax.all_to_all(packed, "ctx", 0, 0, tiled=True)
-    summed = jnp.einsum("ij,jrc->irc", mask, chunks, precision=highest)
-    back = lax.all_to_all(summed, "ctx", 0, 0, tiled=True).reshape(total_rows, width)
-    state_in = back[:state_rows].reshape(heads, feats, width)
-    norm_in = back[state_rows : state_rows + norm_rows].reshape(-1)[: heads * feats]
-    return (state_in, norm_in.reshape(heads, feats))
+    summed = jnp.einsum("ij,jrc->irc", mask, chunks, precision=high)
+    back = lax.all_to_all(summed, "ctx", 0, 0, tiled=True).reshape(-1, width)
+    back = back[: heads * head_rows].reshape(heads, head_rows, width)
+    state_in = back[:, :feats]
+    norm_in = back[:, feats:].reshape(heads, norm_rows * width)[:, :feats]
+    return (state_in, norm_in)
 
 
 def local(query, key, value_in, gate, conv_weight, doc_lengths, d_out):
@@ -141,27 +141,35 @@
     q_float = query.astype(jnp.float32).reshape(tok_rows, HEADS, KD)
     k_float = key.astype(jnp.float32).reshape(tok_rows, HEADS, KD)
     v_float = value_rows.astype(jnp.float32).reshape(tok_rows, HEADS, VD)
-    scores = jnp.einsum("thd,shd->hts", q_float, k_float, precision=highest) * 0.25
+    scores = (
+        jnp.einsum(
+            "thd,shd->hts",
+            query.reshape(tok_rows, HEADS, KD),
+            key.reshape(tok_rows, HEADS, KD),
+            preferred_element_type=jnp.float32,
+        )
+        * 0.25
+    )
     kernel = 1.0 + scores + 0.5 * scores * scores
     allowed = (local_pos[:, None] >= local_pos[None, :]) & (doc_ids[:, None] == doc_ids[None, :])
     weights = jnp.where(allowed[None], kernel, 0.0)
-    numerator = jnp.einsum("hts,shv->thv", weights, v_float, precision=highest)
+    numerator = jnp.einsum("hts,shv->thv", weights, v_float, precision=high)
     denominator = jnp.transpose(jnp.sum(weights, axis=2), (1, 0))
     phi_query, spread_query = feature_rows(q_float)
     phi_key, spread_key = feature_rows(k_float)
     last_mask = (doc_ids == doc_ids[tok_rows - 1]).astype(jnp.float32)
     masked_key = phi_key * last_mask[None, None, :]
-    local_state = jnp.einsum("hft,thv->hfv", masked_key, v_float, precision=highest)
+    local_state = jnp.einsum("hft,thv->hfv", masked_key, v_float, precision=high)
     local_norm = jnp.sum(masked_key, axis=2)
     restart_all, closes_all = block_flags(doc_lengths, lax.axis_size("ctx"), tok_rows)
     forward_mask, backward_mask = scan_masks(restart_all, closes_all)
     state_in, norm_in = state_scan(local_state, local_norm, forward_mask)
     inside = (doc_ids == prev_doc).astype(jnp.float32)
     numerator = numerator + inside[:, None, None] * jnp.einsum(
-        "hft,hfv->thv", phi_query, state_in, precision=highest
+        "hft,hfv->thv", phi_query, state_in, precision=high
     )
     denominator = denominator + inside[:, None] * jnp.einsum(
-        "hft,hf->th", phi_query, norm_in, precision=highest
+        "hft,hf->th", phi_query, norm_in, precision=high
     )
     attended = numerator / denominator[:, :, None]
     mixed = attended.reshape(tok_rows, HEADS * VD).astype(jnp.bfloat16)
@@ -170,27 +178,27 @@
     grad_den = -jnp.sum(upstream * attended, axis=2) / denominator
     first_mask = (doc_ids == doc_ids[0]).astype(jnp.float32)
     masked_query = phi_query * first_mask[None, None, :]
-    back_state = jnp.einsum("hft,thv->hfv", masked_query, grad_num, precision=highest)
-    back_norm = jnp.einsum("hft,th->hf", masked_query, grad_den, precision=highest)
+    back_state = jnp.einsum("hft,thv->hfv", masked_query, grad_num, precision=high)
+    back_norm = jnp.einsum("hft,th->hf", masked_query, grad_den, precision=high)
     grad_state_in, grad_norm_in = state_scan(back_state, back_norm, backward_mask)
     outside = (doc_ids == next_doc).astype(jnp.float32)
-    grad_v = jnp.einsum("hts,thv->shv", weights, grad_num, precision=highest)
+    grad_v = jnp.einsum("hts,thv->shv", weights, grad_num, precision=high)
     grad_v = grad_v + outside[:, None, None] * jnp.einsum(
-        "hfs,hfv->shv", phi_key, grad_state_in, precision=highest
+        "hfs,hfv->shv", phi_key, grad_state_in, precision=high
     )
     grad_weights = (
-        jnp.einsum("thv,shv->hts", grad_num, v_float, precision=highest)
+        jnp.einsum("thv,shv->hts", grad_num, v_float, precision=high)
         + jnp.transpose(grad_den, (1, 0))[:, :, None]
     )
     grad_scores = jnp.where(allowed[None], grad_weights * (1.0 + scores), 0.0)
-    grad_q = jnp.einsum("hts,shd->thd", grad_scores, k_float, precision=highest) * 0.25
-    grad_k = jnp.einsum("hts,thd->shd", grad_scores, q_float, precision=highest) * 0.25
+    grad_q = jnp.einsum("hts,shd->thd", grad_scores, k_float, precision=high) * 0.25
+    grad_k = jnp.einsum("hts,thd->shd", grad_scores, q_float, precision=high) * 0.25
     grad_phi_query = inside[None, None, :] * (
-        jnp.einsum("hfv,thv->hft", state_in, grad_num, precision=highest)
+        jnp.einsum("hfv,thv->hft", state_in, grad_num, precision=high)
         + norm_in[:, :, None] * jnp.transpose(grad_den, (1, 0))[:, None, :]
     )
     grad_phi_key = outside[None, None, :] * (
-        jnp.einsum("hfv,shv->hfs", grad_state_in, v_float, precision=highest)
+        jnp.einsum("hfv,shv->hfs", grad_state_in, v_float, precision=high)
         + grad_norm_in[:, :, None]
     )
     grad_q = grad_q + jnp.transpose(feature_grad(grad_phi_query, spread_query), (2, 0, 1))

time: 195 us -> 185 us (0.949)
  matrix products: 35.8 us -> 25.6 us
  local copies, waits for them, and re-layouts: 45.2 us -> 42.2 us
  waiting for transfers between devices: 49 us -> 51.4 us
    dot_general x16, matrix products: 35.8 us -> 25.6 us  [the longest x1 4.52 us: local(): grad_v = jnp.einsum('hts,thv->shv', weights, grad_num, precision=high)]
    reshape x16 -> x10, local copies, waits for them, and re-layouts: 5.42 us -> 2.9 us  [the longest x2 1.78 us: state_scan(): packed = packed.reshape(devices, -1, width)]
    all_to_all x2, waiting for transfers between devices: 16.8 us -> 19.2 us  [state_scan(): back = lax.all_to_all(summed, 'ctx', 0, 0, tiled=True).reshape(-1, width)]
    unnamed x107 -> x111, local copies, waits for them, and re-layouts: 10.6 us -> 11.8 us
where the time goes in v1:
time: 185 us; the launch traced here: 184 us
  waiting for transfers between devices  51.4 us (28%)
  local copies, waits for them, and re-layouts  42.2 us (23%)
  starting transfers between devices  35.5 us (19%)
  other arithmetic  27.3 us (15%)
  matrix products  25.6 us (14%)
    all_to_all x2, waiting for transfers between devices, state_scan(): chunks = lax.all_to_all(packed, 'ctx', 0, 0, tiled=True)  32.2 us
    all_to_all x2, waiting for transfers between devices, state_scan(): back = lax.all_to_all(summed, 'ctx', 0, 0, tiled=True).reshape(-1, width)  19.2 us
    all_to_all x2, starting transfers between devices, state_scan(): chunks = lax.all_to_all(packed, 'ctx', 0, 0, tiled=True)  16.6 us
    unnamed x111, local copies, waits for them, and re-layouts  11.8 us
    all_to_all x2, starting transfers between devices, state_scan(): back = lax.all_to_all(summed, 'ctx', 0, 0, tiled=True).reshape(-1, width)  11.1 us
    concatenate x2, local copies, waits for them, and re-layouts, feature_rows(): outer = jnp.concatenate(pieces, axis=1) * jnp.asarray(weight)[None, :, None]  9.82 us
    ppermute x2, starting transfers between devices, shifted(): return lax.ppermute(block, axis, route)  7.86 us
    mul x30, other arithmetic, feature_rows(): pieces.append(spread[:, i:i + 1, :] * spread[:, i:, :])  7.81 us
  transfers between devices with their start and end apart: 6, of which 4 were waited for; matrix products, arithmetic and copies ran while one was open for 35% of the time, Pallas kernels for 0%

profile of v1, /device:TPU:32, one launch (start us, length us, event | category | flops | bytes accessed | tf_op | source)
XLA Modules:
  0.0 183.6 jit_solution(464811738010172865)
XLA Ops:
  0.6 1.3 slice.274
  1.9 3.5 %collective-permute-start = (bf16[2,1024]{1,0:T(2,128)(2,1)}, bf16[2,1024]{1,0:T(2,128)(2,1)}, u32[]{:S(2)}, u32[]{:S(2)}) collective-permute-start(bf16[2,1024]{1,0:T(2,128)(2,1)} %slice.274), channel_id=1, source_target_pairs={{0,8},{8,16},{16,24},{24,32},{32,40},{40,48},{48,56},{56,64},{64,7... | collective-permute-start | bytes 12296 | tf_op jit(solution)/shard_map/ppermute | solution.py:23
  5.4 0.9 copy.102
  6.5 0.9 copy.101
  7.6 0.7 broadcast_add_fusion.3
  8.2 0.8 fusion.93
  9.1 0.7 copy.100
  10.3 0.7 compare_select_fusion
  11.5 1.2 compare_convert_fusion.5
  12.8 0.6 fusion.94
  17.4 0.7 slice_multiply_fusion.15
  21.4 0.7 convert_multiply_fusion
  22.1 0.7 broadcast_multiply_fusion.4
  23.4 0.7 pad_add_fusion.1
  24.1 4.0 %concatenate.35 = f32[8,136,256]{2,1,0:T(8,128)S(1)} concatenate(f32[8,16,256]{2,1,0:T(8,128)S(1)} %get-tuple-element.40, f32[8,15,256]{2,1,0:T(8,128)S(1)} %slice_multiply_fusion.8, f32[8,14,256]{2,1,0:T(8,128)S(1)} %slice_multiply_fusion.7, f32[8,13,256]{2,1,0:T(8,128)S(1)} %slice_multiply_fusion.6, f32[8,12,256]{2,1,0:T(8,128)S(1)} %slice_multiply_fusion.5, ...), dimensions={1} | concatenate | bytes 2228224 | tf_op jit(solution)/shard_map/concatenate | solution.py:50
  28.1 5.8 %concatenate.32 = f32[8,136,256]{2,1,0:T(8,128)S(1)} concatenate(f32[8,16,256]{2,1,0:T(8,128)} %get-tuple-element.57, f32[8,15,256]{2,1,0:T(8,128)S(1)} %copy-done.20, f32[8,14,256]{2,1,0:T(8,128)S(1)} %slice_multiply_fusion.14, f32[8,13,256]{2,1,0:T(8,128)S(1)} %slice_multiply_fusion.13, f32[8,12,256]{2,1,0:T(8,128)S(1)} %slice_multiply_fusion.12, ...), dimensions={1} | concatenate | bytes 2228224 | tf_op jit(solution)/shard_map/concatenate | solution.py:50
  34.0 2.0 %broadcast_multiply_fusion = (f32[8,136,256]{2,1,0:T(8,128)}, f32[8,136,256]{2,1,0:T(8,128)S(1)}) fusion(f32[8,136,256]{2,1,0:T(8,128)S(1)} %concatenate.35, f32[136]{0:T(256)} %constant.84.clone, f32[8,136,256]{2,1,0:T(8,128)S(1)} %concatenate.32), kind=kLoop, calls=%fused_computation.70 | loop fusion | flops 557056 | bytes 4456992 | tf_op jit(solution)/shard_map/mul | solution.py:50
  36.0 2.5 %compare_convert_fusion.1 = (f32[256]{0:T(256)}, f32[256]{0:T(256)}, f32[256]{0:T(256)S(1)}, f32[256]{0:T(256)S(1)}, f32[256]{0:T(256)S(1)}, /*index=5*/f32[256]{0:T(256)S(1)}, f32[256]{0:T(256)S(1)}) fusion(s32[256]{0:T(256)S(1)} %get-tuple-element.34, s32[258]{0:T(512)S(1)} %copy-done.32, s32[]{:T(128)} %bitcast.41, s32[]{:T(128)} %bitcast.16, ...), kind=kLoop, calls=%fused_computation.200 | loop fusion | flops 3584 | bytes 12300 | tf_op jit(solution)/shard_map/convert_element_type | solution.py:216
  39.1 1.5 fusion.43
  41.4 0.9 reshape.390
  42.3 11.1 %all-to-all-start = ((f32[32,39,128]{2,1,0:T(8,128)}), f32[32,39,128]{2,1,0:T(8,128)S(1)}, u32[]{:S(2)}, u32[]{:S(2)}) async-start(f32[32,39,128]{2,1,0:T(8,128)} %reshape.390), calls=%async_computation | async-start | bytes 1310720 | tf_op jit(solution)/shard_map/all_to_all | solution.py:100
  53.9 0.7 gather_fusion.1
  54.7 0.7 gather_fusion
  55.4 17.5 %all-to-all-done = f32[32,39,128]{2,1,0:T(8,128)S(1)} async-done(((f32[32,39,128]{2,1,0:T(8,128)}), f32[32,39,128]{2,1,0:T(8,128)S(1)}, u32[]{:S(2)}, u32[]{:S(2)}) %all-to-all-start) | async-done | bytes 639008 | tf_op jit(solution)/shard_map/all_to_all | solution.py:100
  73.3 1.2 copy.108
  74.5 5.6 %all-to-all-start.1 = ((f32[32,39,128]{2,1,0:T(8,128)}), f32[32,39,128]{2,1,0:T(8,128)S(1)}, u32[]{:S(2)}, u32[]{:S(2)}) async-start(f32[32,39,128]{2,1,0:T(8,128)} %copy.108), calls=%async_computation.1 | async-start | bytes 1310720 | tf_op jit(solution)/shard_map/all_to_all | solution.py:102
  80.0 1.2 copy.109
  81.4 0.8 fusion.40
  82.2 1.3 copy-done.40
  83.5 2.0 %fusion.41 = f32[8,128,256]{2,1,0:T(8,128)} fusion(f32[8,256,256]{1,2,0:T(8,128)S(1)} %get-tuple-element.98, pred[256,256]{0,1:T(8,128)(4,1)S(1)} %fusion.52, bf16[32,8,8,128]{3,2,1,0:T(8,128)(2,1)S(1)} %fusion.43), kind=kOutput, calls=%fused_computation.74 | convolution fusion | flops 405798912 | bytes 3735552 | tf_op jit(solution)/shard_map/hts,shv->thv/dot_general | solution.py:156
  85.5 13.3 %all-to-all-done.1 = f32[32,39,128]{2,1,0:T(8,128)S(1)} async-done(((f32[32,39,128]{2,1,0:T(8,128)}), f32[32,39,128]{2,1,0:T(8,128)S(1)}, u32[]{:S(2)}, u32[]{:S(2)}) %all-to-all-start.1) | async-done | bytes 639008 | tf_op jit(solution)/shard_map/all_to_all | solution.py:102
  99.0 0.9 reshape.392
  99.9 0.9 slice_bitcast_fusion.1
  101.3 3.4 %multiply_reduce_fusion.3 = (f32[256,8]{0,1:T(8,128)S(1)}, bf16[256,8,128]{0,2,1:T(8,128)(2,1)}) fusion(f32[256,1024]{0,1:T(8,128)S(1)} %copy-done.16, f32[256,8]{0,1:T(8,128)S(1)} %fusion.73, f32[8,128,256]{2,1,0:T(8,128)} %fusion.41, f32[8,136,256]{2,1,0:T(8,128)S(1)} %copy-done.15, f32[8,16,256]{2,1,0:T(8,128)S(1)} %copy-done.24, f32[153]{0:T(256)S(1)} %copy-done.30, ...), kind=kOutput, calls=%fused_computation.51 | convolution fusion | flops 242845696 | bytes 4519524 | tf_op jit(solution)/shard_map/hft,hfv->thv/dot_general | solution.py:168
  104.8 1.7 fusion.8
  106.5 0.8 fusion.6
  107.3 1.1 pad_maximum_fusion.6
  108.6 0.9 reshape.400
  109.5 5.5 %all-to-all-start.2 = ((f32[32,39,128]{2,1,0:T(8,128)}), f32[32,39,128]{2,1,0:T(8,128)S(1)}, u32[]{:S(2)}, u32[]{:S(2)}) async-start(f32[32,39,128]{2,1,0:T(8,128)} %reshape.400), calls=%async_computation.2 | async-start | bytes 1310720 | tf_op jit(solution)/shard_map/all_to_all | solution.py:100
  115.3 0.7 gather_fusion.3
  116.0 0.7 gather_fusion.2
  116.7 0.7 copy.190
  117.4 0.7 copy.189
  118.1 1.0 copy.126
  119.1 14.7 %all-to-all-done.2 = f32[32,39,128]{2,1,0:T(8,128)S(1)} async-done(((f32[32,39,128]{2,1,0:T(8,128)}), f32[32,39,128]{2,1,0:T(8,128)S(1)}, u32[]{:S(2)}, u32[]{:S(2)}) %all-to-all-start.2) | async-done | bytes 639008 | tf_op jit(solution)/shard_map/all_to_all | solution.py:100
  134.1 1.3 copy.120
  135.4 5.5 %all-to-all-start.3 = ((f32[32,39,128]{2,1,0:T(8,128)}), f32[32,39,128]{2,1,0:T(8,128)S(1)}, u32[]{:S(2)}, u32[]{:S(2)}) async-start(f32[32,39,128]{2,1,0:T(8,128)} %copy.120), calls=%async_computation.3 | async-start | bytes 1310720 | tf_op jit(solution)/shard_map/all_to_all | solution.py:102
  140.9 1.8 %fusion = f32[8,153,256]{2,1,0:T(8,128)S(1)} fusion(f32[8,256]{1,0:T(8,128)S(1)} %bitcast_divide_fusion, f32[8,153]{1,0:T(8,128)S(1)} %get-tuple-element.73, f32[256]{0:T(256)S(1)} %get-tuple-element.84, f32[8,155,128]{2,1,0:T(8,128)} %reshape.392, f32[256,8,128]{0,2,1:T(8,128)S(1)} %bitcast.211, f32[256,8]{0,1:T(8,128)S(1)} %fusion.73), kind=kOutput, calls=%fused_computation.13 | convolution fusion | flops 241850368 | bytes 2959136 | tf_op jit(solution)/shard_map/hfv,thv->hft/dot_general | solution.py:197
  142.8 1.1 copy-done.12
  144.3 2.3 %gather_fusion.4 = f32[256,8,256]{2,1,0:T(8,128)} fusion(f32[8,136,256]{2,0,1:T(8,128)S(1)} %copy.115, s32[1024]{0:T(1024)S(1)} %pad_clamp_fusion.1), kind=kCustom, calls=%fused_computation.clone | custom fusion | bytes 4195328 | tf_op jit(solution)/shard_map/jit(_take)/gather | solution.py:59
  146.7 4.5 %fusion.39 = f32[8,128,256]{2,1,0:T(8,128)} fusion(f32[8,256,256]{1,2,0:T(8,128)} %copy-done.40, pred[256,256]{0,1:T(8,128)(4,1)S(1)} %fusion.52, f32[256,8,128]{0,2,1:T(8,128)} %bitcast.209, f32[256,8]{0,1:T(8,128)S(1)} %fusion.73), kind=kOutput, calls=%fused_computation.72 | convolution fusion | flops 406061056 | bytes 4268032 | tf_op jit(solution)/shard_map/hts,thv->shv/dot_general | solution.py:185
  151.2 2.4 %multiply_select_fusion = f32[8,256,256]{1,2,0:T(8,128)} fusion(f32[8,256,256]{1,2,0:T(8,128)S(1)} %copy-done.41, f32[8,256]{1,0:T(8,128)S(1)} %bitcast_divide_fusion, pred[256,256]{0,1:T(8,128)(4,1)S(1)} %fusion.52, bf16[32,8,8,128]{3,2,1,0:T(8,128)(2,1)S(1)} %copy-done.10, f32[256,8,128]{0,2,1:T(8,128)S(1)} %bitcast.212, f32[256,8]{0,1:T(8,128)S(1)} %fusion.73), kind=kOutput, calls=%fused_computation.10 | convolution fusion | flops 405536768 | bytes 5849088 | tf_op jit(solution)/shard_map/thv,shv->hts/dot_general | solution.py:190
  153.6 5.9 %all-to-all-done.3 = f32[32,39,128]{2,1,0:T(8,128)S(1)} async-done(((f32[32,39,128]{2,1,0:T(8,128)}), f32[32,39,128]{2,1,0:T(8,128)S(1)}, u32[]{:S(2)}, u32[]{:S(2)}) %all-to-all-start.3) | async-done | bytes 639008 | tf_op jit(solution)/shard_map/all_to_all | solution.py:102
  160.3 2.3 %fusion.2 = f32[8,128,256]{2,1,0:T(8,128)S(1)} fusion(f32[8,128,256]{2,1,0:T(8,128)} %fusion.39, f32[8,136,256]{2,1,0:T(8,128)S(1)} %get-tuple-element.94, f32[8,16,256]{2,1,0:T(8,128)S(1)} %copy-done.14, f32[153]{0:T(256)S(1)} %copy-done.30, f32[8,155,128]{2,1,0:T(8,128)S(1)} %reshape.402, f32[256]{0:T(256)S(1)} %copy-done.31), kind=kOutput, calls=%fused_computation.17 | convolution fusion | flops 241799168 | bytes 3978852 | tf_op jit(solution)/shard_map/hfs,hfv->shv/dot_general | solution.py:186
  164.3 2.4 %multiply_convert_fusion = (bf16[256,1024]{1,0:T(8,128)(2,1)}, f32[256,1024]{1,0:T(8,128)S(1)}) fusion(f32[256,1024]{1,0:T(8,128)S(1)} %copy.124, bf16[256,1024]{1,0:T(8,128)(2,1)S(1)} %copy-done.8, f32[256]{0:T(256)S(1)} %copy-done.26, bf16[256,1024]{1,0:T(8,128)(2,1)S(1)} %copy-done.6, bf16[2,1024]{1,0:T(2,128)(2,1)} %collective-permute-done, ...), kind=kLoop, calls=%fused_computation.50 | loop fusion | flops 6815744 | bytes 3688448 | tf_op jit(solution)/shard_map/convert_element_type | solution.py:209
  166.7 4.4 %collective-permute-start.1 = (f32[2,1024]{1,0:T(2,128)S(1)}, f32[2,1024]{1,0:T(2,128)S(1)}, u32[]{:S(2)}, u32[]{:S(2)}) collective-permute-start(f32[2,1024]{1,0:T(2,128)S(1)} %slice.450), channel_id=1, source_target_pairs={{8,0},{16,8},{24,16},{32,24},{40,32},{48,40},{56,48},{64,56},{72,6... | collective-permute-start | bytes 24584 | tf_op jit(solution)/shard_map/ppermute | solution.py:23
  171.6 2.4 %gather_fusion.5 = f32[256,8,256]{2,1,0:T(8,128)} fusion(f32[8,136,256]{2,0,1:T(8,128)S(1)} %copy.122, s32[1024]{0:T(1024)S(1)} %pad_clamp_fusion.1), kind=kCustom, calls=%fused_computation.1.clone | custom fusion | bytes 4195328 | tf_op jit(solution)/shard_map/jit(_take)/gather | solution.py:59
  174.0 2.0 %bitcast_multiply_fusion = (f32[8,256,256]{2,0,1:T(8,128)S(1)}, f32[8,256,256]{2,0,1:T(8,128)S(1)}) fusion(f32[256,8,256]{2,1,0:T(8,128)} %gather_fusion.5, f32[256]{0:T(256)S(1)} %copy-done.38, f32[256,8,256]{2,1,0:T(8,128)S(1)} %copy-done), kind=kLoop, calls=%fused_computation.6 | loop fusion | flops 1048576 | bytes 8389632 | tf_op jit(solution)/shard_map/mul | solution.py:59
  176.1 1.4 copy-done.1
  177.6 1.6 fusion.17
  179.4 1.5 fusion.16
  180.9 0.7 copy.128
  181.6 0.7 copy.127
  182.4 1.2 fusion.23
  (198 shorter events, 16.5 us)
Async XLA Ops:
  1.9 37.1 %collective-permute-start = (bf16[2,1024]{1,0:T(2,128)(2,1)}, bf16[2,1024]{1,0:T(2,128)(2,1)}, u32[]{:S(2)}, u32[]{:S(2)}) collective-permute-start(bf16[2,1024]{1,0:T(2,128)(2,1)} %slice.274), channel_id=1, source_target_pairs={{0,8},{8,16},{16,24},{24,32},{32,40},{40,48},{48,56},{56,64},{64,7... | collective-permute-start | bytes 12296 | tf_op jit(solution)/shard_map/ppermute | solution.py:23
  10.0 5.9 %copy-start.34 = (s32[32]{0:T(128)}, s32[32]{0:T(128)S(1)}, u32[]{:S(2)}) copy-start(s32[32]{0:T(128)S(1)} %reduce.2) | copy-start | bytes 388
  22.9 5.3 %copy-start.20 = (f32[8,15,256]{2,1,0:T(8,128)S(1)}, f32[8,15,256]{2,1,0:T(8,128)}, u32[]{:S(2)}) copy-start(f32[8,15,256]{2,1,0:T(8,128)} %slice_multiply_fusion.15) | copy-start | bytes 368644
  33.9 2.0 %copy-start.32 = (s32[258]{0:T(512)S(1)}, s32[258]{0:T(512)}, u32[]{:S(2)}) copy-start(s32[258]{0:T(512)} %get-tuple-element.87) | copy-start | bytes 3100
  33.9 2.0 %copy-start.33 = (s32[258]{0:T(512)S(1)}, s32[258]{0:T(512)}, u32[]{:S(2)}) copy-start(s32[258]{0:T(512)} %get-tuple-element.88) | copy-start | bytes 3100
  33.9 4.5 %copy-start.13 = (f32[8,16,256]{2,1,0:T(8,128)S(1)}, f32[8,16,256]{2,1,0:T(8,128)}, u32[]{:S(2)}) copy-start(f32[8,16,256]{2,1,0:T(8,128)} %get-tuple-element.56) | copy-start | bytes 393220
  34.0 4.5 %copy-start.29 = (f32[153]{0:T(256)S(1)}, f32[153]{0:T(256)}, u32[]{:S(2)}) copy-start(f32[153]{0:T(256)} %pad.29.clone) | copy-start | bytes 1840
  35.9 3.1 %copy-start.5 = (bf16[256,1024]{1,0:T(8,128)(2,1)S(1)}, bf16[256,1024]{1,0:T(8,128)(2,1)}, u32[]{:S(2)}) copy-start(bf16[256,1024]{1,0:T(8,128)(2,1)} %param.18) | copy-start | bytes 1572868
  36.0 3.1 %copy-start.7 = (bf16[256,1024]{1,0:T(8,128)(2,1)S(1)}, bf16[256,1024]{1,0:T(8,128)(2,1)}, u32[]{:S(2)}) copy-start(bf16[256,1024]{1,0:T(8,128)(2,1)} %param.19) | copy-start | bytes 1572868
  38.5 2.1 %copy-start.25 = (f32[256]{0:T(256)}, f32[256]{0:T(256)S(1)}, u32[]{:S(2)}) copy-start(f32[256]{0:T(256)S(1)} %get-tuple-element.85) | copy-start | bytes 3076
  38.5 2.1 %copy-start.27 = (f32[256]{0:T(256)}, f32[256]{0:T(256)S(1)}, u32[]{:S(2)}) copy-start(f32[256]{0:T(256)S(1)} %get-tuple-element.86) | copy-start | bytes 3076
  38.5 2.1 %copy-start.14 = (f32[8,16,256]{2,1,0:T(8,128)S(1)}, f32[8,16,256]{2,1,0:T(8,128)}, u32[]{:S(2)}) copy-start(f32[8,16,256]{2,1,0:T(8,128)} %get-tuple-element.56) | copy-start | bytes 393220
  40.6 41.6 %copy-start.9 = (bf16[32,8,8,128]{3,2,1,0:T(8,128)(2,1)}, bf16[32,8,8,128]{3,2,1,0:T(8,128)(2,1)S(1)}, u32[]{:S(2)}) copy-start(bf16[32,8,8,128]{3,2,1,0:T(8,128)(2,1)S(1)} %fusion.43) | copy-start | bytes 1572868
  41.4 12.0 %copy-start.35 = (s32[32]{0:T(128)S(1)}, s32[32]{0:T(128)}, u32[]{:S(2)}) copy-start(s32[32]{0:T(128)} %copy-done.34) | copy-start | bytes 388
  42.3 30.6 %all-to-all-start = ((f32[32,39,128]{2,1,0:T(8,128)}), f32[32,39,128]{2,1,0:T(8,128)S(1)}, u32[]{:S(2)}, u32[]{:S(2)}) async-start(f32[32,39,128]{2,1,0:T(8,128)} %reshape.390), calls=%async_computation | async-start | bytes 1310720 | tf_op jit(solution)/shard_map/all_to_all | solution.py:100
  74.5 5.6 %copy-start.19 = (bf16[256,1024]{1,0:T(8,128)(2,1)S(1)}, bf16[256,1024]{1,0:T(8,128)(2,1)}, u32[]{:S(2)}) copy-start(bf16[256,1024]{1,0:T(8,128)(2,1)} %param.22) | copy-start | bytes 1572868
  74.5 24.4 %all-to-all-start.1 = ((f32[32,39,128]{2,1,0:T(8,128)}), f32[32,39,128]{2,1,0:T(8,128)S(1)}, u32[]{:S(2)}, u32[]{:S(2)}) async-start(f32[32,39,128]{2,1,0:T(8,128)} %copy.108), calls=%async_computation.1 | async-start | bytes 1310720 | tf_op jit(solution)/shard_map/all_to_all | solution.py:102
  82.2 1.3 copy-start.40
  98.9 1.8 copy-start.24
  98.9 1.8 copy-start.30
  99.0 1.8 copy-start.15
  99.8 1.5 copy-start.16
  109.5 8.6 %copy-start.39 = (s32[256]{0:T(256)S(1)}, s32[256]{0:T(256)}, u32[]{:S(2)}) copy-start(s32[256]{0:T(256)} %constant.113) | copy-start | bytes 3076
  109.5 8.6 %copy-start.23 = (bf16[256,8,128]{0,2,1:T(8,128)(2,1)S(1)}, bf16[256,8,128]{0,2,1:T(8,128)(2,1)}, u32[]{:S(2)}) copy-start(bf16[256,8,128]{0,2,1:T(8,128)(2,1)} %get-tuple-element.38) | copy-start | bytes 1572868
  109.5 24.3 %all-to-all-start.2 = ((f32[32,39,128]{2,1,0:T(8,128)}), f32[32,39,128]{2,1,0:T(8,128)S(1)}, u32[]{:S(2)}, u32[]{:S(2)}) async-start(f32[32,39,128]{2,1,0:T(8,128)} %reshape.400), calls=%async_computation.2 | async-start | bytes 1310720 | tf_op jit(solution)/shard_map/all_to_all | solution.py:100
  135.4 5.5 %copy-start.17 = (f32[256,1024]{0,1:T(8,128)S(1)}, f32[256,1024]{0,1:T(8,128)}, u32[]{:S(2)}) copy-start(f32[256,1024]{0,1:T(8,128)} %copy.109) | copy-start | bytes 3145732
  135.4 24.1 %all-to-all-start.3 = ((f32[32,39,128]{2,1,0:T(8,128)}), f32[32,39,128]{2,1,0:T(8,128)S(1)}, u32[]{:S(2)}, u32[]{:S(2)}) async-start(f32[32,39,128]{2,1,0:T(8,128)} %copy.120), calls=%async_computation.3 | async-start | bytes 1310720 | tf_op jit(solution)/shard_map/all_to_all | solution.py:102
  142.8 1.1 copy-start.12
  146.7 4.5 %copy-start.10 = (bf16[32,8,8,128]{3,2,1,0:T(8,128)(2,1)S(1)}, bf16[32,8,8,128]{3,2,1,0:T(8,128)(2,1)}, u32[]{:S(2)}) copy-start(bf16[32,8,8,128]{3,2,1,0:T(8,128)(2,1)} %copy-done.9) | copy-start | bytes 1572868
  146.7 4.5 %copy-start.18 = (f32[256,1024]{0,1:T(8,128)S(1)}, f32[256,1024]{0,1:T(8,128)}, u32[]{:S(2)}) copy-start(f32[256,1024]{0,1:T(8,128)} %copy.109) | copy-start | bytes 3145732
  146.7 4.5 %copy-start.41 = (f32[8,256,256]{1,2,0:T(8,128)S(1)}, f32[8,256,256]{1,2,0:T(8,128)}, u32[]{:S(2)}) copy-start(f32[8,256,256]{1,2,0:T(8,128)} %copy-done.40) | copy-start | bytes 6291460
  159.6 0.7 copy-start.31
  162.6 1.0 copy-start.11
  163.0 1.3 copy-start.6
  163.0 1.3 copy-start.8
  163.0 1.3 copy-start.26
  163.0 1.3 copy-start.28
  164.3 6.8 %copy-start.2 = (f32[8,153,256]{2,1,0:T(8,128)}, f32[8,153,256]{2,1,0:T(8,128)S(1)}, u32[]{:S(2)}) copy-start(f32[8,153,256]{2,1,0:T(8,128)S(1)} %fusion.1) | copy-start | bytes 3760132
  166.7 4.5 %copy-start.3 = (f32[256,1024]{1,0:T(8,128)}, f32[256,1024]{1,0:T(8,128)S(1)}, u32[]{:S(2)}) copy-start(f32[256,1024]{1,0:T(8,128)S(1)} %get-tuple-element.36) | copy-start | bytes 3145732
  166.7 15.7 %collective-permute-start.1 = (f32[2,1024]{1,0:T(2,128)S(1)}, f32[2,1024]{1,0:T(2,128)S(1)}, u32[]{:S(2)}, u32[]{:S(2)}) collective-permute-start(f32[2,1024]{1,0:T(2,128)S(1)} %slice.450), channel_id=1, source_target_pairs={{8,0},{16,8},{24,16},{32,24},{40,32},{48,40},{56,48},{64,56},{72,6... | collective-permute-start | bytes 24584 | tf_op jit(solution)/shard_map/ppermute | solution.py:23
  171.6 2.4 %copy-start = (f32[256,8,256]{2,1,0:T(8,128)S(1)}, f32[256,8,256]{2,1,0:T(8,128)}, u32[]{:S(2)}) copy-start(f32[256,8,256]{2,1,0:T(8,128)} %gather_fusion.4) | copy-start | bytes 6291460
  171.6 2.4 %copy-start.38 = (f32[256]{0:T(256)S(1)}, f32[256]{0:T(256)}, u32[]{:S(2)}) copy-start(f32[256]{0:T(256)} %constant.86.clone) | copy-start | bytes 3076
  174.0 2.0 %copy-start.22 = (f32[8,256,16]{1,0,2:T(8,128)S(1)}, f32[8,256,16]{1,0,2:T(8,128)}, u32[]{:S(2)}) copy-start(f32[8,256,16]{1,0,2:T(8,128)} %copy.190) | copy-start | bytes 393220
  176.0 1.6 copy-start.1
  177.5 1.6 copy-start.21
  179.3 3.0 %copy-start.4 = (f32[256,1024]{1,0:T(8,128)S(1)}, f32[256,1024]{1,0:T(8,128)}, u32[]{:S(2)}) copy-start(f32[256,1024]{1,0:T(8,128)} %copy-done.3) | copy-start | bytes 3145732
  179.4 3.0 %copy-start.36 = (f32[256]{0:T(256)S(1)}, f32[256]{0:T(256)}, u32[]{:S(2)}) copy-start(f32[256]{0:T(256)} %get-tuple-element.78) | copy-start | bytes 3076
  179.4 3.0 %copy-start.37 = (f32[256]{0:T(256)S(1)}, f32[256]{0:T(256)}, u32[]{:S(2)}) copy-start(f32[256]{0:T(256)} %get-tuple-element.79) | copy-start | bytes 3076

commit v2 on v1

--- a/solution.py
+++ b/solution.py
@@ -31,34 +31,34 @@
 
 def pair_tables(width):
     rows, cols = np.triu_indices(width)
-    weight = np.where(rows == cols, quad_scale, quad_scale * math.sqrt(2.0)).astype(np.float32)
-    place = np.zeros((width, width), np.int32)
-    place[rows, cols] = np.arange(rows.size)
-    place[cols, rows] = np.arange(rows.size)
-    spread_weight = np.where(np.eye(width, dtype=bool), 2.0, 1.0) * weight[place]
-    return rows, cols, weight, place.reshape(-1), spread_weight.astype(np.float32).reshape(-1)
+    quad_weight = np.where(rows == cols, quad_scale, quad_scale * math.sqrt(2.0))
+    first = np.concatenate([[-1], np.full(width, -1), rows])
+    second = np.concatenate([[-1], np.arange(width), cols])
+    scale = np.concatenate([[1.0], np.full(width, 0.5), quad_weight]).astype(np.float32)
+    dims = np.arange(width)
+    pick_first = (first[:, None] == dims[None, :]).astype(np.float32)
+    pick_second = (second[:, None] == dims[None, :]).astype(np.float32)
+    return pick_first, (first < 0).astype(np.float32), pick_second, (second < 0).astype(np.float32), scale
 
 
 def feature_rows(values):
-    spread = jnp.transpose(values, (1, 2, 0))
-    head_count, width, token_count = spread.shape
-    rows, cols, weight, _, _ = pair_tables(width)
-    ones_row = jnp.ones((head_count, 1, token_count), jnp.float32)
-    pieces = []
-    for i in range(width):
-        pieces.append(spread[:, i : i + 1, :] * spread[:, i:, :])
-    outer = jnp.concatenate(pieces, axis=1) * jnp.asarray(weight)[None, :, None]
-    return (jnp.concatenate([ones_row, 0.5 * spread, outer], axis=1), spread)
-
-
-def feature_grad(grad_phi, spread):
-    head_count, width, token_count = spread.shape
-    _, _, _, place, spread_weight = pair_tables(width)
-    linear = 0.5 * grad_phi[:, 1 : 1 + width]
-    quad = grad_phi[:, 1 + width :]
-    paired = jnp.take(quad, jnp.asarray(place), axis=1) * jnp.asarray(spread_weight)[None, :, None]
-    paired = paired.reshape(head_count, width, width, token_count)
-    return linear + jnp.einsum("hijt,hjt->hit", paired, spread, precision=high)
+    token_count, head_count, width = values.shape
+    pick_first, one_first, pick_second, one_second, scale = pair_tables(width)
+    picks = jnp.asarray(np.stack([pick_first, pick_second]), jnp.bfloat16)
+    chosen = jnp.einsum("pfd,thd->phft", picks, values, preferred_element_type=jnp.float32)
+    left = chosen[0] + jnp.asarray(one_first)[None, :, None]
+    right = chosen[1] + jnp.asarray(one_second)[None, :, None]
+    return (jnp.asarray(scale)[None, :, None] * left * right, (left, right))
+
+
+def feature_grad(grad_phi, factors):
+    left, right = factors
+    width = 16
+    pick_first, _, pick_second, _, scale = pair_tables(width)
+    scaled = grad_phi * jnp.asarray(scale)[None, :, None]
+    picks = jnp.asarray(np.concatenate([pick_first, pick_second], axis=0))
+    both = jnp.concatenate([scaled * right, scaled * left], axis=1)
+    return jnp.einsum("fd,hft->thd", picks, both, precision=high)
 
 
 def block_flags(doc_lengths, devices, rows):
@@ -155,8 +155,8 @@
     weights = jnp.where(allowed[None], kernel, 0.0)
     numerator = jnp.einsum("hts,shv->thv", weights, v_float, precision=high)
     denominator = jnp.transpose(jnp.sum(weights, axis=2), (1, 0))
-    phi_query, spread_query = feature_rows(q_float)
-    phi_key, spread_key = feature_rows(k_float)
+    phi_query, spread_query = feature_rows(query.reshape(tok_rows, HEADS, KD))
+    phi_key, spread_key = feature_rows(key.reshape(tok_rows, HEADS, KD))
     last_mask = (doc_ids == doc_ids[tok_rows - 1]).astype(jnp.float32)
     masked_key = phi_key * last_mask[None, None, :]
     local_state = jnp.einsum("hft,thv->hfv", masked_key, v_float, precision=high)
@@ -201,8 +201,8 @@
         jnp.einsum("hfv,shv->hfs", grad_state_in, v_float, precision=high)
         + grad_norm_in[:, :, None]
     )
-    grad_q = grad_q + jnp.transpose(feature_grad(grad_phi_query, spread_query), (2, 0, 1))
-    grad_k = grad_k + jnp.transpose(feature_grad(grad_phi_key, spread_key), (2, 0, 1))
+    grad_q = grad_q + feature_grad(grad_phi_query, spread_query)
+    grad_k = grad_k + feature_grad(grad_phi_key, spread_key)
     grad_query = grad_q.reshape(tok_rows, HEADS * KD).astype(jnp.bfloat16)
     grad_key = grad_k.reshape(tok_rows, HEADS * KD).astype(jnp.bfloat16)
     grad_core = grad_v.reshape(tok_rows, channels)

time: 185 us -> 189 us (1.022)
  other arithmetic: 27.3 us -> 19.7 us
  matrix products: 25.6 us -> 33.1 us
  waiting for transfers between devices: 51.4 us -> 55.2 us
    mul x34 -> x0, other arithmetic: 13.2 us -> none  [the longest x30 7.81 us: feature_rows(): pieces.append(spread[:, i:i + 1, :] * spread[:, i:, :])]
    concatenate x3 -> x0, local copies, waits for them, and re-layouts: 10.4 us -> none  [the longest x2 9.82 us: feature_rows(): outer = jnp.concatenate(pieces, axis=1) * jnp.asarray(weight)[None, :, None]]
    gather x2 -> x0, local copies, waits for them, and re-layouts: 4.69 us -> none  [feature_grad(): jnp.take(quad, jnp.asarray(place), axis=1)]
    pad x2, local copies, waits for them, and re-layouts: 0.09 us -> 3.99 us  [state_scan(): packed = jnp.pad(packed, ((0, spare), (0, 0)))]
    reshape x2, local copies, waits for them, and re-layouts: 0.09 us -> 3.93 us  [state_scan(): packed = jnp.concatenate([local_state, flat_norm.reshape(heads, norm_rows...]
    dot_general x0 -> x4, matrix products: none -> 3.47 us  [the longest x2 1.82 us: feature_rows(): jnp.einsum('pfd,thd->phft', picks, values, preferred_element_type=jnp.flo...]
    unnamed x111 -> x45, local copies, waits for them, and re-layouts: 11.8 us -> 8.44 us
    all_to_all x2, waiting for transfers between devices: 19.2 us -> 22.5 us  [state_scan(): back = lax.all_to_all(summed, 'ctx', 0, 0, tiled=True).reshape(-1, width)]
  transfers between devices with their start and end apart: 6 -> 6, of which waited for: 4 -> 4; matrix products, arithmetic and copies ran while one was open for 35% -> 20% of each run, Pallas kernels for 0% -> 0%
where the time goes in v2:
time: 189 us; the launch traced here: 187 us
  waiting for transfers between devices  55.2 us (29%)
  local copies, waits for them, and re-layouts  42.4 us (22%)
  starting transfers between devices  35.3 us (19%)
  matrix products  33.1 us (18%)
  other arithmetic  19.7 us (10%)
    all_to_all x2, waiting for transfers between devices, state_scan(): chunks = lax.all_to_all(packed, 'ctx', 0, 0, tiled=True)  32.7 us
    all_to_all x2, waiting for transfers between devices, state_scan(): back = lax.all_to_all(summed, 'ctx', 0, 0, tiled=True).reshape(-1, width)  22.5 us
    all_to_all x2, starting transfers between devices, state_scan(): chunks = lax.all_to_all(packed, 'ctx', 0, 0, tiled=True)  16.6 us
    all_to_all x2, starting transfers between devices, state_scan(): back = lax.all_to_all(summed, 'ctx', 0, 0, tiled=True).reshape(-1, width)  10.9 us
    unnamed x45, local copies, waits for them, and re-layouts  8.44 us
    ppermute x2, starting transfers between devices, shifted(): return lax.ppermute(block, axis, route)  7.85 us
    pad x2, local copies, waits for them, and re-layouts, state_scan(): packed = jnp.pad(packed, ((0, spare), (0, 0)))  3.99 us
    reshape x2, local copies, waits for them, and re-layouts, state_scan(): packed = packed.reshape(devices, -1, width)  3.95 us
  transfers between devices with their start and end apart: 6, of which 4 were waited for; matrix products, arithmetic and copies ran while one was open for 20% of the time, Pallas kernels for 0%

profile of v2, /device:TPU:32, one launch (start us, length us, event | category | flops | bytes accessed | tf_op | source)
XLA Modules:
  0.0 186.8 jit_solution(3996464515320141735)
XLA Ops:
  0.6 0.7 slice.92
  1.4 3.5 %collective-permute-start = (bf16[2,1024]{1,0:T(2,128)(2,1)S(1)}, bf16[2,1024]{1,0:T(2,128)(2,1)S(1)}, u32[]{:S(2)}, u32[]{:S(2)}) collective-permute-start(bf16[2,1024]{1,0:T(2,128)(2,1)S(1)} %slice.92), channel_id=1, source_target_pairs={{0,8},{8,16},{16,24},{24,32},{32,40},{40,48},{48,56},{56,64},{64,7... | collective-permute-start | bytes 12296 | tf_op jit(solution)/shard_map/ppermute | solution.py:23
  4.9 0.7 broadcast_add_fusion.3
  5.5 0.7 copy.106
  6.7 0.7 compare_select_fusion
  9.3 0.9 copy.107
  10.2 0.9 copy.108
  11.2 1.3 convolution_bitcast_fusion
  13.1 2.1 %compare_convert_fusion.1 = (f32[256]{0:T(256)S(1)}, f32[256]{0:T(256)S(1)}, f32[256]{0:T(256)S(1)}, f32[256]{0:T(256)S(1)}, f32[256]{0:T(256)S(1)}, /*index=5*/f32[256]{0:T(256)S(1)}, f32[256]{0:T(256)S(1)}) fusion(s32[256]{0:T(256)S(1)} %get-tuple-element.33, s32[258]{0:T(512)S(1)} %get-tuple-element.61, s32[]{:T(128)} %bitcast.38, s32[]{:T(128)} %bitcast.17, ...), kind=kLoop, calls=%fused_computation.141 | loop fusion | flops 3584 | bytes 12300 | tf_op jit(solution)/shard_map/convert_element_type | solution.py:216
  15.2 2.0 %multiply_reduce_fusion = (f32[8,153]{1,0:T(8,128)S(1)}, f32[8,153,256]{2,1,0:T(8,128)}, f32[8,153,256]{2,1,0:T(8,128)}) fusion(f32[256]{0:T(256)S(1)} %get-tuple-element.57, f32[153]{0:T(256)S(1)} %copy-done.14, f32[2,8,153,256]{3,2,1,0:T(8,128)S(1)} %convolution_bitcast_fusion.1, f32[153]{0:T(256)S(1)} %copy-done.13, f32[153]{0:T(256)S(1)} %copy-done.15, ...), kind=kLoop, calls=%fused_computation.42 | loop fusion | flops 3132216 | bytes 7528012 | tf_op jit(solution)/shard_map/reduce_sum | solution.py:163
  17.3 2.4 %fusion.57 = bf16[32,8,8,128]{3,2,1,0:T(8,128)(2,1)S(1)} fusion(bf16[256,1024]{1,0:T(8,128)(2,1)} %param.23, f32[256]{0:T(256)S(1)} %get-tuple-element.59, bf16[256,1024]{1,0:T(8,128)(2,1)} %param.22, bf16[2,1024]{1,0:T(2,128)(2,1)S(1)} %collective-permute-done, f32[1024]{0:T(1024)S(1)} %bitcast.168, f32[256]{0:T(256)S(1)} %get-tuple-element.60, ...), kind=kLoop, calls=%fused_computation.90 | loop fusion | flops 5767168 | bytes 1591296
  20.3 0.9 pad_maximum_fusion.1
  21.2 2.0 %reshape.382 = f32[1240,128]{1,0:T(8,128)} reshape(f32[8,155,128]{2,1,0:T(8,128)} %pad_maximum_fusion.1) | data formatting | bytes 1269760 | tf_op jit(solution)/shard_map/reshape | solution.py:96
  23.2 2.0 %pad.15 = f32[1248,128]{1,0:T(8,128)} pad(f32[1240,128]{1,0:T(8,128)} %reshape.382, f32[]{:T(128)} %constant.72.clone.1), padding=0_8x0_0 | pad | bytes 1273860 | tf_op jit(solution)/shard_map/jit(_pad)/pad | solution.py:98
  25.1 2.0 %reshape.383 = f32[32,39,128]{2,1,0:T(8,128)} reshape(f32[1248,128]{1,0:T(8,128)} %pad.15) | data formatting | bytes 1277952 | tf_op jit(solution)/shard_map/reshape | solution.py:99
  27.1 11.1 %all-to-all-start = ((f32[32,39,128]{2,1,0:T(8,128)}), f32[32,39,128]{2,1,0:T(8,128)}, u32[]{:S(2)}, u32[]{:S(2)}) async-start(f32[32,39,128]{2,1,0:T(8,128)} %reshape.383), calls=%async_computation | async-start | bytes 1310720 | tf_op jit(solution)/shard_map/all_to_all | solution.py:100
  38.8 0.7 gather_fusion.1
  39.5 0.7 gather_fusion
  40.2 17.6 %all-to-all-done = f32[32,39,128]{2,1,0:T(8,128)} async-done(((f32[32,39,128]{2,1,0:T(8,128)}), f32[32,39,128]{2,1,0:T(8,128)}, u32[]{:S(2)}, u32[]{:S(2)}) %all-to-all-start) | async-done | bytes 639008 | tf_op jit(solution)/shard_map/all_to_all | solution.py:100
  57.8 1.5 fusion.47
  59.3 1.2 copy.114
  60.5 5.5 %all-to-all-start.1 = ((f32[32,39,128]{2,1,0:T(8,128)}), f32[32,39,128]{2,1,0:T(8,128)}, u32[]{:S(2)}, u32[]{:S(2)}) async-start(f32[32,39,128]{2,1,0:T(8,128)} %copy.114), calls=%async_computation.1 | async-start | bytes 1310720 | tf_op jit(solution)/shard_map/all_to_all | solution.py:102
  66.0 2.3 %copy.115 = f32[256,1024]{0,1:T(8,128)} copy(bf16[256,1024]{1,0:T(8,128)(2,1)} %param.26) | data formatting | bytes 1572864 | tf_op jit(solution)/shard_map/reshape | solution.py:176
  68.3 0.8 fusion.54
  69.1 1.3 copy-done.16
  70.5 2.0 %fusion.55 = f32[8,128,256]{2,1,0:T(8,128)} fusion(f32[8,256,256]{1,2,0:T(8,128)S(1)} %get-tuple-element.68, pred[256,256]{0,1:T(8,128)(4,1)S(1)} %fusion.66, bf16[32,8,8,128]{3,2,1,0:T(8,128)(2,1)S(1)} %fusion.57), kind=kOutput, calls=%fused_computation.86 | convolution fusion | flops 405798912 | bytes 3735552 | tf_op jit(solution)/shard_map/hts,shv->thv/dot_general | solution.py:156
  72.5 12.4 %all-to-all-done.1 = f32[32,39,128]{2,1,0:T(8,128)} async-done(((f32[32,39,128]{2,1,0:T(8,128)}), f32[32,39,128]{2,1,0:T(8,128)}, u32[]{:S(2)}, u32[]{:S(2)}) %all-to-all-start.1) | async-done | bytes 639008 | tf_op jit(solution)/shard_map/all_to_all | solution.py:102
  84.8 2.0 %reshape.384 = f32[1248,128]{1,0:T(8,128)} reshape(f32[32,39,128]{2,1,0:T(8,128)} %all-to-all-done.1) | data formatting | bytes 1277952 | tf_op jit(solution)/shard_map/reshape | solution.py:102
  86.8 1.9 %slice.134 = f32[1240,128]{1,0:T(8,128)} slice(f32[1248,128]{1,0:T(8,128)} %reshape.384), slice={[0:1240], [0:128]} | slice | bytes 1269760 | tf_op jit(solution)/shard_map/slice | solution.py:103
  88.8 2.0 %reshape.385 = f32[8,155,128]{2,1,0:T(8,128)} reshape(f32[1240,128]{1,0:T(8,128)} %slice.134) | data formatting | bytes 1269760 | tf_op jit(solution)/shard_map/reshape | solution.py:103
  90.8 0.9 slice_bitcast_fusion.5
  91.7 1.7 fusion.75
  93.4 3.8 %multiply_reduce_fusion.1 = (f32[256,8]{0,1:T(8,128)S(1)}, bf16[256,8,128]{0,2,1:T(8,128)(2,1)}) fusion(f32[256,1024]{0,1:T(8,128)} %copy.115, f32[256,8]{0,1:T(8,128)S(1)} %fusion.83, f32[8,128,256]{2,1,0:T(8,128)} %fusion.55, f32[8,153,256]{2,1,0:T(8,128)S(1)} %copy-done.3, f32[8,155,128]{2,1,0:T(8,128)} %reshape.385, f32[256]{0:T(256)S(1)} %get-tuple-element.58), kind=kOutput, calls=%fused_computation.67 | convolution fusion | flops 242219008 | bytes 4527104 | tf_op jit(solution)/shard_map/hft,hfv->thv/dot_general | solution.py:168
  97.2 1.6 fusion.22
  99.5 2.0 %pad_maximum_fusion.2 = f32[8,155,128]{2,1,0:T(8,128)} fusion(f32[8,2,128]{2,1,0:T(2,128)S(1)} %reshape.390, f32[8,153,128]{2,1,0:T(8,128)} %fusion.22), kind=kLoop, calls=%fused_computation.72 | loop fusion | flops 158720 | bytes 1269760 | tf_op jit(solution)/shard_map/concatenate | solution.py:94
  101.5 2.0 %reshape.391 = f32[1240,128]{1,0:T(8,128)} reshape(f32[8,155,128]{2,1,0:T(8,128)} %pad_maximum_fusion.2) | data formatting | bytes 1269760 | tf_op jit(solution)/shard_map/reshape | solution.py:96
  103.5 2.0 %pad.17 = f32[1248,128]{1,0:T(8,128)} pad(f32[1240,128]{1,0:T(8,128)} %reshape.391, f32[]{:T(128)} %constant.72.clone.1), padding=0_8x0_0 | pad | bytes 1273860 | tf_op jit(solution)/shard_map/jit(_pad)/pad | solution.py:98
  105.5 2.0 %reshape.392 = f32[32,39,128]{2,1,0:T(8,128)} reshape(f32[1248,128]{1,0:T(8,128)} %pad.17) | data formatting | bytes 1277952 | tf_op jit(solution)/shard_map/reshape | solution.py:99
  107.5 5.5 %all-to-all-start.2 = ((f32[32,39,128]{2,1,0:T(8,128)}), f32[32,39,128]{2,1,0:T(8,128)}, u32[]{:S(2)}, u32[]{:S(2)}) async-start(f32[32,39,128]{2,1,0:T(8,128)} %reshape.392), calls=%async_computation.2 | async-start | bytes 1310720 | tf_op jit(solution)/shard_map/all_to_all | solution.py:100
  113.2 0.7 gather_fusion.3
  113.9 0.7 gather_fusion.2
  114.6 2.0 %copy.130 = bf16[256,1024]{1,0:T(8,128)(2,1)} copy(bf16[256,1024]{0,1:T(8,128)(2,1)} %bitcast.159) | data formatting | bytes 1048576
  116.7 15.1 %all-to-all-done.2 = f32[32,39,128]{2,1,0:T(8,128)} async-done(((f32[32,39,128]{2,1,0:T(8,128)}), f32[32,39,128]{2,1,0:T(8,128)}, u32[]{:S(2)}, u32[]{:S(2)}) %all-to-all-start.2) | async-done | bytes 639008 | tf_op jit(solution)/shard_map/all_to_all | solution.py:100
  131.7 1.5 fusion.45
  133.2 1.2 copy.125
  134.4 5.4 %all-to-all-start.3 = ((f32[32,39,128]{2,1,0:T(8,128)}), f32[32,39,128]{2,1,0:T(8,128)}, u32[]{:S(2)}, u32[]{:S(2)}) async-start(f32[32,39,128]{2,1,0:T(8,128)} %copy.125), calls=%async_computation.3 | async-start | bytes 1310720 | tf_op jit(solution)/shard_map/all_to_all | solution.py:102
  139.9 3.5 %fusion.9 = f32[8,153,256]{2,1,0:T(8,128)} fusion(f32[8,256]{1,0:T(8,128)S(1)} %bitcast_divide_fusion, f32[8,153]{1,0:T(8,128)S(1)} %get-tuple-element.44, f32[256]{0:T(256)S(1)} %get-tuple-element.58, f32[153]{0:T(256)S(1)} %copy-done.15, f32[8,155,128]{2,1,0:T(8,128)} %reshape.385, f32[256,8,128]{0,2,1:T(8,128)} %bitcast.149, f32[256,8]{0,1:T(8,128)S(1)} %fusion.83), kind=kOutput, calls=%fused_computation.18 | convolution fusion | flops 242163712 | bytes 2959748 | tf_op jit(solution)/shard_map/hfv,thv->hft/dot_general | solution.py:197
  143.4 2.5 %fusion.53 = f32[8,128,256]{2,1,0:T(8,128)} fusion(f32[8,256,256]{1,2,0:T(8,128)S(1)} %copy-done.17, pred[256,256]{0,1:T(8,128)(4,1)S(1)} %fusion.66, f32[256,8,128]{0,2,1:T(8,128)S(1)} %bitcast.151, f32[256,8]{0,1:T(8,128)S(1)} %fusion.83), kind=kOutput, calls=%fused_computation.84 | convolution fusion | flops 406061056 | bytes 4268032 | tf_op jit(solution)/shard_map/hts,thv->shv/dot_general | solution.py:185
  145.9 2.4 %multiply_select_fusion = f32[8,256,256]{1,2,0:T(8,128)} fusion(f32[8,256,256]{1,2,0:T(8,128)S(1)} %copy-done.17, f32[8,256]{1,0:T(8,128)S(1)} %bitcast_divide_fusion, pred[256,256]{0,1:T(8,128)(4,1)S(1)} %fusion.66, bf16[32,8,8,128]{3,2,1,0:T(8,128)(2,1)S(1)} %fusion.57, f32[256,8,128]{0,2,1:T(8,128)S(1)} %bitcast.152, f32[256,8]{0,1:T(8,128)S(1)} %fusion.83), kind=kOutput, calls=%fused_computation.12 | convolution fusion | flops 405536768 | bytes 5849088 | tf_op jit(solution)/shard_map/thv,shv->hts/dot_general | solution.py:190
  148.4 10.2 %all-to-all-done.3 = f32[32,39,128]{2,1,0:T(8,128)} async-done(((f32[32,39,128]{2,1,0:T(8,128)}), f32[32,39,128]{2,1,0:T(8,128)}, u32[]{:S(2)}, u32[]{:S(2)}) %all-to-all-start.3) | async-done | bytes 639008 | tf_op jit(solution)/shard_map/all_to_all | solution.py:102
  158.5 1.1 reshape.393
  159.7 0.9 slice.140
  160.6 1.1 reshape.394
  161.8 3.7 %fusion.12 = f32[8,128,256]{2,1,0:T(8,128)} fusion(f32[8,128,256]{2,1,0:T(8,128)} %fusion.53, f32[8,153,256]{2,1,0:T(8,128)} %get-tuple-element.35, f32[8,155,128]{2,1,0:T(8,128)S(1)} %reshape.394, f32[256]{0:T(256)S(1)} %get-tuple-element.32), kind=kOutput, calls=%fused_computation.23 | convolution fusion | flops 241172480 | bytes 3986432 | tf_op jit(solution)/shard_map/hfs,hfv->shv/dot_general | solution.py:186
  165.5 2.5 %copy.128 = f32[256,1024]{1,0:T(8,128)} copy(f32[256,1024]{0,1:T(8,128)} %bitcast.148) | data formatting | bytes 2097152 | tf_op jit(solution)/shard_map/reshape | solution.py:208
  168.0 3.7 %multiply_convert_fusion = (bf16[256,1024]{1,0:T(8,128)(2,1)}, f32[256,1024]{1,0:T(8,128)S(1)}) fusion(f32[256,1024]{1,0:T(8,128)} %copy.128, bf16[256,1024]{1,0:T(8,128)(2,1)} %param.23, f32[256]{0:T(256)S(1)} %get-tuple-element.59, bf16[256,1024]{1,0:T(8,128)(2,1)} %param.22, bf16[2,1024]{1,0:T(2,128)(2,1)S(1)} %collective-permute-done, ...), kind=kLoop, calls=%fused_computation.66 | loop fusion | flops 6815744 | bytes 3688448 | tf_op jit(solution)/shard_map/convert_element_type | solution.py:209
  171.7 4.4 %collective-permute-start.1 = (f32[2,1024]{1,0:T(2,128)S(1)}, f32[2,1024]{1,0:T(2,128)S(1)}, u32[]{:S(2)}, u32[]{:S(2)}) collective-permute-start(f32[2,1024]{1,0:T(2,128)S(1)} %slice.144), channel_id=1, source_target_pairs={{8,0},{16,8},{24,16},{32,24},{40,32},{48,40},{56,48},{64,56},{72,6... | collective-permute-start | bytes 24584 | tf_op jit(solution)/shard_map/ppermute | solution.py:23
  176.2 2.3 %fusion.29 = (f32[8,153,256]{2,1,0:T(8,128)S(1)}, f32[8,153,256]{2,1,0:T(8,128)S(1)}, f32[8,153,256]{2,1,0:T(8,128)S(1)}, f32[8,153,256]{2,1,0:T(8,128)S(1)}) fusion(f32[8,153,256]{2,1,0:T(8,128)} %fusion.9, f32[2,8,153,256]{3,2,1,0:T(8,128)S(1)} %convolution_bitcast_fusion, f32[153]{0:T(256)S(1)} %copy-done.14, f32[153]{0:T(256)S(1)} %copy-done.13, ...), kind=kOutput, calls=%fused_computation.48 | convolution fusion | flops 244094976 | bytes 12447308 | tf_op jit(solution)/shard_map/hfv,shv->hfs/dot_general | solution.py:201
  178.5 0.8 fusion.4
  179.3 0.8 copy-done.4
  180.7 0.8 fusion
  182.0 0.7 copy.132
  182.8 0.7 copy.131
  183.5 3.3 %fusion.39 = bf16[256,1024]{1,0:T(8,128)(2,1)} fusion(f32[256,1024]{1,0:T(8,128)} %copy-done.7, f32[2,1024]{1,0:T(2,128)S(1)} %collective-permute-done.1, f32[256]{0:T(256)S(1)} %get-tuple-element.50, f32[256]{0:T(256)S(1)} %get-tuple-element.49, f32[1024]{0:T(1024)S(1)} %bitcast.170, f32[1024]{0:T(1024)S(1)} %bitcast.167, f32[1024]{0:T(1024)S(1)} %bitcast.164), kind=kLoop, calls=%fused_computation.62 | loop fusion | flops 2621440 | bytes 1595392 | tf_op jit(solution)/shard_map/convert_element_type | solution.py:220
  (86 shorter events, 6.3 us)
Async XLA Ops:
  1.4 15.9 %collective-permute-start = (bf16[2,1024]{1,0:T(2,128)(2,1)S(1)}, bf16[2,1024]{1,0:T(2,128)(2,1)S(1)}, u32[]{:S(2)}, u32[]{:S(2)}) collective-permute-start(bf16[2,1024]{1,0:T(2,128)(2,1)S(1)} %slice.92), channel_id=1, source_target_pairs={{0,8},{8,16},{16,24},{24,32},{32,40},{40,48},{48,56},{56,64},{64,7... | collective-permute-start | bytes 12296 | tf_op jit(solution)/shard_map/ppermute | solution.py:23
  11.2 1.3 copy-start.11
  12.5 2.7 %copy-start.13 = (f32[153]{0:T(256)S(1)}, f32[153]{0:T(256)}, u32[]{:S(2)}) copy-start(f32[153]{0:T(256)} %constant.76.clone) | copy-start | bytes 1840
  12.5 2.7 %copy-start.14 = (f32[153]{0:T(256)S(1)}, f32[153]{0:T(256)}, u32[]{:S(2)}) copy-start(f32[153]{0:T(256)} %constant.77.clone) | copy-start | bytes 1840
  12.5 2.7 %copy-start.15 = (f32[153]{0:T(256)S(1)}, f32[153]{0:T(256)}, u32[]{:S(2)}) copy-start(f32[153]{0:T(256)} %constant.78.clone) | copy-start | bytes 1840
  13.0 4.2 %copy-start = (f32[2,8,153,256]{3,2,1,0:T(8,128)}, f32[2,8,153,256]{3,2,1,0:T(8,128)S(1)}, u32[]{:S(2)}) copy-start(f32[2,8,153,256]{3,2,1,0:T(8,128)S(1)} %convolution_bitcast_fusion.1) | copy-start | bytes 7520260
  15.2 2.0 %copy-start.12 = (bf16[3,1024]{1,0:T(4,128)(2,1)S(1)}, bf16[3,1024]{1,0:T(4,128)(2,1)}, u32[]{:S(2)}) copy-start(bf16[3,1024]{1,0:T(4,128)(2,1)} %param.24) | copy-start | bytes 18436
  17.3 2.5 %copy-start.2 = (f32[8,153,256]{2,1,0:T(8,128)S(1)}, f32[8,153,256]{2,1,0:T(8,128)}, u32[]{:S(2)}) copy-start(f32[8,153,256]{2,1,0:T(8,128)} %get-tuple-element.35) | copy-start | bytes 3760132
  19.7 126.2 %copy-start.5 = (bf16[32,8,8,128]{3,2,1,0:T(8,128)(2,1)}, bf16[32,8,8,128]{3,2,1,0:T(8,128)(2,1)S(1)}, u32[]{:S(2)}) copy-start(bf16[32,8,8,128]{3,2,1,0:T(8,128)(2,1)S(1)} %fusion.57) | copy-start | bytes 1572868
  27.1 30.7 %all-to-all-start = ((f32[32,39,128]{2,1,0:T(8,128)}), f32[32,39,128]{2,1,0:T(8,128)}, u32[]{:S(2)}, u32[]{:S(2)}) async-start(f32[32,39,128]{2,1,0:T(8,128)} %reshape.383), calls=%async_computation | async-start | bytes 1310720 | tf_op jit(solution)/shard_map/all_to_all | solution.py:100
  60.5 24.4 %all-to-all-start.1 = ((f32[32,39,128]{2,1,0:T(8,128)}), f32[32,39,128]{2,1,0:T(8,128)}, u32[]{:S(2)}, u32[]{:S(2)}) async-start(f32[32,39,128]{2,1,0:T(8,128)} %copy.114), calls=%async_computation.1 | async-start | bytes 1310720 | tf_op jit(solution)/shard_map/all_to_all | solution.py:102
  69.1 1.3 copy-start.16
  90.8 2.6 %copy-start.3 = (f32[8,153,256]{2,1,0:T(8,128)S(1)}, f32[8,153,256]{2,1,0:T(8,128)}, u32[]{:S(2)}) copy-start(f32[8,153,256]{2,1,0:T(8,128)} %get-tuple-element.51) | copy-start | bytes 3760132
  93.4 3.8 %copy-start.8 = (f32[256,1024]{0,1:T(8,128)S(1)}, f32[256,1024]{0,1:T(8,128)}, u32[]{:S(2)}) copy-start(f32[256,1024]{0,1:T(8,128)} %copy.115) | copy-start | bytes 3145732
  107.5 24.3 %all-to-all-start.2 = ((f32[32,39,128]{2,1,0:T(8,128)}), f32[32,39,128]{2,1,0:T(8,128)}, u32[]{:S(2)}, u32[]{:S(2)}) async-start(f32[32,39,128]{2,1,0:T(8,128)} %reshape.392), calls=%async_computation.2 | async-start | bytes 1310720 | tf_op jit(solution)/shard_map/all_to_all | solution.py:100
  134.4 24.1 %all-to-all-start.3 = ((f32[32,39,128]{2,1,0:T(8,128)}), f32[32,39,128]{2,1,0:T(8,128)}, u32[]{:S(2)}, u32[]{:S(2)}) async-start(f32[32,39,128]{2,1,0:T(8,128)} %copy.125), calls=%async_computation.3 | async-start | bytes 1310720 | tf_op jit(solution)/shard_map/all_to_all | solution.py:102
  139.9 3.6 %copy-start.9 = (f32[256,1024]{0,1:T(8,128)S(1)}, f32[256,1024]{0,1:T(8,128)}, u32[]{:S(2)}) copy-start(f32[256,1024]{0,1:T(8,128)} %copy.115) | copy-start | bytes 3145732
  139.9 3.6 %copy-start.17 = (f32[8,256,256]{1,2,0:T(8,128)S(1)}, f32[8,256,256]{1,2,0:T(8,128)}, u32[]{:S(2)}) copy-start(f32[8,256,256]{1,2,0:T(8,128)} %copy-done.16) | copy-start | bytes 6291460
  168.0 8.1 %copy-start.1 = (f32[2,8,153,256]{3,2,1,0:T(8,128)S(1)}, f32[2,8,153,256]{3,2,1,0:T(8,128)}, u32[]{:S(2)}) copy-start(f32[2,8,153,256]{3,2,1,0:T(8,128)} %copy-done) | copy-start | bytes 7520260
  168.0 8.1 %copy-start.6 = (bf16[32,8,8,128]{3,2,1,0:T(8,128)(2,1)S(1)}, bf16[32,8,8,128]{3,2,1,0:T(8,128)(2,1)}, u32[]{:S(2)}) copy-start(bf16[32,8,8,128]{3,2,1,0:T(8,128)(2,1)} %copy-done.5) | copy-start | bytes 1572868
  171.7 4.4 %copy-start.7 = (f32[256,1024]{1,0:T(8,128)}, f32[256,1024]{1,0:T(8,128)S(1)}, u32[]{:S(2)}) copy-start(f32[256,1024]{1,0:T(8,128)S(1)} %get-tuple-element.41) | copy-start | bytes 3145732
  171.7 11.8 %collective-permute-start.1 = (f32[2,1024]{1,0:T(2,128)S(1)}, f32[2,1024]{1,0:T(2,128)S(1)}, u32[]{:S(2)}, u32[]{:S(2)}) collective-permute-start(f32[2,1024]{1,0:T(2,128)S(1)} %slice.144), channel_id=1, source_target_pairs={{8,0},{16,8},{24,16},{32,24},{40,32},{48,40},{56,48},{64,56},{72,6... | collective-permute-start | bytes 24584 | tf_op jit(solution)/shard_map/ppermute | solution.py:23
  176.1 2.3 %copy-start.10 = (f32[306,16,1]{0,1,2:T(8,128)S(1)}, f32[306,16,1]{0,1,2:T(8,128)}, u32[]{:S(2)}) copy-start(f32[306,16,1]{0,1,2:T(8,128)} %constant.89) | copy-start | bytes 58756
  178.5 1.6 copy-start.4

commit v3 on v2

--- a/solution.py
+++ b/solution.py
@@ -35,6 +35,12 @@
     first = np.concatenate([[-1], np.full(width, -1), rows])
     second = np.concatenate([[-1], np.arange(width), cols])
     scale = np.concatenate([[1.0], np.full(width, 0.5), quad_weight]).astype(np.float32)
+    feats = scale.size
+    padded = -(-(feats + -(-feats // 128)) // 8) * 8
+    extra = padded - feats
+    first = np.concatenate([first, np.full(extra, width)])
+    second = np.concatenate([second, np.full(extra, width)])
+    scale = np.concatenate([scale, np.zeros(extra, np.float32)])
     dims = np.arange(width)
     pick_first = (first[:, None] == dims[None, :]).astype(np.float32)
     pick_second = (second[:, None] == dims[None, :]).astype(np.float32)
@@ -88,22 +94,16 @@
     devices = mask.shape[0]
     heads, feats, width = local_state.shape
     norm_rows = -(-feats // width)
-    head_rows = feats + norm_rows
-    spare = (-heads * head_rows) % devices
-    flat_norm = jnp.pad(local_norm, ((0, 0), (0, norm_rows * width - feats)))
-    packed = jnp.concatenate(
-        [local_state, flat_norm.reshape(heads, norm_rows, width)], axis=1
-    ).reshape(heads * head_rows, width)
-    if spare:
-        packed = jnp.pad(packed, ((0, spare), (0, 0)))
-    packed = packed.reshape(devices, -1, width)
+    room = feats - norm_rows
+    norm_block = jnp.pad(local_norm, ((0, 0), (0, norm_rows * width - feats)))
+    packed = lax.dynamic_update_slice(
+        local_state, norm_block.reshape(heads, norm_rows, width), (0, room, 0)
+    ).reshape(devices, -1, width)
     chunks = lax.all_to_all(packed, "ctx", 0, 0, tiled=True)
     summed = jnp.einsum("ij,jrc->irc", mask, chunks, precision=high)
-    back = lax.all_to_all(summed, "ctx", 0, 0, tiled=True).reshape(-1, width)
-    back = back[: heads * head_rows].reshape(heads, head_rows, width)
-    state_in = back[:, :feats]
-    norm_in = back[:, feats:].reshape(heads, norm_rows * width)[:, :feats]
-    return (state_in, norm_in)
+    back = lax.all_to_all(summed, "ctx", 0, 0, tiled=True).reshape(heads, feats, width)
+    norm_in = back[:, room:].reshape(heads, norm_rows * width)[:, :feats]
+    return (back, norm_in)
 
 
 def local(query, key, value_in, gate, conv_weight, doc_lengths, d_out):

time: 189 us -> 167 us (0.88)
  local copies, waits for them, and re-layouts: 42.4 us -> 24.1 us
    reshape x10 -> x2, local copies, waits for them, and re-layouts: 14.2 us -> 0.02 us  [state_scan(): norm_block.reshape(heads, norm_rows, width)]
    pad x4 -> x2, local copies, waits for them, and re-layouts: 4.01 us -> 0.02 us  [state_scan(): norm_block = jnp.pad(local_norm, ((0, 0), (0, norm_rows * width - feats)))]
    concatenate x2 -> x0, other arithmetic: 2.89 us -> none  [state_scan(): jnp.concatenate([local_state, flat_norm.reshape(heads, norm_rows, width)]...]
    slice x3 -> x1, local copies, waits for them, and re-layouts: 2.9 us -> 0.6 us  [state_scan(): norm_in = back[:, room:].reshape(heads, norm_rows * width)[:, :feats]]
    unnamed x45 -> x83, local copies, waits for them, and re-layouts: 8.44 us -> 10.3 us
  transfers between devices with their start and end apart: 6 -> 6, of which waited for: 4 -> 4; matrix products, arithmetic and copies ran while one was open for 20% -> 24% of each run, Pallas kernels for 0% -> 0%
where the time goes in v3:
time: 167 us; the launch traced here: 166 us
  waiting for transfers between devices  54.4 us (33%)
  starting transfers between devices  35.2 us (21%)
  matrix products  32.5 us (19%)
  local copies, waits for them, and re-layouts  24.1 us (14%)
  other arithmetic  18.4 us (11%)
    all_to_all x2, waiting for transfers between devices, state_scan(): chunks = lax.all_to_all(packed, 'ctx', 0, 0, tiled=True)  31.9 us
    all_to_all x2, waiting for transfers between devices, state_scan(): lax.all_to_all(summed, 'ctx', 0, 0, tiled=True).reshape(heads, feats, width)  22.4 us
    all_to_all x2, starting transfers between devices, state_scan(): chunks = lax.all_to_all(packed, 'ctx', 0, 0, tiled=True)  16.5 us
    all_to_all x2, starting transfers between devices, state_scan(): lax.all_to_all(summed, 'ctx', 0, 0, tiled=True).reshape(heads, feats, width)  10.8 us
    unnamed x83, local copies, waits for them, and re-layouts  10.3 us
    ppermute x2, starting transfers between devices, shifted(): return lax.ppermute(block, axis, route)  7.85 us
    convert_element_type x1, other arithmetic, local(): (grad_core * convolved * opening * (1.0 - opening)).astype(jnp.bfloat16)  3.72 us
    dot_general x1, matrix products, local(): jnp.einsum('hfs,hfv->shv', phi_key, grad_state_in, precision=high)  3.71 us
  transfers between devices with their start and end apart: 6, of which 4 were waited for; matrix products, arithmetic and copies ran while one was open for 24% of the time, Pallas kernels for 0%

profile of v3, /device:TPU:32, one launch (start us, length us, event | category | flops | bytes accessed | tf_op | source)
XLA Modules:
  0.0 165.9 jit_solution(17102121811026938597)
XLA Ops:
  0.6 0.7 slice.80
  1.4 3.5 %collective-permute-start = (bf16[2,1024]{1,0:T(2,128)(2,1)S(1)}, bf16[2,1024]{1,0:T(2,128)(2,1)S(1)}, u32[]{:S(2)}, u32[]{:S(2)}) collective-permute-start(bf16[2,1024]{1,0:T(2,128)(2,1)S(1)} %slice.80), channel_id=1, source_target_pairs={{0,8},{8,16},{16,24},{24,32},{32,40},{40,48},{48,56},{56,64},{64,7... | collective-permute-start | bytes 12296 | tf_op jit(solution)/shard_map/ppermute | solution.py:23
  4.9 0.7 broadcast_add_fusion.3
  5.5 0.7 copy.108
  6.5 0.2 fusion.82
  6.7 0.7 compare_select_fusion
  7.3 0.6 fusion.99
  8.0 1.2 compare_convert_fusion.5
  9.3 0.6 fusion.98
  9.8 0.9 copy.109
  10.8 0.9 copy.110
  11.7 1.3 convolution_bitcast_fusion
  13.1 0.5 convolution_bitcast_fusion.1
  13.7 2.7 %compare_convert_fusion.1 = (f32[256]{0:T(256)}, f32[256]{0:T(256)}, f32[256]{0:T(256)S(1)}, f32[256]{0:T(256)S(1)}, f32[256]{0:T(256)S(1)}, /*index=5*/f32[256]{0:T(256)S(1)}, f32[256]{0:T(256)S(1)}) fusion(s32[256]{0:T(256)S(1)} %get-tuple-element.33, s32[258]{0:T(512)S(1)} %get-tuple-element.61, s32[]{:T(128)} %bitcast.40, s32[]{:T(128)} %bitcast.17, ...), kind=kLoop, calls=%fused_computation.135 | loop fusion | flops 3584 | bytes 12300 | tf_op jit(solution)/shard_map/convert_element_type | solution.py:216
  16.4 1.9 %multiply_reduce_fusion = (f32[8,160]{1,0:T(8,128)S(1)}, f32[8,160,256]{2,1,0:T(8,128)}, f32[8,160,256]{2,1,0:T(8,128)}) fusion(f32[256]{0:T(256)S(1)} %get-tuple-element.57, f32[160]{0:T(256)S(1)} %copy-done.30, f32[2,8,160,256]{3,2,1,0:T(8,128)S(1)} %convolution_bitcast_fusion.1, f32[160]{0:T(256)S(1)} %copy-done.28, f32[160]{0:T(256)S(1)} %copy-done.32, ...), kind=kLoop, calls=%fused_computation.42 | loop fusion | flops 3275520 | bytes 7872384 | tf_op jit(solution)/shard_map/reduce_sum | solution.py:163
  18.4 2.4 %fusion.53 = bf16[32,8,8,128]{3,2,1,0:T(8,128)(2,1)S(1)} fusion(bf16[256,1024]{1,0:T(8,128)(2,1)} %param.23, f32[256]{0:T(256)S(1)} %get-tuple-element.59, bf16[256,1024]{1,0:T(8,128)(2,1)} %param.22, bf16[2,1024]{1,0:T(2,128)(2,1)S(1)} %collective-permute-done, f32[1024]{0:T(1024)S(1)} %bitcast.181, f32[256]{0:T(256)S(1)} %get-tuple-element.60, ...), kind=kLoop, calls=%fused_computation.84 | loop fusion | flops 5767168 | bytes 1591296
  20.9 0.5 fusion.24
  21.4 0.8 copy-done.9
  22.3 11.1 %all-to-all-start = ((f32[32,40,128]{2,1,0:T(8,128)}), f32[32,40,128]{2,1,0:T(8,128)}, u32[]{:S(2)}, u32[]{:S(2)}) async-start(f32[32,40,128]{2,1,0:T(8,128)} %bitcast.160), calls=%async_computation | async-start | bytes 1310720 | tf_op jit(solution)/shard_map/all_to_all | solution.py:102
  33.4 0.2 convert_reduce_fusion.2
  33.7 0.5 compare_convert_fusion.4
  34.5 0.7 gather_fusion.1
  35.2 0.7 gather_fusion
  35.9 17.1 %all-to-all-done = f32[32,40,128]{2,1,0:T(8,128)} async-done(((f32[32,40,128]{2,1,0:T(8,128)}), f32[32,40,128]{2,1,0:T(8,128)}, u32[]{:S(2)}, u32[]{:S(2)}) %all-to-all-start) | async-done | bytes 655392 | tf_op jit(solution)/shard_map/all_to_all | solution.py:102
  53.0 1.5 fusion.44
  54.4 1.2 copy.116
  55.7 5.5 %all-to-all-start.1 = ((f32[32,40,128]{2,1,0:T(8,128)}), f32[32,40,128]{2,1,0:T(8,128)}, u32[]{:S(2)}, u32[]{:S(2)}) async-start(f32[32,40,128]{2,1,0:T(8,128)} %copy.116), calls=%async_computation.1 | async-start | bytes 1310720 | tf_op jit(solution)/shard_map/all_to_all | solution.py:104
  61.2 2.3 %copy.117 = f32[256,1024]{0,1:T(8,128)} copy(bf16[256,1024]{1,0:T(8,128)(2,1)} %param.26) | data formatting | bytes 1572864 | tf_op jit(solution)/shard_map/reshape | solution.py:176
  63.5 0.8 fusion.50
  64.3 1.3 copy-done.35
  65.6 2.1 %fusion.51 = f32[8,128,256]{2,1,0:T(8,128)} fusion(f32[8,256,256]{1,2,0:T(8,128)S(1)} %get-tuple-element.68, pred[256,256]{0,1:T(8,128)(4,1)S(1)} %fusion.62, bf16[32,8,8,128]{3,2,1,0:T(8,128)(2,1)S(1)} %fusion.53), kind=kOutput, calls=%fused_computation.80 | convolution fusion | flops 405798912 | bytes 3735552 | tf_op jit(solution)/shard_map/hts,shv->thv/dot_general | solution.py:156
  67.7 12.3 %all-to-all-done.1 = f32[32,40,128]{2,1,0:T(8,128)} async-done(((f32[32,40,128]{2,1,0:T(8,128)}), f32[32,40,128]{2,1,0:T(8,128)}, u32[]{:S(2)}, u32[]{:S(2)}) %all-to-all-start.1) | async-done | bytes 655392 | tf_op jit(solution)/shard_map/all_to_all | solution.py:104
  80.0 0.9 slice_bitcast_fusion.5
  80.9 0.6 fusion.96
  81.5 1.7 %fusion.71 = f32[8,1,256]{2,1,0:T(1,128)S(1)} fusion(f32[8,160,256]{2,1,0:T(8,128)} %get-tuple-element.51, f32[8,160,1]{1,0,2:T(8,128)S(1)} %get-tuple-element.45), kind=kOutput, calls=%fused_computation.119 | convolution fusion | flops 1966080 | bytes 1324032 | tf_op jit(solution)/shard_map/hft,hf->th/dot_general | solution.py:171
  83.3 3.7 %multiply_reduce_fusion.1 = (f32[256,8]{0,1:T(8,128)S(1)}, bf16[256,8,128]{0,2,1:T(8,128)(2,1)}) fusion(f32[256,1024]{0,1:T(8,128)} %copy.117, f32[256,8]{0,1:T(8,128)S(1)} %fusion.79, f32[8,128,256]{2,1,0:T(8,128)} %fusion.51, f32[8,160,128]{2,1,0:T(8,128)} %bitcast.19, f32[8,160,256]{2,1,0:T(8,128)S(1)} %copy-done.3, f32[256]{0:T(256)S(1)} %get-tuple-element.58), kind=kOutput, calls=%fused_computation.67 | convolution fusion | flops 253229056 | bytes 4604928 | tf_op jit(solution)/shard_map/hft,hfv->thv/dot_general | solution.py:168
  87.0 0.6 fusion.20
  87.6 2.3 %fusion.22 = f32[8,160,128]{2,1,0:T(8,128)S(1)} fusion(f32[8,160,256]{2,1,0:T(8,128)} %get-tuple-element.51, f32[256]{0:T(256)S(1)} %get-tuple-element.56, f32[256,8,128]{0,2,1:T(8,128)} %bitcast.161, f32[256,8]{0,1:T(8,128)S(1)} %fusion.79), kind=kOutput, calls=%fused_computation.40 | convolution fusion | flops 252248064 | bytes 3023872 | tf_op jit(solution)/shard_map/hft,thv->hfv/dot_general | solution.py:181
  90.0 0.9 copy-done.11
  90.9 5.4 %all-to-all-start.2 = ((f32[32,40,128]{2,1,0:T(8,128)}), f32[32,40,128]{2,1,0:T(8,128)S(1)}, u32[]{:S(2)}, u32[]{:S(2)}) async-start(f32[32,40,128]{2,1,0:T(8,128)} %bitcast.165), calls=%async_computation.2 | async-start | bytes 1310720 | tf_op jit(solution)/shard_map/all_to_all | solution.py:102
  96.6 0.8 gather_fusion.3
  97.4 0.7 gather_fusion.2
  98.1 2.0 %copy.132 = bf16[256,1024]{1,0:T(8,128)(2,1)} copy(bf16[256,1024]{0,1:T(8,128)(2,1)} %bitcast.172) | data formatting | bytes 1048576
  100.2 14.9 %all-to-all-done.2 = f32[32,40,128]{2,1,0:T(8,128)S(1)} async-done(((f32[32,40,128]{2,1,0:T(8,128)}), f32[32,40,128]{2,1,0:T(8,128)S(1)}, u32[]{:S(2)}, u32[]{:S(2)}) %all-to-all-start.2) | async-done | bytes 655392 | tf_op jit(solution)/shard_map/all_to_all | solution.py:102
  115.1 0.4 fusion.42
  115.5 1.3 copy.127
  116.8 5.3 %all-to-all-start.3 = ((f32[32,40,128]{2,1,0:T(8,128)}), f32[32,40,128]{2,1,0:T(8,128)S(1)}, u32[]{:S(2)}, u32[]{:S(2)}) async-start(f32[32,40,128]{2,1,0:T(8,128)} %copy.127), calls=%async_computation.3 | async-start | bytes 1310720 | tf_op jit(solution)/shard_map/all_to_all | solution.py:104
  122.2 3.5 %fusion.9 = f32[8,160,256]{2,1,0:T(8,128)} fusion(f32[8,160,128]{2,1,0:T(8,128)} %bitcast.19, f32[8,256]{1,0:T(8,128)S(1)} %bitcast_divide_fusion, f32[8,160]{1,0:T(8,128)S(1)} %copy-done.24, f32[256]{0:T(256)S(1)} %copy-done.22, f32[160]{0:T(256)S(1)} %copy-done.33, f32[256,8,128]{0,2,1:T(8,128)} %bitcast.162, f32[256,8]{0,1:T(8,128)S(1)} %fusion.79), kind=kOutput, calls=%fused_computation.18 | convolution fusion | flops 253231104 | bytes 3037824 | tf_op jit(solution)/shard_map/hfv,thv->hft/dot_general | solution.py:197
  125.7 2.5 %fusion.49 = f32[8,128,256]{2,1,0:T(8,128)} fusion(f32[8,256,256]{1,2,0:T(8,128)S(1)} %copy-done.36, pred[256,256]{0,1:T(8,128)(4,1)S(1)} %fusion.62, f32[256,8,128]{0,2,1:T(8,128)S(1)} %bitcast.163, f32[256,8]{0,1:T(8,128)S(1)} %fusion.79), kind=kOutput, calls=%fused_computation.78 | convolution fusion | flops 406061056 | bytes 4268032 | tf_op jit(solution)/shard_map/hts,thv->shv/dot_general | solution.py:185
  128.2 2.4 %multiply_select_fusion = f32[8,256,256]{1,2,0:T(8,128)} fusion(f32[8,256,256]{1,2,0:T(8,128)S(1)} %copy-done.36, f32[8,256]{1,0:T(8,128)S(1)} %bitcast_divide_fusion, pred[256,256]{0,1:T(8,128)(4,1)S(1)} %fusion.62, bf16[32,8,8,128]{3,2,1,0:T(8,128)(2,1)S(1)} %copy-done.6, f32[256,8,128]{0,2,1:T(8,128)S(1)} %bitcast.164, f32[256,8]{0,1:T(8,128)S(1)} %fusion.79), kind=kOutput, calls=%fused_computation.12 | convolution fusion | flops 405536768 | bytes 5849088 | tf_op jit(solution)/shard_map/thv,shv->hts/dot_general | solution.py:190
  130.6 10.2 %all-to-all-done.3 = f32[32,40,128]{2,1,0:T(8,128)S(1)} async-done(((f32[32,40,128]{2,1,0:T(8,128)}), f32[32,40,128]{2,1,0:T(8,128)S(1)}, u32[]{:S(2)}, u32[]{:S(2)}) %all-to-all-start.3) | async-done | bytes 655392 | tf_op jit(solution)/shard_map/all_to_all | solution.py:104
  140.8 3.7 %fusion.12 = f32[8,128,256]{2,1,0:T(8,128)} fusion(f32[8,128,256]{2,1,0:T(8,128)} %fusion.49, f32[8,160,128]{2,1,0:T(8,128)S(1)} %bitcast.157, f32[8,160,256]{2,1,0:T(8,128)} %get-tuple-element.35, f32[256]{0:T(256)S(1)} %copy-done.23), kind=kOutput, calls=%fused_computation.23 | convolution fusion | flops 252182528 | bytes 4064256 | tf_op jit(solution)/shard_map/hfs,hfv->shv/dot_general | solution.py:186
  144.5 2.6 %copy.130 = f32[256,1024]{1,0:T(8,128)} copy(f32[256,1024]{0,1:T(8,128)} %bitcast.159) | data formatting | bytes 2097152 | tf_op jit(solution)/shard_map/reshape | solution.py:208
  147.1 3.7 %multiply_convert_fusion = (bf16[256,1024]{1,0:T(8,128)(2,1)}, f32[256,1024]{1,0:T(8,128)S(1)}) fusion(f32[256,1024]{1,0:T(8,128)} %copy.130, bf16[256,1024]{1,0:T(8,128)(2,1)} %param.23, f32[256]{0:T(256)S(1)} %copy-done.18, bf16[256,1024]{1,0:T(8,128)(2,1)} %param.22, bf16[2,1024]{1,0:T(2,128)(2,1)S(1)} %copy-done.16, f32[1024]{0:T(1024)S(1)} %bitcast.182, ...), kind=kLoop, calls=%fused_computation.66 | loop fusion | flops 6815744 | bytes 3688448 | tf_op jit(solution)/shard_map/convert_element_type | solution.py:209
  150.8 4.4 %collective-permute-start.1 = (f32[2,1024]{1,0:T(2,128)S(1)}, f32[2,1024]{1,0:T(2,128)S(1)}, u32[]{:S(2)}, u32[]{:S(2)}) collective-permute-start(f32[2,1024]{1,0:T(2,128)S(1)} %slice.124), channel_id=1, source_target_pairs={{8,0},{16,8},{24,16},{32,24},{40,32},{48,40},{56,48},{64,56},{72,6... | collective-permute-start | bytes 24584 | tf_op jit(solution)/shard_map/ppermute | solution.py:23
  155.3 2.3 %fusion.29 = (f32[8,160,256]{2,1,0:T(8,128)S(1)}, f32[8,160,256]{2,1,0:T(8,128)S(1)}, f32[8,160,256]{2,1,0:T(8,128)S(1)}, f32[8,160,256]{2,1,0:T(8,128)S(1)}) fusion(f32[8,160,256]{2,1,0:T(8,128)} %fusion.9, f32[2,8,160,256]{3,2,1,0:T(8,128)S(1)} %convolution_bitcast_fusion, f32[160]{0:T(256)S(1)} %copy-done.31, f32[160]{0:T(256)S(1)} %copy-done.29, ...), kind=kOutput, calls=%fused_computation.48 | convolution fusion | flops 255262720 | bytes 12984192 | tf_op jit(solution)/shard_map/hfv,shv->hfs/dot_general | solution.py:201
  157.6 0.7 fusion.4
  158.4 0.8 copy-done.4
  159.2 0.7 fusion.33
  159.9 0.7 fusion
  160.7 0.5 fusion.32
  161.1 0.7 copy.134
  161.9 0.7 copy.133
  162.6 3.3 %fusion.39 = bf16[256,1024]{1,0:T(8,128)(2,1)} fusion(f32[256,1024]{1,0:T(8,128)} %copy-done.8, f32[2,1024]{1,0:T(2,128)S(1)} %collective-permute-done.1, f32[256]{0:T(256)S(1)} %copy-done.27, f32[256]{0:T(256)S(1)} %copy-done.26, f32[1024]{0:T(1024)S(1)} %bitcast.183, f32[1024]{0:T(1024)S(1)} %bitcast.180, f32[1024]{0:T(1024)S(1)} %bitcast.177), kind=kLoop, calls=%fused_computation.62 | loop fusion | flops 2621440 | bytes 1595392 | tf_op jit(solution)/shard_map/convert_element_type | solution.py:220
  (112 shorter events, 1.3 us)
Async XLA Ops:
  1.4 17.0 %collective-permute-start = (bf16[2,1024]{1,0:T(2,128)(2,1)S(1)}, bf16[2,1024]{1,0:T(2,128)(2,1)S(1)}, u32[]{:S(2)}, u32[]{:S(2)}) collective-permute-start(bf16[2,1024]{1,0:T(2,128)(2,1)S(1)} %slice.80), channel_id=1, source_target_pairs={{0,8},{8,16},{16,24},{24,32},{32,40},{40,48},{48,56},{56,64},{64,7... | collective-permute-start | bytes 12296 | tf_op jit(solution)/shard_map/ppermute | solution.py:23
  11.7 1.3 copy-start.13
  13.1 3.3 %copy-start.28 = (f32[160]{0:T(256)S(1)}, f32[160]{0:T(256)}, u32[]{:S(2)}) copy-start(f32[160]{0:T(256)} %constant.78.clone) | copy-start | bytes 1924
  13.1 3.3 %copy-start.30 = (f32[160]{0:T(256)S(1)}, f32[160]{0:T(256)}, u32[]{:S(2)}) copy-start(f32[160]{0:T(256)} %constant.79.clone) | copy-start | bytes 1924
  13.1 3.3 %copy-start.32 = (f32[160]{0:T(256)S(1)}, f32[160]{0:T(256)}, u32[]{:S(2)}) copy-start(f32[160]{0:T(256)} %constant.80.clone) | copy-start | bytes 1924
  13.6 4.7 %copy-start = (f32[2,8,160,256]{3,2,1,0:T(8,128)}, f32[2,8,160,256]{3,2,1,0:T(8,128)S(1)}, u32[]{:S(2)}) copy-start(f32[2,8,160,256]{3,2,1,0:T(8,128)S(1)} %convolution_bitcast_fusion.1) | copy-start | bytes 7864324
  16.4 2.0 %copy-start.17 = (f32[256]{0:T(256)}, f32[256]{0:T(256)S(1)}, u32[]{:S(2)}) copy-start(f32[256]{0:T(256)S(1)} %get-tuple-element.59) | copy-start | bytes 3076
  16.4 2.0 %copy-start.19 = (f32[256]{0:T(256)}, f32[256]{0:T(256)S(1)}, u32[]{:S(2)}) copy-start(f32[256]{0:T(256)S(1)} %get-tuple-element.60) | copy-start | bytes 3076
  16.4 66.9 %copy-start.21 = (f32[256]{0:T(256)}, f32[256]{0:T(256)S(1)}, u32[]{:S(2)}) copy-start(f32[256]{0:T(256)S(1)} %get-tuple-element.58) | copy-start | bytes 3076
  16.4 1.9 %copy-start.14 = (bf16[3,1024]{1,0:T(4,128)(2,1)S(1)}, bf16[3,1024]{1,0:T(4,128)(2,1)}, u32[]{:S(2)}) copy-start(bf16[3,1024]{1,0:T(4,128)(2,1)} %param.24) | copy-start | bytes 18436
  18.4 2.5 %copy-start.2 = (f32[8,160,256]{2,1,0:T(8,128)S(1)}, f32[8,160,256]{2,1,0:T(8,128)}, u32[]{:S(2)}) copy-start(f32[8,160,256]{2,1,0:T(8,128)} %get-tuple-element.35) | copy-start | bytes 3932164
  18.4 3.0 %copy-start.15 = (bf16[2,1024]{1,0:T(2,128)(2,1)}, bf16[2,1024]{1,0:T(2,128)(2,1)S(1)}, u32[]{:S(2)}) copy-start(bf16[2,1024]{1,0:T(2,128)(2,1)S(1)} %collective-permute-done) | copy-start | bytes 12292
  20.8 43.5 %copy-start.5 = (bf16[32,8,8,128]{3,2,1,0:T(8,128)(2,1)}, bf16[32,8,8,128]{3,2,1,0:T(8,128)(2,1)S(1)}, u32[]{:S(2)}) copy-start(bf16[32,8,8,128]{3,2,1,0:T(8,128)(2,1)S(1)} %fusion.53) | copy-start | bytes 1572868
  21.4 0.8 copy-start.9
  22.3 30.7 %all-to-all-start = ((f32[32,40,128]{2,1,0:T(8,128)}), f32[32,40,128]{2,1,0:T(8,128)}, u32[]{:S(2)}, u32[]{:S(2)}) async-start(f32[32,40,128]{2,1,0:T(8,128)} %bitcast.160), calls=%async_computation | async-start | bytes 1310720 | tf_op jit(solution)/shard_map/all_to_all | solution.py:102
  34.5 21.2 %copy-start.25 = (s32[1024]{0:T(1024)}, s32[1024]{0:T(1024)S(1)}, u32[]{:S(2)}) copy-start(s32[1024]{0:T(1024)S(1)} %pad_clamp_fusion.1) | copy-start | bytes 12292
  55.7 24.4 %all-to-all-start.1 = ((f32[32,40,128]{2,1,0:T(8,128)}), f32[32,40,128]{2,1,0:T(8,128)}, u32[]{:S(2)}, u32[]{:S(2)}) async-start(f32[32,40,128]{2,1,0:T(8,128)} %copy.116), calls=%async_computation.1 | async-start | bytes 1310720 | tf_op jit(solution)/shard_map/all_to_all | solution.py:104
  64.3 1.3 copy-start.35
  80.0 3.2 %copy-start.3 = (f32[8,160,256]{2,1,0:T(8,128)S(1)}, f32[8,160,256]{2,1,0:T(8,128)}, u32[]{:S(2)}) copy-start(f32[8,160,256]{2,1,0:T(8,128)} %get-tuple-element.51) | copy-start | bytes 3932164
  90.0 6.3 %copy-start.34 = (s32[32,1]{0,1:T(1,128)S(1)}, s32[32,1]{0,1:T(1,128)}, u32[]{:S(2)}) copy-start(s32[32,1]{0,1:T(1,128)} %get-tuple-element.72) | copy-start | bytes 388
  90.0 0.9 copy-start.11
  90.9 24.2 %all-to-all-start.2 = ((f32[32,40,128]{2,1,0:T(8,128)}), f32[32,40,128]{2,1,0:T(8,128)S(1)}, u32[]{:S(2)}, u32[]{:S(2)}) async-start(f32[32,40,128]{2,1,0:T(8,128)} %bitcast.165), calls=%async_computation.2 | async-start | bytes 1310720 | tf_op jit(solution)/shard_map/all_to_all | solution.py:102
  115.5 6.7 %copy-start.22 = (f32[256]{0:T(256)S(1)}, f32[256]{0:T(256)}, u32[]{:S(2)}) copy-start(f32[256]{0:T(256)} %copy-done.21) | copy-start | bytes 3076
  115.5 6.7 %copy-start.24 = (f32[8,160]{1,0:T(8,128)S(1)}, f32[8,160]{1,0:T(8,128)}, u32[]{:S(2)}) copy-start(f32[8,160]{1,0:T(8,128)} %get-tuple-element.44) | copy-start | bytes 15364
  115.5 6.7 %copy-start.33 = (f32[160]{0:T(256)S(1)}, f32[160]{0:T(256)}, u32[]{:S(2)}) copy-start(f32[160]{0:T(256)} %constant.80.clone) | copy-start | bytes 1924
  116.8 24.0 %all-to-all-start.3 = ((f32[32,40,128]{2,1,0:T(8,128)}), f32[32,40,128]{2,1,0:T(8,128)S(1)}, u32[]{:S(2)}, u32[]{:S(2)}) async-start(f32[32,40,128]{2,1,0:T(8,128)} %copy.127), calls=%async_computation.3 | async-start | bytes 1310720 | tf_op jit(solution)/shard_map/all_to_all | solution.py:104
  122.2 3.5 %copy-start.10 = (f32[256,1024]{0,1:T(8,128)S(1)}, f32[256,1024]{0,1:T(8,128)}, u32[]{:S(2)}) copy-start(f32[256,1024]{0,1:T(8,128)} %copy.117) | copy-start | bytes 3145732
  122.2 3.5 %copy-start.36 = (f32[8,256,256]{1,2,0:T(8,128)S(1)}, f32[8,256,256]{1,2,0:T(8,128)}, u32[]{:S(2)}) copy-start(f32[8,256,256]{1,2,0:T(8,128)} %copy-done.35) | copy-start | bytes 6291460
  125.7 2.5 %copy-start.6 = (bf16[32,8,8,128]{3,2,1,0:T(8,128)(2,1)S(1)}, bf16[32,8,8,128]{3,2,1,0:T(8,128)(2,1)}, u32[]{:S(2)}) copy-start(bf16[32,8,8,128]{3,2,1,0:T(8,128)(2,1)} %copy-done.5) | copy-start | bytes 1572868
  128.2 12.6 %copy-start.23 = (f32[256]{0:T(256)S(1)}, f32[256]{0:T(256)}, u32[]{:S(2)}) copy-start(f32[256]{0:T(256)} %get-tuple-element.32) | copy-start | bytes 3076
  144.5 2.6 %copy-start.16 = (bf16[2,1024]{1,0:T(2,128)(2,1)S(1)}, bf16[2,1024]{1,0:T(2,128)(2,1)}, u32[]{:S(2)}) copy-start(bf16[2,1024]{1,0:T(2,128)(2,1)} %copy-done.15) | copy-start | bytes 12292
  144.5 2.6 %copy-start.18 = (f32[256]{0:T(256)S(1)}, f32[256]{0:T(256)}, u32[]{:S(2)}) copy-start(f32[256]{0:T(256)} %copy-done.17) | copy-start | bytes 3076
  144.5 2.6 %copy-start.20 = (f32[256]{0:T(256)S(1)}, f32[256]{0:T(256)}, u32[]{:S(2)}) copy-start(f32[256]{0:T(256)} %copy-done.19) | copy-start | bytes 3076
  147.1 8.2 %copy-start.1 = (f32[2,8,160,256]{3,2,1,0:T(8,128)S(1)}, f32[2,8,160,256]{3,2,1,0:T(8,128)}, u32[]{:S(2)}) copy-start(f32[2,8,160,256]{3,2,1,0:T(8,128)} %copy-done) | copy-start | bytes 7864324
  147.1 8.2 %copy-start.7 = (bf16[32,8,8,128]{3,2,1,0:T(8,128)(2,1)S(1)}, bf16[32,8,8,128]{3,2,1,0:T(8,128)(2,1)}, u32[]{:S(2)}) copy-start(bf16[32,8,8,128]{3,2,1,0:T(8,128)(2,1)} %copy-done.5) | copy-start | bytes 1572868
  147.1 8.2 %copy-start.29 = (f32[160]{0:T(256)S(1)}, f32[160]{0:T(256)}, u32[]{:S(2)}) copy-start(f32[160]{0:T(256)} %constant.78.clone) | copy-start | bytes 1924
  147.1 8.2 %copy-start.31 = (f32[160]{0:T(256)S(1)}, f32[160]{0:T(256)}, u32[]{:S(2)}) copy-start(f32[160]{0:T(256)} %constant.79.clone) | copy-start | bytes 1924
  150.8 4.4 %copy-start.8 = (f32[256,1024]{1,0:T(8,128)}, f32[256,1024]{1,0:T(8,128)S(1)}, u32[]{:S(2)}) copy-start(f32[256,1024]{1,0:T(8,128)S(1)} %get-tuple-element.41) | copy-start | bytes 3145732
  150.8 11.8 %collective-permute-start.1 = (f32[2,1024]{1,0:T(2,128)S(1)}, f32[2,1024]{1,0:T(2,128)S(1)}, u32[]{:S(2)}, u32[]{:S(2)}) collective-permute-start(f32[2,1024]{1,0:T(2,128)S(1)} %slice.124), channel_id=1, source_target_pairs={{8,0},{16,8},{24,16},{32,24},{40,32},{48,40},{56,48},{64,56},{72,6... | collective-permute-start | bytes 24584 | tf_op jit(solution)/shard_map/ppermute | solution.py:23
  155.3 2.3 %copy-start.12 = (f32[320,16,1]{0,1,2:T(8,128)S(1)}, f32[320,16,1]{0,1,2:T(8,128)}, u32[]{:S(2)}) copy-start(f32[320,16,1]{0,1,2:T(8,128)} %constant.87) | copy-start | bytes 61444
  157.6 1.6 copy-start.4
  160.6 2.0 %copy-start.26 = (f32[256]{0:T(256)S(1)}, f32[256]{0:T(256)}, u32[]{:S(2)}) copy-start(f32[256]{0:T(256)} %get-tuple-element.49) | copy-start | bytes 3076
  160.6 2.0 %copy-start.27 = (f32[256]{0:T(256)S(1)}, f32[256]{0:T(256)}, u32[]{:S(2)}) copy-start(f32[256]{0:T(256)} %get-tuple-element.50) | copy-start | bytes 3076

commit v4 on v3

--- a/solution.py
+++ b/solution.py
@@ -90,7 +90,7 @@
     return forward.astype(jnp.float32), backward.astype(jnp.float32)
 
 
-def state_scan(local_state, local_norm, mask):
+def state_scan(local_state, local_norm, mask, filler):
     devices = mask.shape[0]
     heads, feats, width = local_state.shape
     norm_rows = -(-feats // width)
@@ -100,10 +100,11 @@
         local_state, norm_block.reshape(heads, norm_rows, width), (0, room, 0)
     ).reshape(devices, -1, width)
     chunks = lax.all_to_all(packed, "ctx", 0, 0, tiled=True)
+    chunks, filler = lax.optimization_barrier((chunks, filler))
     summed = jnp.einsum("ij,jrc->irc", mask, chunks, precision=high)
     back = lax.all_to_all(summed, "ctx", 0, 0, tiled=True).reshape(heads, feats, width)
     norm_in = back[:, room:].reshape(heads, norm_rows * width)[:, :feats]
-    return (back, norm_in)
+    return (back, norm_in, filler)
 
 
 def local(query, key, value_in, gate, conv_weight, doc_lengths, d_out):
@@ -163,7 +164,9 @@
     local_norm = jnp.sum(masked_key, axis=2)
     restart_all, closes_all = block_flags(doc_lengths, lax.axis_size("ctx"), tok_rows)
     forward_mask, backward_mask = scan_masks(restart_all, closes_all)
-    state_in, norm_in = state_scan(local_state, local_norm, forward_mask)
+    state_in, norm_in, (numerator, denominator) = state_scan(
+        local_state, local_norm, forward_mask, (numerator, denominator)
+    )
     inside = (doc_ids == prev_doc).astype(jnp.float32)
     numerator = numerator + inside[:, None, None] * jnp.einsum(
         "hft,hfv->thv", phi_query, state_in, precision=high
@@ -180,12 +183,8 @@
     masked_query = phi_query * first_mask[None, None, :]
     back_state = jnp.einsum("hft,thv->hfv", masked_query, grad_num, precision=high)
     back_norm = jnp.einsum("hft,th->hf", masked_query, grad_den, precision=high)
-    grad_state_in, grad_norm_in = state_scan(back_state, back_norm, backward_mask)
     outside = (doc_ids == next_doc).astype(jnp.float32)
     grad_v = jnp.einsum("hts,thv->shv", weights, grad_num, precision=high)
-    grad_v = grad_v + outside[:, None, None] * jnp.einsum(
-        "hfs,hfv->shv", phi_key, grad_state_in, precision=high
-    )
     grad_weights = (
         jnp.einsum("thv,shv->hts", grad_num, v_float, precision=high)
         + jnp.transpose(grad_den, (1, 0))[:, :, None]
@@ -197,11 +196,17 @@
         jnp.einsum("hfv,thv->hft", state_in, grad_num, precision=high)
         + norm_in[:, :, None] * jnp.transpose(grad_den, (1, 0))[:, None, :]
     )
+    grad_q = grad_q + feature_grad(grad_phi_query, spread_query)
+    grad_state_in, grad_norm_in, (grad_v, grad_q, grad_k) = state_scan(
+        back_state, back_norm, backward_mask, (grad_v, grad_q, grad_k)
+    )
+    grad_v = grad_v + outside[:, None, None] * jnp.einsum(
+        "hfs,hfv->shv", phi_key, grad_state_in, precision=high
+    )
     grad_phi_key = outside[None, None, :] * (
         jnp.einsum("hfv,shv->hfs", grad_state_in, v_float, precision=high)
         + grad_norm_in[:, :, None]
     )
-    grad_q = grad_q + feature_grad(grad_phi_query, spread_query)
     grad_k = grad_k + feature_grad(grad_phi_key, spread_key)
     grad_query = grad_q.reshape(tok_rows, HEADS * KD).astype(jnp.bfloat16)
     grad_key = grad_k.reshape(tok_rows, HEADS * KD).astype(jnp.bfloat16)

time: 167 us -> 161 us (0.964)
  other arithmetic: 18.4 us -> 13.2 us
  waiting for transfers between devices: 54.4 us -> 52.2 us
    all_to_all x2, waiting for transfers between devices: 31.9 us -> 22.4 us  [state_scan(): chunks = lax.all_to_all(packed, 'ctx', 0, 0, tiled=True)]
    all_to_all x2, waiting for transfers between devices: 22.4 us -> 29.8 us  [state_scan(): lax.all_to_all(summed, 'ctx', 0, 0, tiled=True).reshape(heads, feats, width)]
    convert_element_type x1, other arithmetic: 3.72 us -> 1.66 us  [local(): (grad_core * convolved * opening * (1.0 - opening)).astype(jnp.bfloat16)]
    convert_element_type x1, other arithmetic: 3.28 us -> 1.23 us  [local(): grad_value.astype(jnp.bfloat16)]
    unnamed x83 -> x53, local copies, waits for them, and re-layouts: 10.3 us -> 9.89 us
  transfers between devices with their start and end apart: 6 -> 6, of which waited for: 4 -> 4; matrix products, arithmetic and copies ran while one was open for 24% -> 23% of each run, Pallas kernels for 0% -> 0%
where the time goes in v4:
time: 161 us; the launch traced here: 158 us
  waiting for transfers between devices  52.2 us (32%)
  starting transfers between devices  35.2 us (22%)
  matrix products  31.2 us (19%)
  local copies, waits for them, and re-layouts  25.3 us (16%)
  other arithmetic  13.2 us (8%)
    all_to_all x2, waiting for transfers between devices, state_scan(): lax.all_to_all(summed, 'ctx', 0, 0, tiled=True).reshape(heads, feats, width)  29.8 us
    all_to_all x2, waiting for transfers between devices, state_scan(): chunks = lax.all_to_all(packed, 'ctx', 0, 0, tiled=True)  22.4 us
    all_to_all x2, starting transfers between devices, state_scan(): chunks = lax.all_to_all(packed, 'ctx', 0, 0, tiled=True)  16.6 us
    all_to_all x2, starting transfers between devices, state_scan(): lax.all_to_all(summed, 'ctx', 0, 0, tiled=True).reshape(heads, feats, width)  10.8 us
    unnamed x53, local copies, waits for them, and re-layouts  9.89 us
    ppermute x2, starting transfers between devices, shifted(): return lax.ppermute(block, axis, route)  7.86 us
    dot_general x1, matrix products, local(): jnp.einsum('hft,hfv->thv', phi_query, state_in, precision=high)  3.69 us
    dot_general x1, matrix products, local(): jnp.einsum('hfs,hfv->shv', phi_key, grad_state_in, precision=high)  3.68 us
  transfers between devices with their start and end apart: 6, of which 4 were waited for; matrix products, arithmetic and copies ran while one was open for 23% of the time, Pallas kernels for 0%

profile of v4, /device:TPU:32, one launch (start us, length us, event | category | flops | bytes accessed | tf_op | source)
XLA Modules:
  0.0 158.4 jit_solution(10866844196502103457)
XLA Ops:
  0.6 0.7 slice.83
  1.4 3.5 %collective-permute-start = (bf16[2,1024]{1,0:T(2,128)(2,1)S(1)}, bf16[2,1024]{1,0:T(2,128)(2,1)S(1)}, u32[]{:S(2)}, u32[]{:S(2)}) collective-permute-start(bf16[2,1024]{1,0:T(2,128)(2,1)S(1)} %slice.83), channel_id=1, source_target_pairs={{0,8},{8,16},{16,24},{24,32},{32,40},{40,48},{48,56},{56,64},{64,7... | collective-permute-start | bytes 12296 | tf_op jit(solution)/shard_map/ppermute | solution.py:23
  4.9 0.7 broadcast_add_fusion.3
  5.6 0.8 fusion.104
  6.4 0.7 copy.109
  7.6 0.7 compare_select_fusion
  8.3 0.6 fusion.106
  8.9 0.6 compare_convert_fusion.4
  9.5 0.6 fusion.105
  10.1 0.9 copy.111
  11.1 0.9 copy.108
  12.0 1.3 convolution_bitcast_fusion.1
  13.4 0.5 convolution_bitcast_fusion
  14.0 2.7 %compare_convert_fusion.1 = (f32[256]{0:T(256)S(1)}, f32[256]{0:T(256)}, f32[256]{0:T(256)S(1)}, f32[256]{0:T(256)S(1)}, f32[256]{0:T(256)S(1)}, /*index=5*/f32[256]{0:T(256)S(1)}, f32[256]{0:T(256)S(1)}) fusion(s32[256]{0:T(256)S(1)} %get-tuple-element.47, s32[258]{0:T(512)S(1)} %get-tuple-element.75, s32[]{:T(128)} %bitcast.32, s32[]{:T(128)} %bitcast.16, ...), kind=kLoop, calls=%fused_computation.136 | loop fusion | flops 3584 | bytes 12300 | tf_op jit(solution)/shard_map/convert_element_type | solution.py:221
  16.6 1.9 %multiply_reduce_fusion = (f32[8,160]{1,0:T(8,128)S(1)}, f32[8,160,256]{2,1,0:T(8,128)}, f32[8,160,256]{2,1,0:T(8,128)}) fusion(f32[256]{0:T(256)S(1)} %get-tuple-element.74, f32[160]{0:T(256)S(1)} %copy-done.15, f32[2,8,160,256]{3,2,1,0:T(8,128)S(1)} %convolution_bitcast_fusion.1, f32[160]{0:T(256)S(1)} %copy-done.16, f32[160]{0:T(256)S(1)} %copy-done.14, ...), kind=kLoop, calls=%fused_computation.45 | loop fusion | flops 3275520 | bytes 7872384 | tf_op jit(solution)/shard_map/reduce_sum | solution.py:164
  18.5 0.2 convert_reduce_fusion.2
  18.8 2.5 %fusion.60 = bf16[32,8,8,128]{3,2,1,0:T(8,128)(2,1)S(1)} fusion(bf16[256,1024]{1,0:T(8,128)(2,1)} %param.23, f32[256]{0:T(256)S(1)} %get-tuple-element.72, bf16[256,1024]{1,0:T(8,128)(2,1)} %param.22, bf16[2,1024]{1,0:T(2,128)(2,1)S(1)} %collective-permute-done, f32[1024]{0:T(1024)S(1)} %bitcast.192, f32[256]{0:T(256)S(1)} %get-tuple-element.73, ...), kind=kLoop, calls=%fused_computation.87 | loop fusion | flops 5767168 | bytes 1591296
  21.3 0.5 fusion.25
  21.9 0.8 copy-done.5
  22.7 11.1 %all-to-all-start = ((f32[32,40,128]{2,1,0:T(8,128)}), f32[32,40,128]{2,1,0:T(8,128)}, u32[]{:S(2)}, u32[]{:S(2)}) async-start(f32[32,40,128]{2,1,0:T(8,128)} %bitcast.171), calls=%async_computation | async-start | bytes 1310720 | tf_op jit(solution)/shard_map/all_to_all | solution.py:102
  34.1 0.7 gather_fusion.1
  34.8 0.7 gather_fusion
  35.7 0.8 fusion.58
  36.5 1.3 copy-done.20
  37.8 2.1 %convolution_bitcast_fusion.2 = f32[256,8,128]{0,2,1:T(8,128)} fusion(f32[8,256,256]{1,2,0:T(8,128)S(1)} %get-tuple-element.82, pred[256,256]{0,1:T(8,128)(4,1)S(1)} %fusion.69, bf16[32,8,8,128]{3,2,1,0:T(8,128)(2,1)S(1)} %fusion.60), kind=kOutput, calls=%fused_computation.22 | convolution fusion | flops 405798912 | bytes 3735552 | tf_op jit(solution)/shard_map/hts,shv->thv/dot_general | solution.py:157
  39.9 13.5 %all-to-all-done = f32[32,40,128]{2,1,0:T(8,128)} async-done(((f32[32,40,128]{2,1,0:T(8,128)}), f32[32,40,128]{2,1,0:T(8,128)}, u32[]{:S(2)}, u32[]{:S(2)}) %all-to-all-start) | async-done | bytes 655392 | tf_op jit(solution)/shard_map/all_to_all | solution.py:102
  53.4 1.5 fusion.53
  54.8 1.2 copy.116
  56.1 5.5 %all-to-all-start.1 = ((f32[32,40,128]{2,1,0:T(8,128)}), f32[32,40,128]{2,1,0:T(8,128)}, u32[]{:S(2)}, u32[]{:S(2)}) async-start(f32[32,40,128]{2,1,0:T(8,128)} %copy.116), calls=%async_computation.1 | async-start | bytes 1310720 | tf_op jit(solution)/shard_map/all_to_all | solution.py:105
  61.8 1.2 gather_fusion.3
  63.0 1.2 gather_fusion.2
  64.2 2.2 %copy.117 = f32[256,1024]{0,1:T(8,128)} copy(bf16[256,1024]{1,0:T(8,128)(2,1)} %param.26) | data formatting | bytes 1572864 | tf_op jit(solution)/shard_map/reshape | solution.py:179
  66.5 14.0 %all-to-all-done.1 = f32[32,40,128]{2,1,0:T(8,128)} async-done(((f32[32,40,128]{2,1,0:T(8,128)}), f32[32,40,128]{2,1,0:T(8,128)}, u32[]{:S(2)}, u32[]{:S(2)}) %all-to-all-start.1) | async-done | bytes 655392 | tf_op jit(solution)/shard_map/all_to_all | solution.py:105
  80.4 0.9 slice_bitcast_fusion.5
  81.3 1.7 %fusion.77 = f32[8,1,256]{2,1,0:T(1,128)S(1)} fusion(f32[8,160,256]{2,1,0:T(8,128)} %get-tuple-element.67, f32[8,160,1]{1,0,2:T(8,128)S(1)} %get-tuple-element.61), kind=kOutput, calls=%fused_computation.121 | convolution fusion | flops 1966080 | bytes 1324032 | tf_op jit(solution)/shard_map/hft,hf->th/dot_general | solution.py:174
  83.1 3.7 %multiply_reduce_fusion.1 = (f32[256,8]{0,1:T(8,128)S(1)}, bf16[256,8,128]{0,2,1:T(8,128)(2,1)}) fusion(f32[256,1024]{0,1:T(8,128)} %copy.117, f32[256,8]{0,1:T(8,128)S(1)} %bitcast_add_fusion, f32[256,8,128]{0,2,1:T(8,128)} %convolution_bitcast_fusion.2, f32[8,160,128]{2,1,0:T(8,128)} %bitcast.21, f32[8,160,256]{2,1,0:T(8,128)S(1)} %copy-done.1, ...), kind=kOutput, calls=%fused_computation.72 | convolution fusion | flops 253229056 | bytes 4604928 | tf_op jit(solution)/shard_map/hft,hfv->thv/dot_general | solution.py:171
  86.8 0.6 fusion.21
  87.4 0.6 copy-done.8
  88.0 1.6 %fusion.23 = f32[8,160,128]{2,1,0:T(8,128)} fusion(f32[8,160,256]{2,1,0:T(8,128)S(1)} %copy-done.1, f32[256]{0:T(256)S(1)} %get-tuple-element.70, f32[256,8,128]{0,2,1:T(8,128)S(1)} %bitcast.173, f32[256,8]{0,1:T(8,128)S(1)} %bitcast_add_fusion), kind=kOutput, calls=%fused_computation.43 | convolution fusion | flops 252248064 | bytes 3023872 | tf_op jit(solution)/shard_map/hft,thv->hfv/dot_general | solution.py:184
  89.6 0.6 constant_dynamic-update-slice_fusion
  90.2 5.5 %all-to-all-start.2 = ((f32[32,40,128]{2,1,0:T(8,128)}), f32[32,40,128]{2,1,0:T(8,128)}, u32[]{:S(2)}, u32[]{:S(2)}) async-start(f32[32,40,128]{2,1,0:T(8,128)} %bitcast.176), calls=%async_computation.2 | async-start | bytes 1310720 | tf_op jit(solution)/shard_map/all_to_all | solution.py:102
  95.7 3.4 %fusion.30 = (f32[8,160,256]{2,1,0:T(8,128)S(1)}, f32[8,160,256]{2,1,0:T(8,128)S(1)}) fusion(f32[2,8,160,256]{3,2,1,0:T(8,128)} %copy-done.2, f32[160]{0:T(256)S(1)} %copy-done.15, f32[160]{0:T(256)S(1)} %copy-done.16, f32[160]{0:T(256)S(1)} %copy-done.14, f32[8,256]{1,0:T(8,128)S(1)} %get-tuple-element.58, f32[8,160]{1,0:T(8,128)S(1)} %get-tuple-element.60, ...), kind=kOutput, calls=%fused_computation.51 | convolution fusion | flops 254541824 | bytes 6971264 | tf_op jit(solution)/shard_map/hfv,thv->hft/dot_general | solution.py:196
  99.2 0.7 fusion
  99.9 0.4 copy-done.9
  100.4 1.1 multiply_select_fusion
  101.5 0.7 fusion.34
  102.2 0.5 fusion.36
  102.7 0.4 copy-done.13
  103.0 2.5 %convolution_bitcast_fusion.3 = f32[256,8,128]{0,2,1:T(8,128)} fusion(f32[8,256,256]{1,2,0:T(8,128)S(1)} %copy-done.21, pred[256,256]{0,1:T(8,128)(4,1)S(1)} %copy-done.13, f32[256,8,128]{0,2,1:T(8,128)S(1)} %bitcast.175, f32[256,8]{0,1:T(8,128)S(1)} %bitcast_add_fusion), kind=kOutput, calls=%fused_computation.26 | convolution fusion | flops 406061056 | bytes 4268032 | tf_op jit(solution)/shard_map/hts,thv->shv/dot_general | solution.py:187
  105.5 9.0 %all-to-all-done.2 = f32[32,40,128]{2,1,0:T(8,128)} async-done(((f32[32,40,128]{2,1,0:T(8,128)}), f32[32,40,128]{2,1,0:T(8,128)}, u32[]{:S(2)}, u32[]{:S(2)}) %all-to-all-start.2) | async-done | bytes 655392 | tf_op jit(solution)/shard_map/all_to_all | solution.py:102
  114.5 1.5 fusion.51
  115.9 1.2 copy.128
  117.2 5.3 %all-to-all-start.3 = ((f32[32,40,128]{2,1,0:T(8,128)}), f32[32,40,128]{2,1,0:T(8,128)S(1)}, u32[]{:S(2)}, u32[]{:S(2)}) async-start(f32[32,40,128]{2,1,0:T(8,128)} %copy.128), calls=%async_computation.3 | async-start | bytes 1310720 | tf_op jit(solution)/shard_map/all_to_all | solution.py:105
  122.5 2.0 %copy.132 = bf16[256,1024]{1,0:T(8,128)(2,1)} copy(bf16[256,1024]{0,1:T(8,128)(2,1)} %bitcast.183) | data formatting | bytes 1048576
  124.6 0.7 copy.133
  125.3 15.8 %all-to-all-done.3 = f32[32,40,128]{2,1,0:T(8,128)S(1)} async-done(((f32[32,40,128]{2,1,0:T(8,128)}), f32[32,40,128]{2,1,0:T(8,128)S(1)}, u32[]{:S(2)}, u32[]{:S(2)}) %all-to-all-start.3) | async-done | bytes 655392 | tf_op jit(solution)/shard_map/all_to_all | solution.py:105
  141.2 3.7 %fusion.13 = f32[256,8,128]{0,2,1:T(8,128)} fusion(f32[256,8,128]{0,2,1:T(8,128)} %convolution_bitcast_fusion.3, f32[8,160,128]{2,1,0:T(8,128)S(1)} %bitcast.168, f32[8,160,256]{2,1,0:T(8,128)} %get-tuple-element.49, f32[256]{0:T(256)S(1)} %get-tuple-element.46), kind=kOutput, calls=%fused_computation.25 | convolution fusion | flops 252182528 | bytes 4064256 | tf_op jit(solution)/shard_map/hfs,hfv->shv/dot_general | solution.py:203
  144.8 2.6 %copy.130 = f32[256,1024]{1,0:T(8,128)} copy(f32[256,1024]{0,1:T(8,128)} %bitcast.170) | data formatting | bytes 2097152 | tf_op jit(solution)/shard_map/reshape | solution.py:213
  147.5 2.1 %fusion.28 = (f32[8,160,256]{2,1,0:T(8,128)S(1)}, f32[8,160,256]{2,1,0:T(8,128)S(1)}) fusion(f32[2,8,160,256]{3,2,1,0:T(8,128)S(1)} %convolution_bitcast_fusion.1, f32[160]{0:T(256)S(1)} %copy-done.15, f32[160]{0:T(256)S(1)} %copy-done.16, f32[160]{0:T(256)S(1)} %copy-done.14, f32[8,160]{1,0:T(8,128)S(1)} %bitcast.195, f32[8,160,128]{2,1,0:T(8,128)S(1)} %bitcast.169, ...), kind=kOutput, calls=%fused_computation.49 | convolution fusion | flops 253952000 | bytes 6430592 | tf_op jit(solution)/shard_map/hfv,shv->hfs/dot_general | solution.py:207
  149.6 1.7 %multiply_convert_fusion = (bf16[256,1024]{1,0:T(8,128)(2,1)}, f32[256,1024]{1,0:T(8,128)S(1)}) fusion(f32[256,1024]{1,0:T(8,128)S(1)} %copy-done.4, bf16[256,1024]{1,0:T(8,128)(2,1)S(1)} %copy-done.7, f32[256]{0:T(256)S(1)} %get-tuple-element.72, bf16[256,1024]{1,0:T(8,128)(2,1)S(1)} %copy-done.6, bf16[2,1024]{1,0:T(2,128)(2,1)S(1)} %collective-permute-done, ...), kind=kLoop, calls=%fused_computation.71 | loop fusion | flops 6815744 | bytes 3688448 | tf_op jit(solution)/shard_map/convert_element_type | solution.py:214
  151.2 4.4 %collective-permute-start.1 = (f32[2,1024]{1,0:T(2,128)S(1)}, f32[2,1024]{1,0:T(2,128)S(1)}, u32[]{:S(2)}, u32[]{:S(2)}) collective-permute-start(f32[2,1024]{1,0:T(2,128)S(1)} %slice.124), channel_id=1, source_target_pairs={{8,0},{16,8},{24,16},{32,24},{40,32},{48,40},{56,48},{64,56},{72,6... | collective-permute-start | bytes 24584 | tf_op jit(solution)/shard_map/ppermute | solution.py:23
  155.6 0.7 fusion.40
  156.4 0.7 copy.134
  157.1 1.2 fusion.48
  (81 shorter events, 1.5 us)
Async XLA Ops:
  1.4 17.4 %collective-permute-start = (bf16[2,1024]{1,0:T(2,128)(2,1)S(1)}, bf16[2,1024]{1,0:T(2,128)(2,1)S(1)}, u32[]{:S(2)}, u32[]{:S(2)}) collective-permute-start(bf16[2,1024]{1,0:T(2,128)(2,1)S(1)} %slice.83), channel_id=1, source_target_pairs={{0,8},{8,16},{16,24},{24,32},{32,40},{40,48},{48,56},{56,64},{64,7... | collective-permute-start | bytes 12296 | tf_op jit(solution)/shard_map/ppermute | solution.py:23
  12.0 1.3 copy-start.11
  13.3 3.3 %copy-start.14 = (f32[160]{0:T(256)S(1)}, f32[160]{0:T(256)}, u32[]{:S(2)}) copy-start(f32[160]{0:T(256)} %constant.80.clone) | copy-start | bytes 1924
  13.3 3.3 %copy-start.15 = (f32[160]{0:T(256)S(1)}, f32[160]{0:T(256)}, u32[]{:S(2)}) copy-start(f32[160]{0:T(256)} %constant.79.clone) | copy-start | bytes 1924
  13.4 3.3 %copy-start.16 = (f32[160]{0:T(256)S(1)}, f32[160]{0:T(256)}, u32[]{:S(2)}) copy-start(f32[160]{0:T(256)} %constant.78.clone) | copy-start | bytes 1924
  13.9 4.6 %copy-start.2 = (f32[2,8,160,256]{3,2,1,0:T(8,128)}, f32[2,8,160,256]{3,2,1,0:T(8,128)S(1)}, u32[]{:S(2)}) copy-start(f32[2,8,160,256]{3,2,1,0:T(8,128)S(1)} %convolution_bitcast_fusion) | copy-start | bytes 7864324
  18.8 2.5 %copy-start = (f32[8,160,256]{2,1,0:T(8,128)S(1)}, f32[8,160,256]{2,1,0:T(8,128)}, u32[]{:S(2)}) copy-start(f32[8,160,256]{2,1,0:T(8,128)} %get-tuple-element.49) | copy-start | bytes 3932164
  21.3 78.6 %copy-start.3 = (bf16[32,8,8,128]{3,2,1,0:T(8,128)(2,1)}, bf16[32,8,8,128]{3,2,1,0:T(8,128)(2,1)S(1)}, u32[]{:S(2)}) copy-start(bf16[32,8,8,128]{3,2,1,0:T(8,128)(2,1)S(1)} %fusion.60) | copy-start | bytes 1572868
  21.9 0.8 copy-start.5
  22.7 30.7 %all-to-all-start = ((f32[32,40,128]{2,1,0:T(8,128)}), f32[32,40,128]{2,1,0:T(8,128)}, u32[]{:S(2)}, u32[]{:S(2)}) async-start(f32[32,40,128]{2,1,0:T(8,128)} %bitcast.171), calls=%async_computation | async-start | bytes 1310720 | tf_op jit(solution)/shard_map/all_to_all | solution.py:102
  35.6 64.3 %copy-start.12 = (pred[256,256]{0,1:T(8,128)(4,1)}, pred[256,256]{0,1:T(8,128)(4,1)S(1)}, u32[]{:S(2)}) copy-start(pred[256,256]{0,1:T(8,128)(4,1)S(1)} %fusion.69) | copy-start | bytes 196612
  36.4 1.3 copy-start.20
  56.1 24.4 %all-to-all-start.1 = ((f32[32,40,128]{2,1,0:T(8,128)}), f32[32,40,128]{2,1,0:T(8,128)}, u32[]{:S(2)}, u32[]{:S(2)}) async-start(f32[32,40,128]{2,1,0:T(8,128)} %copy.116), calls=%async_computation.1 | async-start | bytes 1310720 | tf_op jit(solution)/shard_map/all_to_all | solution.py:105
  80.4 2.6 %copy-start.1 = (f32[8,160,256]{2,1,0:T(8,128)S(1)}, f32[8,160,256]{2,1,0:T(8,128)}, u32[]{:S(2)}) copy-start(f32[8,160,256]{2,1,0:T(8,128)} %get-tuple-element.67) | copy-start | bytes 3932164
  86.8 1.2 copy-start.8
  90.2 24.3 %all-to-all-start.2 = ((f32[32,40,128]{2,1,0:T(8,128)}), f32[32,40,128]{2,1,0:T(8,128)}, u32[]{:S(2)}, u32[]{:S(2)}) async-start(f32[32,40,128]{2,1,0:T(8,128)} %bitcast.176), calls=%async_computation.2 | async-start | bytes 1310720 | tf_op jit(solution)/shard_map/all_to_all | solution.py:102
  95.7 3.5 %copy-start.10 = (f32[320,16,1]{0,1,2:T(8,128)S(1)}, f32[320,16,1]{0,1,2:T(8,128)}, u32[]{:S(2)}) copy-start(f32[320,16,1]{0,1,2:T(8,128)} %constant.87) | copy-start | bytes 61444
  95.7 4.3 %copy-start.21 = (f32[8,256,256]{1,2,0:T(8,128)S(1)}, f32[8,256,256]{1,2,0:T(8,128)}, u32[]{:S(2)}) copy-start(f32[8,256,256]{1,2,0:T(8,128)} %copy-done.20) | copy-start | bytes 6291460
  99.2 1.2 copy-start.9
  102.2 0.8 copy-start.13
  103.0 11.4 %copy-start.18 = (s32[32]{0:T(128)S(1)}, s32[32]{0:T(128)}, u32[]{:S(2)}) copy-start(s32[32]{0:T(128)} %gather_fusion.3) | copy-start | bytes 388
  103.0 11.4 %copy-start.19 = (s32[32]{0:T(128)S(1)}, s32[32]{0:T(128)}, u32[]{:S(2)}) copy-start(s32[32]{0:T(128)} %gather_fusion.2) | copy-start | bytes 388
  117.2 24.0 %all-to-all-start.3 = ((f32[32,40,128]{2,1,0:T(8,128)}), f32[32,40,128]{2,1,0:T(8,128)S(1)}, u32[]{:S(2)}, u32[]{:S(2)}) async-start(f32[32,40,128]{2,1,0:T(8,128)} %copy.128), calls=%async_computation.3 | async-start | bytes 1310720 | tf_op jit(solution)/shard_map/all_to_all | solution.py:105
  147.4 2.1 %copy-start.4 = (f32[256,1024]{1,0:T(8,128)S(1)}, f32[256,1024]{1,0:T(8,128)}, u32[]{:S(2)}) copy-start(f32[256,1024]{1,0:T(8,128)} %copy.130) | copy-start | bytes 3145732
  147.4 2.1 %copy-start.6 = (bf16[256,1024]{1,0:T(8,128)(2,1)S(1)}, bf16[256,1024]{1,0:T(8,128)(2,1)}, u32[]{:S(2)}) copy-start(bf16[256,1024]{1,0:T(8,128)(2,1)} %param.22) | copy-start | bytes 1572868
  147.4 2.1 %copy-start.7 = (bf16[256,1024]{1,0:T(8,128)(2,1)S(1)}, bf16[256,1024]{1,0:T(8,128)(2,1)}, u32[]{:S(2)}) copy-start(bf16[256,1024]{1,0:T(8,128)(2,1)} %param.23) | copy-start | bytes 1572868
  151.2 5.9 %collective-permute-start.1 = (f32[2,1024]{1,0:T(2,128)S(1)}, f32[2,1024]{1,0:T(2,128)S(1)}, u32[]{:S(2)}, u32[]{:S(2)}) collective-permute-start(f32[2,1024]{1,0:T(2,128)S(1)} %slice.124), channel_id=1, source_target_pairs={{8,0},{16,8},{24,16},{32,24},{40,32},{48,40},{56,48},{64,56},{72,6... | collective-permute-start | bytes 24584 | tf_op jit(solution)/shard_map/ppermute | solution.py:23
  155.6 1.5 copy-start.17

commit v5 on v4

--- a/solution.py
+++ b/solution.py
@@ -90,7 +90,7 @@
     return forward.astype(jnp.float32), backward.astype(jnp.float32)
 
 
-def state_scan(local_state, local_norm, mask, filler):
+def state_scan(local_state, local_norm, mask, filler, later_filler):
     devices = mask.shape[0]
     heads, feats, width = local_state.shape
     norm_rows = -(-feats // width)
@@ -102,9 +102,11 @@
     chunks = lax.all_to_all(packed, "ctx", 0, 0, tiled=True)
     chunks, filler = lax.optimization_barrier((chunks, filler))
     summed = jnp.einsum("ij,jrc->irc", mask, chunks, precision=high)
-    back = lax.all_to_all(summed, "ctx", 0, 0, tiled=True).reshape(heads, feats, width)
+    back = lax.all_to_all(summed, "ctx", 0, 0, tiled=True)
+    back, later_filler = lax.optimization_barrier((back, later_filler))
+    back = back.reshape(heads, feats, width)
     norm_in = back[:, room:].reshape(heads, norm_rows * width)[:, :feats]
-    return (back, norm_in, filler)
+    return (back, norm_in, filler, later_filler)
 
 
 def local(query, key, value_in, gate, conv_weight, doc_lengths, d_out):
@@ -164,8 +166,8 @@
     local_norm = jnp.sum(masked_key, axis=2)
     restart_all, closes_all = block_flags(doc_lengths, lax.axis_size("ctx"), tok_rows)
     forward_mask, backward_mask = scan_masks(restart_all, closes_all)
-    state_in, norm_in, (numerator, denominator) = state_scan(
-        local_state, local_norm, forward_mask, (numerator, denominator)
+    state_in, norm_in, (numerator, denominator), _ = state_scan(
+        local_state, local_norm, forward_mask, (numerator, denominator), ()
     )
     inside = (doc_ids == prev_doc).astype(jnp.float32)
     numerator = numerator + inside[:, None, None] * jnp.einsum(
@@ -196,10 +198,10 @@
         jnp.einsum("hfv,thv->hft", state_in, grad_num, precision=high)
         + norm_in[:, :, None] * jnp.transpose(grad_den, (1, 0))[:, None, :]
     )
-    grad_q = grad_q + feature_grad(grad_phi_query, spread_query)
-    grad_state_in, grad_norm_in, (grad_v, grad_q, grad_k) = state_scan(
-        back_state, back_norm, backward_mask, (grad_v, grad_q, grad_k)
-    )
+    grad_state_in, grad_norm_in, (grad_v, grad_q, grad_k), grad_q_tail = state_scan(
+        back_state, back_norm, backward_mask, (grad_v, grad_q, grad_k), feature_grad(grad_phi_query, spread_query)
+    )
+    grad_q = grad_q + grad_q_tail
     grad_v = grad_v + outside[:, None, None] * jnp.einsum(
         "hfs,hfv->shv", phi_key, grad_state_in, precision=high
     )

time: 161 us -> 162 us (level)
  other arithmetic: 13.2 us -> 17.2 us
  local copies, waits for them, and re-layouts: 25.3 us -> 23.5 us
  waiting for transfers between devices: 52.2 us -> 50.5 us
    all_to_all x2, waiting for transfers between devices: 29.8 us -> 25.7 us  [state_scan(): back = lax.all_to_all(summed, 'ctx', 0, 0, tiled=True)]
    dot_general x1, matrix products: 3.68 us -> 1.12 us  [local(): jnp.einsum('hfs,hfv->shv', phi_key, grad_state_in, precision=high)]
    all_to_all x2, waiting for transfers between devices: 22.4 us -> 24.8 us  [state_scan(): chunks = lax.all_to_all(packed, 'ctx', 0, 0, tiled=True)]
    convert_element_type x1, other arithmetic: 1.23 us -> 3.25 us  [local(): grad_value.astype(jnp.bfloat16)]
    dot_general x1, matrix products: 1.12 us -> 2.99 us  [local(): jnp.einsum('thv,shv->hts', grad_num, v_float, precision=high)]
    unnamed x53 -> x81, local copies, waits for them, and re-layouts: 9.89 us -> 9.49 us
  transfers between devices with their start and end apart: 6 -> 6, of which waited for: 4 -> 4; matrix products, arithmetic and copies ran while one was open for 23% -> 24% of each run, Pallas kernels for 0% -> 0%
where the time goes in v5:
time: 162 us; the launch traced here: 160 us
  waiting for transfers between devices  50.5 us (31%)
  starting transfers between devices  35.2 us (22%)
  matrix products  32.8 us (20%)
  local copies, waits for them, and re-layouts  23.5 us (15%)
  other arithmetic  17.2 us (11%)
    all_to_all x2, waiting for transfers between devices, state_scan(): back = lax.all_to_all(summed, 'ctx', 0, 0, tiled=True)  25.7 us
    all_to_all x2, waiting for transfers between devices, state_scan(): chunks = lax.all_to_all(packed, 'ctx', 0, 0, tiled=True)  24.8 us
    all_to_all x2, starting transfers between devices, state_scan(): chunks = lax.all_to_all(packed, 'ctx', 0, 0, tiled=True)  16.6 us
    all_to_all x2, starting transfers between devices, state_scan(): back = lax.all_to_all(summed, 'ctx', 0, 0, tiled=True)  10.8 us
    unnamed x81, local copies, waits for them, and re-layouts  9.49 us
    ppermute x2, starting transfers between devices, shifted(): return lax.ppermute(block, axis, route)  7.85 us
    dot_general x1, matrix products, local(): jnp.einsum('hft,hfv->thv', phi_query, state_in, precision=high)  3.78 us
    dot_general x1, matrix products, local(): jnp.einsum('hfv,shv->hfs', grad_state_in, v_float, precision=high)  3.57 us
  transfers between devices with their start and end apart: 6, of which 4 were waited for; matrix products, arithmetic and copies ran while one was open for 24% of the time, Pallas kernels for 0%

profile of v5, /device:TPU:32, one launch (start us, length us, event | category | flops | bytes accessed | tf_op | source)
XLA Modules:
  0.0 160.5 jit_solution(13647482320160810049)
XLA Ops:
  0.6 0.7 slice.83
  1.4 3.5 %collective-permute-start = (bf16[2,1024]{1,0:T(2,128)(2,1)S(1)}, bf16[2,1024]{1,0:T(2,128)(2,1)S(1)}, u32[]{:S(2)}, u32[]{:S(2)}) collective-permute-start(bf16[2,1024]{1,0:T(2,128)(2,1)S(1)} %slice.83), channel_id=1, source_target_pairs={{0,8},{8,16},{16,24},{24,32},{32,40},{40,48},{48,56},{56,64},{64,7... | collective-permute-start | bytes 12296 | tf_op jit(solution)/shard_map/ppermute | solution.py:23
  4.9 0.7 copy.109
  5.8 0.7 broadcast_add_fusion.3
  6.5 0.2 fusion.89
  6.7 0.7 compare_select_fusion
  7.4 0.6 fusion.108
  8.1 1.2 compare_convert_fusion.3
  9.2 0.6 fusion.107
  9.8 0.9 copy.108
  10.8 0.9 copy.111
  11.7 1.3 convolution_bitcast_fusion.1
  13.1 0.5 convolution_bitcast_fusion
  13.8 2.6 %compare_convert_fusion.1 = (f32[256]{0:T(256)}, f32[256]{0:T(256)}, f32[256]{0:T(256)S(1)}, f32[256]{0:T(256)S(1)}, f32[256]{0:T(256)S(1)}, /*index=5*/f32[256]{0:T(256)S(1)}, f32[256]{0:T(256)S(1)}) fusion(s32[256]{0:T(256)S(1)} %get-tuple-element.51, s32[258]{0:T(512)S(1)} %get-tuple-element.79, s32[]{:T(128)} %bitcast.32, s32[]{:T(128)} %bitcast.16, ...), kind=kLoop, calls=%fused_computation.137 | loop fusion | flops 3584 | bytes 12300 | tf_op jit(solution)/shard_map/convert_element_type | solution.py:223
  16.5 1.9 %multiply_reduce_fusion = (f32[8,160]{1,0:T(8,128)S(1)}, f32[8,160,256]{2,1,0:T(8,128)}, f32[8,160,256]{2,1,0:T(8,128)}) fusion(f32[256]{0:T(256)S(1)} %get-tuple-element.78, f32[160]{0:T(256)S(1)} %copy-done.26, f32[2,8,160,256]{3,2,1,0:T(8,128)S(1)} %convolution_bitcast_fusion.1, f32[160]{0:T(256)S(1)} %copy-done.27, f32[160]{0:T(256)S(1)} %copy-done.28, ...), kind=kLoop, calls=%fused_computation.45 | loop fusion | flops 3275520 | bytes 7872384 | tf_op jit(solution)/shard_map/reduce_sum | solution.py:166
  18.4 0.2 convert_reduce_fusion.2
  18.7 2.4 %fusion.62 = bf16[32,8,8,128]{3,2,1,0:T(8,128)(2,1)S(1)} fusion(bf16[256,1024]{1,0:T(8,128)(2,1)} %param.23, f32[256]{0:T(256)S(1)} %get-tuple-element.76, bf16[256,1024]{1,0:T(8,128)(2,1)} %param.22, bf16[2,1024]{1,0:T(2,128)(2,1)S(1)} %collective-permute-done, f32[1024]{0:T(1024)S(1)} %bitcast.194, f32[256]{0:T(256)S(1)} %get-tuple-element.77, ...), kind=kLoop, calls=%fused_computation.87 | loop fusion | flops 5767168 | bytes 1591296
  21.1 0.5 fusion.25
  21.7 0.8 copy-done.8
  22.5 11.1 %all-to-all-start = ((f32[32,40,128]{2,1,0:T(8,128)}), f32[32,40,128]{2,1,0:T(8,128)}, u32[]{:S(2)}, u32[]{:S(2)}) async-start(f32[32,40,128]{2,1,0:T(8,128)} %bitcast.173), calls=%async_computation | async-start | bytes 1310720 | tf_op jit(solution)/shard_map/all_to_all | solution.py:102
  33.9 0.7 gather_fusion.1
  34.6 0.7 gather_fusion
  35.5 0.8 fusion.60
  36.3 1.3 copy-done.34
  37.6 2.1 %convolution_bitcast_fusion.2 = f32[256,8,128]{0,2,1:T(8,128)} fusion(f32[8,256,256]{1,2,0:T(8,128)S(1)} %get-tuple-element.86, pred[256,256]{0,1:T(8,128)(4,1)S(1)} %fusion.71, bf16[32,8,8,128]{3,2,1,0:T(8,128)(2,1)S(1)} %fusion.62), kind=kOutput, calls=%fused_computation.22 | convolution fusion | flops 405798912 | bytes 3735552 | tf_op jit(solution)/shard_map/hts,shv->thv/dot_general | solution.py:159
  39.7 13.5 %all-to-all-done = f32[32,40,128]{2,1,0:T(8,128)} async-done(((f32[32,40,128]{2,1,0:T(8,128)}), f32[32,40,128]{2,1,0:T(8,128)}, u32[]{:S(2)}, u32[]{:S(2)}) %all-to-all-start) | async-done | bytes 655392 | tf_op jit(solution)/shard_map/all_to_all | solution.py:102
  53.2 1.5 fusion.55
  54.7 1.3 copy.116
  55.9 5.5 %all-to-all-start.1 = ((f32[32,40,128]{2,1,0:T(8,128)}), f32[32,40,128]{2,1,0:T(8,128)}, u32[]{:S(2)}, u32[]{:S(2)}) async-start(f32[32,40,128]{2,1,0:T(8,128)} %copy.116), calls=%async_computation.1 | async-start | bytes 1310720 | tf_op jit(solution)/shard_map/all_to_all | solution.py:105
  61.4 2.3 %copy.117 = f32[256,1024]{0,1:T(8,128)} copy(bf16[256,1024]{1,0:T(8,128)(2,1)} %param.26) | data formatting | bytes 1572864 | tf_op jit(solution)/shard_map/reshape | solution.py:181
  63.9 1.2 gather_fusion.3
  65.1 1.2 gather_fusion.2
  66.4 13.9 %all-to-all-done.1 = f32[32,40,128]{2,1,0:T(8,128)} async-done(((f32[32,40,128]{2,1,0:T(8,128)}), f32[32,40,128]{2,1,0:T(8,128)}, u32[]{:S(2)}, u32[]{:S(2)}) %all-to-all-start.1) | async-done | bytes 655392 | tf_op jit(solution)/shard_map/all_to_all | solution.py:105
  80.3 0.9 slice_bitcast_fusion.5
  81.2 0.6 fusion.105
  81.8 1.7 %fusion.79 = f32[8,1,256]{2,1,0:T(1,128)S(1)} fusion(f32[8,160,256]{2,1,0:T(8,128)} %get-tuple-element.71, f32[8,160,1]{1,0,2:T(8,128)S(1)} %get-tuple-element.65), kind=kOutput, calls=%fused_computation.122 | convolution fusion | flops 1966080 | bytes 1324032 | tf_op jit(solution)/shard_map/hft,hf->th/dot_general | solution.py:176
  83.5 3.8 %multiply_reduce_fusion.1 = (f32[256,8]{0,1:T(8,128)S(1)}, bf16[256,8,128]{0,2,1:T(8,128)(2,1)}) fusion(f32[256,1024]{0,1:T(8,128)} %copy.117, f32[256,8]{0,1:T(8,128)S(1)} %bitcast_add_fusion, f32[256,8,128]{0,2,1:T(8,128)} %convolution_bitcast_fusion.2, f32[8,160,128]{2,1,0:T(8,128)} %bitcast.21, f32[8,160,256]{2,1,0:T(8,128)S(1)} %copy-done.2, ...), kind=kOutput, calls=%fused_computation.72 | convolution fusion | flops 253229056 | bytes 4604928 | tf_op jit(solution)/shard_map/hft,hfv->thv/dot_general | solution.py:173
  87.3 1.6 %fusion.23 = f32[8,160,128]{2,1,0:T(8,128)} fusion(f32[8,160,256]{2,1,0:T(8,128)S(1)} %copy-done.2, f32[256]{0:T(256)S(1)} %get-tuple-element.74, f32[256,8,128]{0,2,1:T(8,128)S(1)} %bitcast.176, f32[256,8]{0,1:T(8,128)S(1)} %bitcast_add_fusion), kind=kOutput, calls=%fused_computation.43 | convolution fusion | flops 252248064 | bytes 3023872 | tf_op jit(solution)/shard_map/hft,thv->hfv/dot_general | solution.py:186
  89.0 0.6 fusion.21
  89.6 0.6 constant_dynamic-update-slice_fusion
  90.2 5.5 %all-to-all-start.2 = ((f32[32,40,128]{2,1,0:T(8,128)}), f32[32,40,128]{2,1,0:T(8,128)}, u32[]{:S(2)}, u32[]{:S(2)}) async-start(f32[32,40,128]{2,1,0:T(8,128)} %bitcast.178), calls=%async_computation.2 | async-start | bytes 1310720 | tf_op jit(solution)/shard_map/all_to_all | solution.py:102
  95.7 3.0 %multiply_select_fusion = f32[8,256,256]{1,2,0:T(8,128)S(1)} fusion(f32[8,256,256]{1,2,0:T(8,128)} %copy-done.34, f32[8,256]{1,0:T(8,128)S(1)} %get-tuple-element.62, pred[256,256]{0,1:T(8,128)(4,1)S(1)} %fusion.71, bf16[32,8,8,128]{3,2,1,0:T(8,128)(2,1)S(1)} %fusion.62, f32[256,8,128]{0,2,1:T(8,128)} %bitcast.174, f32[256,8]{0,1:T(8,128)S(1)} %bitcast_add_fusion), kind=kOutput, calls=%fused_computation.12 | convolution fusion | flops 405536768 | bytes 5849088 | tf_op jit(solution)/shard_map/thv,shv->hts/dot_general | solution.py:191
  98.7 0.5 fusion.38
  99.2 0.7 fusion.37
  99.9 0.4 copy-done.35
  100.3 0.4 copy-done.12
  100.7 2.5 %convolution_bitcast_fusion.3 = f32[256,8,128]{0,2,1:T(8,128)} fusion(f32[8,256,256]{1,2,0:T(8,128)S(1)} %copy-done.35, pred[256,256]{0,1:T(8,128)(4,1)S(1)} %copy-done.18, f32[256,8,128]{0,2,1:T(8,128)S(1)} %bitcast.177, f32[256,8]{0,1:T(8,128)S(1)} %copy-done.20), kind=kOutput, calls=%fused_computation.26 | convolution fusion | flops 406061056 | bytes 4268032 | tf_op jit(solution)/shard_map/hts,thv->shv/dot_general | solution.py:189
  103.2 11.3 %all-to-all-done.2 = f32[32,40,128]{2,1,0:T(8,128)} async-done(((f32[32,40,128]{2,1,0:T(8,128)}), f32[32,40,128]{2,1,0:T(8,128)}, u32[]{:S(2)}, u32[]{:S(2)}) %all-to-all-start.2) | async-done | bytes 655392 | tf_op jit(solution)/shard_map/all_to_all | solution.py:102
  114.5 1.5 fusion.53
  116.0 1.3 copy.127
  117.2 5.4 %all-to-all-start.3 = ((f32[32,40,128]{2,1,0:T(8,128)}), f32[32,40,128]{2,1,0:T(8,128)S(1)}, u32[]{:S(2)}, u32[]{:S(2)}) async-start(f32[32,40,128]{2,1,0:T(8,128)} %copy.127), calls=%async_computation.3 | async-start | bytes 1310720 | tf_op jit(solution)/shard_map/all_to_all | solution.py:105
  122.6 2.0 %copy.132 = bf16[256,1024]{1,0:T(8,128)(2,1)} copy(bf16[256,1024]{0,1:T(8,128)(2,1)} %bitcast.185) | data formatting | bytes 1048576
  124.6 3.4 %fusion.30 = (f32[8,160,256]{2,1,0:T(8,128)S(1)}, f32[8,160,256]{2,1,0:T(8,128)S(1)}) fusion(f32[2,8,160,256]{3,2,1,0:T(8,128)} %copy-done.3, f32[160]{0:T(256)} %constant.79.clone, f32[160]{0:T(256)} %constant.78.clone, f32[160]{0:T(256)} %constant.80.clone, f32[8,256]{1,0:T(8,128)} %copy-done.25, f32[8,160]{1,0:T(8,128)} %get-tuple-element.64, ...), kind=kOutput, calls=%fused_computation.51 | convolution fusion | flops 254541824 | bytes 6971264 | tf_op jit(solution)/shard_map/hfv,thv->hft/dot_general | solution.py:198
  128.0 1.4 fusion.34
  129.4 11.8 %all-to-all-done.3 = f32[32,40,128]{2,1,0:T(8,128)S(1)} async-done(((f32[32,40,128]{2,1,0:T(8,128)}), f32[32,40,128]{2,1,0:T(8,128)S(1)}, u32[]{:S(2)}, u32[]{:S(2)}) %all-to-all-start.3) | async-done | bytes 655392 | tf_op jit(solution)/shard_map/all_to_all | solution.py:105
  141.3 3.6 %fusion.28 = (f32[8,160,256]{2,1,0:T(8,128)}, f32[8,160,256]{2,1,0:T(8,128)}) fusion(f32[2,8,160,256]{3,2,1,0:T(8,128)S(1)} %convolution_bitcast_fusion.1, f32[160]{0:T(256)} %constant.79.clone, f32[160]{0:T(256)} %constant.78.clone, f32[160]{0:T(256)} %constant.80.clone, f32[8,160]{1,0:T(8,128)S(1)} %bitcast.197, f32[8,160,128]{2,1,0:T(8,128)S(1)} %bitcast.170, ...), kind=kOutput, calls=%fused_computation.49 | convolution fusion | flops 253952000 | bytes 6430592 | tf_op jit(solution)/shard_map/hfv,shv->hfs/dot_general | solution.py:209
  144.9 1.1 fusion.13
  146.0 1.3 copy.130
  147.3 3.2 %multiply_convert_fusion = (bf16[256,1024]{1,0:T(8,128)(2,1)}, f32[256,1024]{1,0:T(8,128)S(1)}) fusion(f32[256,1024]{1,0:T(8,128)} %copy.130, bf16[256,1024]{1,0:T(8,128)(2,1)} %param.23, f32[256]{0:T(256)} %copy-done.22, bf16[256,1024]{1,0:T(8,128)(2,1)S(1)} %copy-done.9, bf16[2,1024]{1,0:T(2,128)(2,1)S(1)} %collective-permute-done, f32[1024]{0:T(1024)S(1)} %bitcast.195, ...), kind=kLoop, calls=%fused_computation.71 | loop fusion | flops 6815744 | bytes 3688448 | tf_op jit(solution)/shard_map/convert_element_type | solution.py:216
  150.5 4.4 %collective-permute-start.1 = (f32[2,1024]{1,0:T(2,128)S(1)}, f32[2,1024]{1,0:T(2,128)S(1)}, u32[]{:S(2)}, u32[]{:S(2)}) collective-permute-start(f32[2,1024]{1,0:T(2,128)S(1)} %slice.124), channel_id=1, source_target_pairs={{8,0},{16,8},{24,16},{32,24},{40,32},{48,40},{56,48},{64,56},{72,6... | collective-permute-start | bytes 24584 | tf_op jit(solution)/shard_map/ppermute | solution.py:23
  155.0 0.7 fusion.42
  155.7 0.7 copy.133
  156.5 0.7 copy.134
  157.2 3.2 %fusion.50 = bf16[256,1024]{1,0:T(8,128)(2,1)} fusion(f32[256,1024]{1,0:T(8,128)} %copy-done.7, f32[2,1024]{1,0:T(2,128)S(1)} %collective-permute-done.1, f32[256]{0:T(256)S(1)} %copy-done.30, f32[256]{0:T(256)S(1)} %copy-done.29, f32[1024]{0:T(1024)S(1)} %bitcast.196, f32[1024]{0:T(1024)S(1)} %bitcast.193, f32[1024]{0:T(1024)S(1)} %bitcast.190), kind=kLoop, calls=%fused_computation.67 | loop fusion | flops 2621440 | bytes 1595392 | tf_op jit(solution)/shard_map/convert_element_type | solution.py:227
  (110 shorter events, 1.4 us)
Async XLA Ops:
  1.4 17.3 %collective-permute-start = (bf16[2,1024]{1,0:T(2,128)(2,1)S(1)}, bf16[2,1024]{1,0:T(2,128)(2,1)S(1)}, u32[]{:S(2)}, u32[]{:S(2)}) collective-permute-start(bf16[2,1024]{1,0:T(2,128)(2,1)S(1)} %slice.83), channel_id=1, source_target_pairs={{0,8},{8,16},{16,24},{24,32},{32,40},{40,48},{48,56},{56,64},{64,7... | collective-permute-start | bytes 12296 | tf_op jit(solution)/shard_map/ppermute | solution.py:23
  11.7 1.3 copy-start.16
  13.0 0.7 copy-start.21
  13.0 3.4 %copy-start.26 = (f32[160]{0:T(256)S(1)}, f32[160]{0:T(256)}, u32[]{:S(2)}) copy-start(f32[160]{0:T(256)} %constant.79.clone) | copy-start | bytes 1924
  13.1 3.4 %copy-start.27 = (f32[160]{0:T(256)S(1)}, f32[160]{0:T(256)}, u32[]{:S(2)}) copy-start(f32[160]{0:T(256)} %constant.78.clone) | copy-start | bytes 1924
  13.1 3.4 %copy-start.28 = (f32[160]{0:T(256)S(1)}, f32[160]{0:T(256)}, u32[]{:S(2)}) copy-start(f32[160]{0:T(256)} %constant.80.clone) | copy-start | bytes 1924
  13.7 4.6 %copy-start.3 = (f32[2,8,160,256]{3,2,1,0:T(8,128)}, f32[2,8,160,256]{3,2,1,0:T(8,128)S(1)}, u32[]{:S(2)}) copy-start(f32[2,8,160,256]{3,2,1,0:T(8,128)S(1)} %convolution_bitcast_fusion) | copy-start | bytes 7864324
  16.5 2.2 %copy-start.22 = (f32[256]{0:T(256)}, f32[256]{0:T(256)S(1)}, u32[]{:S(2)}) copy-start(f32[256]{0:T(256)S(1)} %get-tuple-element.76) | copy-start | bytes 3076
  16.5 2.2 %copy-start.23 = (f32[256]{0:T(256)}, f32[256]{0:T(256)S(1)}, u32[]{:S(2)}) copy-start(f32[256]{0:T(256)S(1)} %get-tuple-element.77) | copy-start | bytes 3076
  16.5 67.0 %copy-start.31 = (f32[256]{0:T(256)}, f32[256]{0:T(256)S(1)}, u32[]{:S(2)}) copy-start(f32[256]{0:T(256)S(1)} %get-tuple-element.75) | copy-start | bytes 3076
  18.6 2.5 %copy-start = (f32[8,160,256]{2,1,0:T(8,128)S(1)}, f32[8,160,256]{2,1,0:T(8,128)}, u32[]{:S(2)}) copy-start(f32[8,160,256]{2,1,0:T(8,128)} %get-tuple-element.53) | copy-start | bytes 3932164
  21.1 74.6 %copy-start.6 = (bf16[32,8,8,128]{3,2,1,0:T(8,128)(2,1)}, bf16[32,8,8,128]{3,2,1,0:T(8,128)(2,1)S(1)}, u32[]{:S(2)}) copy-start(bf16[32,8,8,128]{3,2,1,0:T(8,128)(2,1)S(1)} %fusion.62) | copy-start | bytes 1572868
  21.7 0.8 copy-start.8
  22.5 30.7 %all-to-all-start = ((f32[32,40,128]{2,1,0:T(8,128)}), f32[32,40,128]{2,1,0:T(8,128)}, u32[]{:S(2)}, u32[]{:S(2)}) async-start(f32[32,40,128]{2,1,0:T(8,128)} %bitcast.173), calls=%async_computation | async-start | bytes 1310720 | tf_op jit(solution)/shard_map/all_to_all | solution.py:102
  35.5 60.2 %copy-start.17 = (pred[256,256]{0,1:T(8,128)(4,1)}, pred[256,256]{0,1:T(8,128)(4,1)S(1)}, u32[]{:S(2)}) copy-start(pred[256,256]{0,1:T(8,128)(4,1)S(1)} %fusion.71) | copy-start | bytes 196612
  36.3 1.3 copy-start.34
  55.9 24.4 %all-to-all-start.1 = ((f32[32,40,128]{2,1,0:T(8,128)}), f32[32,40,128]{2,1,0:T(8,128)}, u32[]{:S(2)}, u32[]{:S(2)}) async-start(f32[32,40,128]{2,1,0:T(8,128)} %copy.116), calls=%async_computation.1 | async-start | bytes 1310720 | tf_op jit(solution)/shard_map/all_to_all | solution.py:105
  80.3 3.2 %copy-start.2 = (f32[8,160,256]{2,1,0:T(8,128)S(1)}, f32[8,160,256]{2,1,0:T(8,128)}, u32[]{:S(2)}) copy-start(f32[8,160,256]{2,1,0:T(8,128)} %get-tuple-element.71) | copy-start | bytes 3932164
  83.5 12.2 %copy-start.19 = (f32[256,8]{0,1:T(8,128)}, f32[256,8]{0,1:T(8,128)S(1)}, u32[]{:S(2)}) copy-start(f32[256,8]{0,1:T(8,128)S(1)} %bitcast_add_fusion) | copy-start | bytes 24580
  83.5 3.8 %copy-start.11 = (f32[256,1024]{0,1:T(8,128)S(1)}, f32[256,1024]{0,1:T(8,128)}, u32[]{:S(2)}) copy-start(f32[256,1024]{0,1:T(8,128)} %copy.117) | copy-start | bytes 3145732
  87.3 8.4 %copy-start.25 = (f32[8,256]{1,0:T(8,128)}, f32[8,256]{1,0:T(8,128)S(1)}, u32[]{:S(2)}) copy-start(f32[8,256]{1,0:T(8,128)S(1)} %get-tuple-element.62) | copy-start | bytes 24580
  90.2 24.3 %all-to-all-start.2 = ((f32[32,40,128]{2,1,0:T(8,128)}), f32[32,40,128]{2,1,0:T(8,128)}, u32[]{:S(2)}, u32[]{:S(2)}) async-start(f32[32,40,128]{2,1,0:T(8,128)} %bitcast.178), calls=%async_computation.2 | async-start | bytes 1310720 | tf_op jit(solution)/shard_map/all_to_all | solution.py:102
  98.7 1.6 copy-start.35
  99.2 1.5 copy-start.12
  99.2 1.5 copy-start.18
  99.2 1.5 copy-start.20
  100.7 13.8 %copy-start.32 = (s32[32]{0:T(128)S(1)}, s32[32]{0:T(128)}, u32[]{:S(2)}) copy-start(s32[32]{0:T(128)} %gather_fusion.3) | copy-start | bytes 388
  100.7 13.8 %copy-start.33 = (s32[32]{0:T(128)S(1)}, s32[32]{0:T(128)}, u32[]{:S(2)}) copy-start(s32[32]{0:T(128)} %gather_fusion.2) | copy-start | bytes 388
  117.2 24.0 %all-to-all-start.3 = ((f32[32,40,128]{2,1,0:T(8,128)}), f32[32,40,128]{2,1,0:T(8,128)S(1)}, u32[]{:S(2)}, u32[]{:S(2)}) async-start(f32[32,40,128]{2,1,0:T(8,128)} %copy.127), calls=%async_computation.3 | async-start | bytes 1310720 | tf_op jit(solution)/shard_map/all_to_all | solution.py:105
  124.6 3.4 %copy-start.14 = (f32[320,16,1]{0,1,2:T(8,128)S(1)}, f32[320,16,1]{0,1,2:T(8,128)}, u32[]{:S(2)}) copy-start(f32[320,16,1]{0,1,2:T(8,128)} %constant.87) | copy-start | bytes 61444
  141.2 3.6 %copy-start.1 = (f32[8,160,256]{2,1,0:T(8,128)S(1)}, f32[8,160,256]{2,1,0:T(8,128)}, u32[]{:S(2)}) copy-start(f32[8,160,256]{2,1,0:T(8,128)} %get-tuple-element.53) | copy-start | bytes 3932164
  141.2 3.6 %copy-start.10 = (f32[256,8,128]{0,2,1:T(8,128)S(1)}, f32[256,8,128]{0,2,1:T(8,128)}, u32[]{:S(2)}) copy-start(f32[256,8,128]{0,2,1:T(8,128)} %convolution_bitcast_fusion.3) | copy-start | bytes 3145732
  141.3 3.6 %copy-start.24 = (f32[256]{0:T(256)S(1)}, f32[256]{0:T(256)}, u32[]{:S(2)}) copy-start(f32[256]{0:T(256)} %get-tuple-element.50) | copy-start | bytes 3076
  146.0 1.3 copy-start.9
  147.3 7.6 %copy-start.13 = (f32[256,8,16]{0,2,1:T(8,128)S(1)}, f32[256,8,16]{0,2,1:T(8,128)}, u32[]{:S(2)}) copy-start(f32[256,8,16]{0,2,1:T(8,128)} %fusion.34) | copy-start | bytes 393220
  147.3 7.6 %copy-start.4 = (f32[8,160,256]{2,1,0:T(8,128)S(1)}, f32[8,160,256]{2,1,0:T(8,128)}, u32[]{:S(2)}) copy-start(f32[8,160,256]{2,1,0:T(8,128)} %get-tuple-element.54) | copy-start | bytes 3932164
  147.3 7.6 %copy-start.5 = (f32[8,160,256]{2,1,0:T(8,128)S(1)}, f32[8,160,256]{2,1,0:T(8,128)}, u32[]{:S(2)}) copy-start(f32[8,160,256]{2,1,0:T(8,128)} %get-tuple-element.55) | copy-start | bytes 3932164
  147.3 7.6 %copy-start.15 = (f32[320,16,1]{0,1,2:T(8,128)S(1)}, f32[320,16,1]{0,1,2:T(8,128)}, u32[]{:S(2)}) copy-start(f32[320,16,1]{0,1,2:T(8,128)} %constant.87) | copy-start | bytes 61444
  150.5 5.2 %copy-start.7 = (f32[256,1024]{1,0:T(8,128)}, f32[256,1024]{1,0:T(8,128)S(1)}, u32[]{:S(2)}) copy-start(f32[256,1024]{1,0:T(8,128)S(1)} %get-tuple-element.59) | copy-start | bytes 3145732
  150.5 6.7 %collective-permute-start.1 = (f32[2,1024]{1,0:T(2,128)S(1)}, f32[2,1024]{1,0:T(2,128)S(1)}, u32[]{:S(2)}, u32[]{:S(2)}) collective-permute-start(f32[2,1024]{1,0:T(2,128)S(1)} %slice.124), channel_id=1, source_target_pairs={{8,0},{16,8},{24,16},{32,24},{40,32},{48,40},{56,48},{64,56},{72,6... | collective-permute-start | bytes 24584 | tf_op jit(solution)/shard_map/ppermute | solution.py:23
  155.0 2.2 %copy-start.29 = (f32[256]{0:T(256)S(1)}, f32[256]{0:T(256)}, u32[]{:S(2)}) copy-start(f32[256]{0:T(256)} %get-tuple-element.69) | copy-start | bytes 3076
  155.0 2.2 %copy-start.30 = (f32[256]{0:T(256)S(1)}, f32[256]{0:T(256)}, u32[]{:S(2)}) copy-start(f32[256]{0:T(256)} %get-tuple-element.70) | copy-start | bytes 3076

commit v6 on v4

--- a/solution.py
+++ b/solution.py
@@ -200,6 +200,7 @@
     grad_state_in, grad_norm_in, (grad_v, grad_q, grad_k) = state_scan(
         back_state, back_norm, backward_mask, (grad_v, grad_q, grad_k)
     )
+    grad_v_local = grad_v
     grad_v = grad_v + outside[:, None, None] * jnp.einsum(
         "hfs,hfv->shv", phi_key, grad_state_in, precision=high
     )
@@ -213,7 +214,11 @@
     grad_core = grad_v.reshape(tok_rows, channels)
     grad_gate = (grad_core * convolved * opening * (1.0 - opening)).astype(jnp.bfloat16)
     grad_conv = grad_core * opening
-    later_rows = shifted(grad_conv[: CONV - 1], "ctx", -1)
+    edge_grad = grad_v_local[: CONV - 1] + outside[: CONV - 1, None, None] * jnp.einsum(
+        "hfs,hfv->shv", phi_key[:, :, : CONV - 1], grad_state_in, precision=high
+    )
+    edge_conv = edge_grad.reshape(CONV - 1, channels) * opening[: CONV - 1]
+    later_rows = shifted(edge_conv, "ctx", -1)
     ahead = jnp.concatenate([grad_conv, later_rows], axis=0)
     ahead_ids = jnp.concatenate([doc_ids, after_ids], axis=0)
     grad_value = jnp.zeros((tok_rows, channels), jnp.float32)

time: 161 us -> 164 us (1.019)
  matrix products: 31.2 us -> 36.1 us
  waiting for transfers between devices: 52.2 us -> 48.9 us
    dot_general x0 -> x2, local copies, waits for them, and re-layouts: none -> 5.16 us  [the longest x1 2.6 us: local(): jnp.einsum('hfs,hfv->shv', phi_key, grad_state_in, precision=high)]
    all_to_all x2, waiting for transfers between devices: 22.4 us -> 18.7 us  [state_scan(): chunks = lax.all_to_all(packed, 'ctx', 0, 0, tiled=True)]
    reshape x1 -> x0, local copies, waits for them, and re-layouts: 2.59 us -> none  [local(): grad_core = grad_v.reshape(tok_rows, channels)]
    dot_general x0 -> x1, matrix products: none -> 1.83 us  [local(): jnp.einsum('hfs,hfv->shv', phi_key[:, :, :CONV - 1], grad_state_in, preci...]
    dot_general x2, matrix products: 1.47 us -> 3.23 us  [feature_grad(): return jnp.einsum('fd,hft->thd', picks, both, precision=high)]
    unnamed x53 -> x49, local copies, waits for them, and re-layouts: 9.89 us -> 9.3 us
  transfers between devices with their start and end apart: 6 -> 6, of which waited for: 4 -> 4; matrix products, arithmetic and copies ran while one was open for 23% -> 25% of each run, Pallas kernels for 0% -> 0%
where the time goes in v6:
time: 164 us; the launch traced here: 161 us
  waiting for transfers between devices  48.9 us (30%)
  matrix products  36.1 us (22%)
  starting transfers between devices  35.3 us (22%)
  local copies, waits for them, and re-layouts  26.8 us (16%)
  other arithmetic  13.1 us (8%)
    all_to_all x2, waiting for transfers between devices, state_scan(): lax.all_to_all(summed, 'ctx', 0, 0, tiled=True).reshape(heads, feats, width)  30.2 us
    all_to_all x2, waiting for transfers between devices, state_scan(): chunks = lax.all_to_all(packed, 'ctx', 0, 0, tiled=True)  18.7 us
    all_to_all x2, starting transfers between devices, state_scan(): chunks = lax.all_to_all(packed, 'ctx', 0, 0, tiled=True)  16.6 us
    all_to_all x2, starting transfers between devices, state_scan(): lax.all_to_all(summed, 'ctx', 0, 0, tiled=True).reshape(heads, feats, width)  10.8 us
    unnamed x49, local copies, waits for them, and re-layouts  9.3 us
    ppermute x2, starting transfers between devices, shifted(): return lax.ppermute(block, axis, route)  7.85 us
    dot_general x1, matrix products, local(): jnp.einsum('hfv,thv->hft', state_in, grad_num, precision=high)  4.77 us
    dot_general x1, matrix products, local(): jnp.einsum('hft,hfv->thv', phi_query, state_in, precision=high)  3.84 us
  transfers between devices with their start and end apart: 6, of which 4 were waited for; matrix products, arithmetic and copies ran while one was open for 25% of the time, Pallas kernels for 0%

profile of v6, /device:TPU:32, one launch (start us, length us, event | category | flops | bytes accessed | tf_op | source)
XLA Modules:
  0.0 161.4 jit_solution(15097787553017620703)
XLA Ops:
  0.6 0.7 slice.92
  1.4 3.5 %collective-permute-start = (bf16[2,1024]{1,0:T(2,128)(2,1)S(1)}, bf16[2,1024]{1,0:T(2,128)(2,1)S(1)}, u32[]{:S(2)}, u32[]{:S(2)}) collective-permute-start(bf16[2,1024]{1,0:T(2,128)(2,1)S(1)} %slice.92), channel_id=1, source_target_pairs={{0,8},{8,16},{16,24},{24,32},{32,40},{40,48},{48,56},{56,64},{64,7... | collective-permute-start | bytes 12296 | tf_op jit(solution)/shard_map/ppermute | solution.py:23
  4.9 0.7 broadcast_add_fusion.3
  5.6 0.8 fusion.108
  6.4 0.7 copy.148
  7.6 0.7 compare_select_fusion
  8.3 0.6 fusion.110
  8.9 0.6 compare_convert_fusion.4
  9.5 0.6 fusion.109
  10.1 0.9 copy.150
  11.1 0.9 copy.147
  12.0 1.3 convolution_bitcast_fusion.1
  13.4 0.5 convolution_bitcast_fusion
  14.0 2.1 %compare_convert_fusion.1 = (f32[256]{0:T(256)S(1)}, f32[256]{0:T(256)S(1)}, f32[256]{0:T(256)S(1)}, f32[256]{0:T(256)S(1)}, f32[256]{0:T(256)S(1)}, /*index=5*/f32[256]{0:T(256)S(1)}, f32[256]{0:T(256)S(1)}) fusion(s32[256]{0:T(256)S(1)} %get-tuple-element.52, s32[258]{0:T(512)S(1)} %get-tuple-element.81, s32[]{:T(128)} %bitcast.32, s32[]{:T(128)} %bitcast.16, ...), kind=kLoop, calls=%fused_computation.144 | loop fusion | flops 3584 | bytes 12300 | tf_op jit(solution)/shard_map/convert_element_type | solution.py:226
  16.1 1.9 %multiply_reduce_fusion = (f32[8,160]{1,0:T(8,128)S(1)}, f32[8,160,256]{2,1,0:T(8,128)}, f32[8,160,256]{2,1,0:T(8,128)}) fusion(f32[256]{0:T(256)S(1)} %get-tuple-element.80, f32[160]{0:T(256)S(1)} %copy-done.15, f32[2,8,160,256]{3,2,1,0:T(8,128)S(1)} %convolution_bitcast_fusion.1, f32[160]{0:T(256)S(1)} %copy-done.16, f32[160]{0:T(256)S(1)} %copy-done.14, ...), kind=kLoop, calls=%fused_computation.41 | loop fusion | flops 3275520 | bytes 7872384 | tf_op jit(solution)/shard_map/reduce_sum | solution.py:164
  18.2 2.6 %fusion.64 = bf16[32,8,8,128]{3,2,1,0:T(8,128)(2,1)S(1)} fusion(f32[256]{0:T(256)S(1)} %get-tuple-element.78, bf16[256,1024]{1,0:T(8,128)(2,1)} %param.22, bf16[2,1024]{1,0:T(2,128)(2,1)S(1)} %collective-permute-done, f32[1024]{0:T(1024)S(1)} %bitcast.210, f32[256]{0:T(256)S(1)} %get-tuple-element.79, f32[1024]{0:T(1024)S(1)} %bitcast.207, ...), kind=kLoop, calls=%fused_computation.91 | loop fusion | flops 5767168 | bytes 1591296
  20.8 0.5 fusion.23
  21.4 0.9 copy-done.7
  22.3 11.1 %all-to-all-start = ((f32[32,40,128]{2,1,0:T(8,128)}), f32[32,40,128]{2,1,0:T(8,128)}, u32[]{:S(2)}, u32[]{:S(2)}) async-start(f32[32,40,128]{2,1,0:T(8,128)} %bitcast.189), calls=%async_computation | async-start | bytes 1310720 | tf_op jit(solution)/shard_map/all_to_all | solution.py:102
  33.7 0.7 gather_fusion.1
  34.4 0.7 gather_fusion
  35.2 0.8 fusion.62
  36.0 1.3 copy-done.18
  37.3 2.0 %convolution_bitcast_fusion.2 = f32[256,8,128]{0,2,1:T(8,128)} fusion(f32[8,256,256]{1,2,0:T(8,128)S(1)} %get-tuple-element.88, pred[256,256]{0,1:T(8,128)(4,1)S(1)} %fusion.73, bf16[32,8,8,128]{3,2,1,0:T(8,128)(2,1)S(1)} %fusion.64), kind=kOutput, calls=%fused_computation.22 | convolution fusion | flops 405798912 | bytes 3735552 | tf_op jit(solution)/shard_map/hts,shv->thv/dot_general | solution.py:157
  39.3 13.6 %all-to-all-done = f32[32,40,128]{2,1,0:T(8,128)} async-done(((f32[32,40,128]{2,1,0:T(8,128)}), f32[32,40,128]{2,1,0:T(8,128)}, u32[]{:S(2)}, u32[]{:S(2)}) %all-to-all-start) | async-done | bytes 655392 | tf_op jit(solution)/shard_map/all_to_all | solution.py:102
  52.9 1.5 fusion.56
  54.4 1.2 copy.155
  55.6 5.5 %all-to-all-start.1 = ((f32[32,40,128]{2,1,0:T(8,128)}), f32[32,40,128]{2,1,0:T(8,128)}, u32[]{:S(2)}, u32[]{:S(2)}) async-start(f32[32,40,128]{2,1,0:T(8,128)} %copy.155), calls=%async_computation.1 | async-start | bytes 1310720 | tf_op jit(solution)/shard_map/all_to_all | solution.py:105
  61.4 0.7 gather_fusion.3
  62.1 1.2 gather_fusion.2
  63.3 2.3 %copy.156 = f32[256,1024]{0,1:T(8,128)} copy(bf16[256,1024]{1,0:T(8,128)(2,1)} %param.26) | data formatting | bytes 1572864 | tf_op jit(solution)/shard_map/reshape | solution.py:179
  65.6 14.4 %all-to-all-done.1 = f32[32,40,128]{2,1,0:T(8,128)} async-done(((f32[32,40,128]{2,1,0:T(8,128)}), f32[32,40,128]{2,1,0:T(8,128)}, u32[]{:S(2)}, u32[]{:S(2)}) %all-to-all-start.1) | async-done | bytes 655392 | tf_op jit(solution)/shard_map/all_to_all | solution.py:105
  80.0 0.9 slice_bitcast_fusion.5
  80.9 1.7 %fusion.82 = f32[8,1,256]{2,1,0:T(1,128)S(1)} fusion(f32[8,160,256]{2,1,0:T(8,128)} %get-tuple-element.73, f32[8,160,1]{1,0,2:T(8,128)S(1)} %get-tuple-element.67), kind=kOutput, calls=%fused_computation.128 | convolution fusion | flops 1966080 | bytes 1324032 | tf_op jit(solution)/shard_map/hft,hf->th/dot_general | solution.py:174
  82.6 3.8 %multiply_reduce_fusion.1 = (f32[256,8]{0,1:T(8,128)S(1)}, bf16[256,8,128]{0,2,1:T(8,128)(2,1)}) fusion(f32[256,1024]{0,1:T(8,128)} %copy.156, f32[256,8]{0,1:T(8,128)S(1)} %bitcast_add_fusion.2, f32[256,8,128]{0,2,1:T(8,128)} %convolution_bitcast_fusion.2, f32[8,160,128]{2,1,0:T(8,128)} %bitcast.21, f32[8,160,256]{2,1,0:T(8,128)S(1)} %copy-done.2, ...), kind=kOutput, calls=%fused_computation.73 | convolution fusion | flops 253229056 | bytes 4604928 | tf_op jit(solution)/shard_map/hft,hfv->thv/dot_general | solution.py:171
  86.5 2.5 %fusion.61 = f32[8,128,256]{2,1,0:T(8,128)} fusion(f32[8,256,256]{1,2,0:T(8,128)S(1)} %copy-done.19, pred[256,256]{0,1:T(8,128)(4,1)S(1)} %fusion.73, f32[256,8,128]{0,2,1:T(8,128)S(1)} %bitcast.191, f32[256,8]{0,1:T(8,128)S(1)} %bitcast_add_fusion.2), kind=kOutput, calls=%fused_computation.86 | convolution fusion | flops 406061056 | bytes 4268032 | tf_op jit(solution)/shard_map/hts,thv->shv/dot_general | solution.py:187
  89.0 1.6 fusion.21
  90.6 0.6 fusion.19
  91.2 0.6 constant_dynamic-update-slice_fusion
  91.8 5.4 %all-to-all-start.2 = ((f32[32,40,128]{2,1,0:T(8,128)}), f32[32,40,128]{2,1,0:T(8,128)}, u32[]{:S(2)}, u32[]{:S(2)}) async-start(f32[32,40,128]{2,1,0:T(8,128)} %bitcast.194), calls=%async_computation.2 | async-start | bytes 1310720 | tf_op jit(solution)/shard_map/all_to_all | solution.py:102
  97.3 4.8 %fusion.28 = (f32[8,160,256]{2,1,0:T(8,128)}, f32[8,160,256]{2,1,0:T(8,128)}) fusion(f32[2,8,160,256]{3,2,1,0:T(8,128)} %copy-done.3, f32[160]{0:T(256)S(1)} %copy-done.15, f32[160]{0:T(256)S(1)} %copy-done.16, f32[160]{0:T(256)S(1)} %copy-done.14, f32[8,256]{1,0:T(8,128)S(1)} %get-tuple-element.64, f32[8,160]{1,0:T(8,128)S(1)} %get-tuple-element.66, ...), kind=kOutput, calls=%fused_computation.47 | convolution fusion | flops 254541824 | bytes 6971264 | tf_op jit(solution)/shard_map/hfv,thv->hft/dot_general | solution.py:196
  102.0 2.6 %copy.159 = f32[8,128,256]{1,0,2:T(8,128)} copy(f32[8,128,256]{2,1,0:T(8,128)} %fusion.61) | data formatting | bytes 2097152 | tf_op jit(solution)/shard_map/hts,thv->shv/dot_general | solution.py:187
  104.6 2.5 %fusion = f32[8,256,16]{1,2,0:T(8,128)S(1)} fusion(f32[320,16,1]{0,1,2:T(8,128)S(1)} %copy-done.12, f32[8,160,256]{2,1,0:T(8,128)} %get-tuple-element.58, f32[8,160,256]{2,1,0:T(8,128)} %get-tuple-element.57), kind=kOutput, calls=%fused_computation.4 | convolution fusion | flops 63569920 | bytes 2772992 | tf_op jit(solution)/shard_map/fd,hft->thd/dot_general | solution.py:67
  107.1 2.7 %multiply_select_fusion = f32[8,256,256]{1,2,0:T(8,128)S(1)} fusion(f32[8,256,256]{1,2,0:T(8,128)} %copy-done.18, f32[8,256]{1,0:T(8,128)S(1)} %get-tuple-element.64, pred[256,256]{0,1:T(8,128)(4,1)S(1)} %fusion.73, bf16[32,8,8,128]{3,2,1,0:T(8,128)(2,1)S(1)} %fusion.64, f32[256,8,128]{0,2,1:T(8,128)S(1)} %bitcast.193, f32[256,8]{0,1:T(8,128)S(1)} %bitcast_add_fusion.2), kind=kOutput, calls=%fused_computation.12 | convolution fusion | flops 405536768 | bytes 5849088 | tf_op jit(solution)/shard_map/thv,shv->hts/dot_general | solution.py:189
  109.8 0.7 fusion.32
  110.5 0.5 fusion.34
  110.9 5.1 %all-to-all-done.2 = f32[32,40,128]{2,1,0:T(8,128)} async-done(((f32[32,40,128]{2,1,0:T(8,128)}), f32[32,40,128]{2,1,0:T(8,128)}, u32[]{:S(2)}, u32[]{:S(2)}) %all-to-all-start.2) | async-done | bytes 655392 | tf_op jit(solution)/shard_map/all_to_all | solution.py:102
  116.1 1.5 fusion.54
  117.6 1.2 copy.168
  118.8 5.4 %all-to-all-start.3 = ((f32[32,40,128]{2,1,0:T(8,128)}), f32[32,40,128]{2,1,0:T(8,128)S(1)}, u32[]{:S(2)}, u32[]{:S(2)}) async-start(f32[32,40,128]{2,1,0:T(8,128)} %copy.168), calls=%async_computation.3 | async-start | bytes 1310720 | tf_op jit(solution)/shard_map/all_to_all | solution.py:105
  124.2 2.0 %copy.173 = bf16[256,1024]{1,0:T(8,128)(2,1)} copy(bf16[256,1024]{0,1:T(8,128)(2,1)} %bitcast.201) | data formatting | bytes 1048576
  126.2 0.7 copy.174
  127.0 15.8 %all-to-all-done.3 = f32[32,40,128]{2,1,0:T(8,128)S(1)} async-done(((f32[32,40,128]{2,1,0:T(8,128)}), f32[32,40,128]{2,1,0:T(8,128)S(1)}, u32[]{:S(2)}, u32[]{:S(2)}) %all-to-all-start.3) | async-done | bytes 655392 | tf_op jit(solution)/shard_map/all_to_all | solution.py:105
  142.8 1.8 %fusion.52 = f32[8,128,2]{1,2,0:T(2,128)S(1)} fusion(f32[8,160,128]{2,1,0:T(8,128)S(1)} %bitcast.182, f32[8,160,256]{2,1,0:T(8,128)} %get-tuple-element.54), kind=kOutput, calls=%fused_computation.77 | convolution fusion | flops 1966080 | bytes 1318912 | tf_op jit(solution)/shard_map/hfs,hfv->shv/dot_general | solution.py:217
  144.6 2.1 %fusion.111 = f32[8,128,256]{2,1,0:T(8,128)} fusion(f32[8,160,128]{2,1,0:T(8,128)S(1)} %bitcast.183, f32[8,160,256]{2,1,0:T(8,128)S(1)} %copy-done.1), kind=kOutput, calls=%fused_computation.199 | convolution fusion | flops 251658240 | bytes 3014656 | tf_op jit(solution)/shard_map/hfs,hfv->shv/dot_general | solution.py:204
  146.7 2.6 %copy.170 = f32[8,128,256]{1,0,2:T(8,128)} copy(f32[8,128,256]{2,1,0:T(8,128)} %fusion.111) | data formatting | bytes 2097152 | tf_op jit(solution)/shard_map/hfs,hfv->shv/dot_general | solution.py:204
  149.3 2.1 %fusion.26 = (f32[8,160,256]{2,1,0:T(8,128)S(1)}, f32[8,160,256]{2,1,0:T(8,128)S(1)}) fusion(f32[2,8,160,256]{3,2,1,0:T(8,128)S(1)} %convolution_bitcast_fusion.1, f32[160]{0:T(256)S(1)} %copy-done.15, f32[160]{0:T(256)S(1)} %copy-done.16, f32[160]{0:T(256)S(1)} %copy-done.14, f32[8,160]{1,0:T(8,128)S(1)} %bitcast.213, f32[8,160,128]{2,1,0:T(8,128)S(1)} %bitcast.185, ...), kind=kOutput, calls=%fused_computation.45 | convolution fusion | flops 253952000 | bytes 6430592 | tf_op jit(solution)/shard_map/hfv,shv->hfs/dot_general | solution.py:208
  151.4 0.3 bitcast_add_fusion
  151.8 0.6 copy-done.8
  152.6 1.7 %fusion.49 = (bf16[256,1024]{1,0:T(8,128)(2,1)}, f32[256,1024]{1,0:T(8,128)S(1)}, f32[256,1024]{1,0:T(8,128)S(1)}) fusion(f32[32,8,8,128]{3,2,1,0:T(8,128)S(1)} %bitcast.188, f32[256]{0:T(256)S(1)} %get-tuple-element.78, bf16[256,1024]{1,0:T(8,128)(2,1)S(1)} %copy-done.8, bf16[2,1024]{1,0:T(2,128)(2,1)S(1)} %collective-permute-done, f32[1024]{0:T(1024)S(1)} %bitcast.211, ...), kind=kLoop, calls=%fused_computation.68 | loop fusion | flops 6815744 | bytes 4737024 | tf_op jit(solution)/shard_map/convert_element_type | solution.py:215
  154.3 4.4 %collective-permute-start.1 = (f32[2,1024]{1,0:T(2,128)S(1)}, f32[2,1024]{1,0:T(2,128)S(1)}, u32[]{:S(2)}, u32[]{:S(2)}) collective-permute-start(f32[2,1024]{1,0:T(2,128)S(1)} %bitcast_multiply_fusion.2), channel_id=1, source_target_pairs={{8,0},{16,8},{24,16},{32,24},{40,32},{48,40},{56,48},{64,56},{72,6... | collective-permute-start | bytes 24584 | tf_op jit(solution)/shard_map/ppermute | solution.py:23
  158.7 0.7 fusion.38
  159.4 0.7 copy.175
  160.2 1.2 fusion.46
  (82 shorter events, 1.9 us)
Async XLA Ops:
  1.4 16.9 %collective-permute-start = (bf16[2,1024]{1,0:T(2,128)(2,1)S(1)}, bf16[2,1024]{1,0:T(2,128)(2,1)S(1)}, u32[]{:S(2)}, u32[]{:S(2)}) collective-permute-start(bf16[2,1024]{1,0:T(2,128)(2,1)S(1)} %slice.92), channel_id=1, source_target_pairs={{0,8},{8,16},{16,24},{24,32},{32,40},{40,48},{48,56},{56,64},{64,7... | collective-permute-start | bytes 12296 | tf_op jit(solution)/shard_map/ppermute | solution.py:23
  12.0 1.3 copy-start.13
  13.3 2.7 %copy-start.14 = (f32[160]{0:T(256)S(1)}, f32[160]{0:T(256)}, u32[]{:S(2)}) copy-start(f32[160]{0:T(256)} %constant.80.clone) | copy-start | bytes 1924
  13.3 2.7 %copy-start.15 = (f32[160]{0:T(256)S(1)}, f32[160]{0:T(256)}, u32[]{:S(2)}) copy-start(f32[160]{0:T(256)} %constant.79.clone) | copy-start | bytes 1924
  13.4 2.7 %copy-start.16 = (f32[160]{0:T(256)S(1)}, f32[160]{0:T(256)}, u32[]{:S(2)}) copy-start(f32[160]{0:T(256)} %constant.78.clone) | copy-start | bytes 1924
  13.9 4.1 %copy-start.3 = (f32[2,8,160,256]{3,2,1,0:T(8,128)}, f32[2,8,160,256]{3,2,1,0:T(8,128)S(1)}, u32[]{:S(2)}) copy-start(f32[2,8,160,256]{3,2,1,0:T(8,128)S(1)} %convolution_bitcast_fusion) | copy-start | bytes 7864324
  18.2 2.6 %copy-start = (f32[8,160,256]{2,1,0:T(8,128)S(1)}, f32[8,160,256]{2,1,0:T(8,128)}, u32[]{:S(2)}) copy-start(f32[8,160,256]{2,1,0:T(8,128)} %get-tuple-element.54) | copy-start | bytes 3932164
  20.8 86.3 %copy-start.4 = (bf16[32,8,8,128]{3,2,1,0:T(8,128)(2,1)}, bf16[32,8,8,128]{3,2,1,0:T(8,128)(2,1)S(1)}, u32[]{:S(2)}) copy-start(bf16[32,8,8,128]{3,2,1,0:T(8,128)(2,1)S(1)} %fusion.64) | copy-start | bytes 1572868
  21.4 0.9 copy-start.7
  22.3 30.7 %all-to-all-start = ((f32[32,40,128]{2,1,0:T(8,128)}), f32[32,40,128]{2,1,0:T(8,128)}, u32[]{:S(2)}, u32[]{:S(2)}) async-start(f32[32,40,128]{2,1,0:T(8,128)} %bitcast.189), calls=%async_computation | async-start | bytes 1310720 | tf_op jit(solution)/shard_map/all_to_all | solution.py:102
  36.0 1.3 copy-start.18
  55.6 24.4 %all-to-all-start.1 = ((f32[32,40,128]{2,1,0:T(8,128)}), f32[32,40,128]{2,1,0:T(8,128)}, u32[]{:S(2)}, u32[]{:S(2)}) async-start(f32[32,40,128]{2,1,0:T(8,128)} %copy.155), calls=%async_computation.1 | async-start | bytes 1310720 | tf_op jit(solution)/shard_map/all_to_all | solution.py:105
  80.0 2.6 %copy-start.2 = (f32[8,160,256]{2,1,0:T(8,128)S(1)}, f32[8,160,256]{2,1,0:T(8,128)}, u32[]{:S(2)}) copy-start(f32[8,160,256]{2,1,0:T(8,128)} %get-tuple-element.73) | copy-start | bytes 3932164
  82.6 3.9 %copy-start.10 = (f32[256,1024]{0,1:T(8,128)S(1)}, f32[256,1024]{0,1:T(8,128)}, u32[]{:S(2)}) copy-start(f32[256,1024]{0,1:T(8,128)} %copy.156) | copy-start | bytes 3145732
  82.6 3.9 %copy-start.19 = (f32[8,256,256]{1,2,0:T(8,128)S(1)}, f32[8,256,256]{1,2,0:T(8,128)}, u32[]{:S(2)}) copy-start(f32[8,256,256]{1,2,0:T(8,128)} %copy-done.18) | copy-start | bytes 6291460
  91.8 24.3 %all-to-all-start.2 = ((f32[32,40,128]{2,1,0:T(8,128)}), f32[32,40,128]{2,1,0:T(8,128)}, u32[]{:S(2)}, u32[]{:S(2)}) async-start(f32[32,40,128]{2,1,0:T(8,128)} %bitcast.194), calls=%async_computation.2 | async-start | bytes 1310720 | tf_op jit(solution)/shard_map/all_to_all | solution.py:102
  102.0 2.6 %copy-start.12 = (f32[320,16,1]{0,1,2:T(8,128)S(1)}, f32[320,16,1]{0,1,2:T(8,128)}, u32[]{:S(2)}) copy-start(f32[320,16,1]{0,1,2:T(8,128)} %constant.87) | copy-start | bytes 61444
  104.6 2.5 %copy-start.11 = (f32[256,1024]{0,1:T(8,128)S(1)}, f32[256,1024]{0,1:T(8,128)}, u32[]{:S(2)}) copy-start(f32[256,1024]{0,1:T(8,128)} %copy.156) | copy-start | bytes 3145732
  110.5 5.6 %copy-start.17 = (s32[32]{0:T(128)S(1)}, s32[32]{0:T(128)}, u32[]{:S(2)}) copy-start(s32[32]{0:T(128)} %gather_fusion.2) | copy-start | bytes 388
  118.8 24.0 %all-to-all-start.3 = ((f32[32,40,128]{2,1,0:T(8,128)}), f32[32,40,128]{2,1,0:T(8,128)S(1)}, u32[]{:S(2)}, u32[]{:S(2)}) async-start(f32[32,40,128]{2,1,0:T(8,128)} %copy.168), calls=%async_computation.3 | async-start | bytes 1310720 | tf_op jit(solution)/shard_map/all_to_all | solution.py:105
  142.8 1.8 %copy-start.1 = (f32[8,160,256]{2,1,0:T(8,128)S(1)}, f32[8,160,256]{2,1,0:T(8,128)}, u32[]{:S(2)}) copy-start(f32[8,160,256]{2,1,0:T(8,128)} %get-tuple-element.54) | copy-start | bytes 3932164
  149.3 2.1 %copy-start.5 = (f32[8,128,256]{1,0,2:T(8,128)S(1)}, f32[8,128,256]{1,0,2:T(8,128)}, u32[]{:S(2)}) copy-start(f32[8,128,256]{1,0,2:T(8,128)} %copy.159) | copy-start | bytes 3145732
  149.3 2.1 %copy-start.6 = (f32[8,128,256]{1,0,2:T(8,128)S(1)}, f32[8,128,256]{1,0,2:T(8,128)}, u32[]{:S(2)}) copy-start(f32[8,128,256]{1,0,2:T(8,128)} %copy.170) | copy-start | bytes 3145732
  151.4 1.0 copy-start.8
  151.4 1.2 copy-start.9
  154.3 5.9 %collective-permute-start.1 = (f32[2,1024]{1,0:T(2,128)S(1)}, f32[2,1024]{1,0:T(2,128)S(1)}, u32[]{:S(2)}, u32[]{:S(2)}) collective-permute-start(f32[2,1024]{1,0:T(2,128)S(1)} %bitcast_multiply_fusion.2), channel_id=1, source_target_pairs={{8,0},{16,8},{24,16},{32,24},{40,32},{48,40},{56,48},{64,56},{72,6... | collective-permute-start | bytes 24584 | tf_op jit(solution)/shard_map/ppermute | solution.py:23

commit v7 on v5

--- a/solution.py
+++ b/solution.py
@@ -166,8 +166,15 @@
     local_norm = jnp.sum(masked_key, axis=2)
     restart_all, closes_all = block_flags(doc_lengths, lax.axis_size("ctx"), tok_rows)
     forward_mask, backward_mask = scan_masks(restart_all, closes_all)
-    state_in, norm_in, (numerator, denominator), _ = state_scan(
-        local_state, local_norm, forward_mask, (numerator, denominator), ()
+    upstream_values = jnp.einsum(
+        "thv,shv->hts",
+        d_out.reshape(tok_rows, HEADS, VD),
+        value_rows.reshape(tok_rows, HEADS, VD),
+        preferred_element_type=jnp.float32,
+    )
+    gate_slope = convolved * opening * (1.0 - opening)
+    state_in, norm_in, (numerator, denominator), (upstream_values, gate_slope) = state_scan(
+        local_state, local_norm, forward_mask, (numerator, denominator), (upstream_values, gate_slope)
     )
     inside = (doc_ids == prev_doc).astype(jnp.float32)
     numerator = numerator + inside[:, None, None] * jnp.einsum(
@@ -188,7 +195,7 @@
     outside = (doc_ids == next_doc).astype(jnp.float32)
     grad_v = jnp.einsum("hts,thv->shv", weights, grad_num, precision=high)
     grad_weights = (
-        jnp.einsum("thv,shv->hts", grad_num, v_float, precision=high)
+        upstream_values / jnp.transpose(denominator, (1, 0))[:, :, None]
         + jnp.transpose(grad_den, (1, 0))[:, :, None]
     )
     grad_scores = jnp.where(allowed[None], grad_weights * (1.0 + scores), 0.0)
@@ -198,10 +205,10 @@
         jnp.einsum("hfv,thv->hft", state_in, grad_num, precision=high)
         + norm_in[:, :, None] * jnp.transpose(grad_den, (1, 0))[:, None, :]
     )
-    grad_state_in, grad_norm_in, (grad_v, grad_q, grad_k), grad_q_tail = state_scan(
-        back_state, back_norm, backward_mask, (grad_v, grad_q, grad_k), feature_grad(grad_phi_query, spread_query)
-    )
-    grad_q = grad_q + grad_q_tail
+    grad_q = grad_q + feature_grad(grad_phi_query, spread_query)
+    grad_state_in, grad_norm_in, (grad_v, grad_q, grad_k), _ = state_scan(
+        back_state, back_norm, backward_mask, (grad_v, grad_q, grad_k), ()
+    )
     grad_v = grad_v + outside[:, None, None] * jnp.einsum(
         "hfs,hfv->shv", phi_key, grad_state_in, precision=high
     )
@@ -213,7 +220,7 @@
     grad_query = grad_q.reshape(tok_rows, HEADS * KD).astype(jnp.bfloat16)
     grad_key = grad_k.reshape(tok_rows, HEADS * KD).astype(jnp.bfloat16)
     grad_core = grad_v.reshape(tok_rows, channels)
-    grad_gate = (grad_core * convolved * opening * (1.0 - opening)).astype(jnp.bfloat16)
+    grad_gate = (grad_core * gate_slope).astype(jnp.bfloat16)
     grad_conv = grad_core * opening
     later_rows = shifted(grad_conv[: CONV - 1], "ctx", -1)
     ahead = jnp.concatenate([grad_conv, later_rows], axis=0)

time: 162 us -> 164 us (1.012)
  local copies, waits for them, and re-layouts: 23.5 us -> 25.7 us
    unnamed x81 -> x42, local copies, waits for them, and re-layouts: 9.49 us -> 13.7 us
    mul x0 -> x1, other arithmetic: none -> 3.6 us  [local(): gate_slope = convolved * opening * (1.0 - opening)]
    all_to_all x2, waiting for transfers between devices: 24.8 us -> 21.5 us  [state_scan(): chunks = lax.all_to_all(packed, 'ctx', 0, 0, tiled=True)]
    dot_general x1, matrix products: 1.12 us -> 3.93 us  [local(): jnp.einsum('hfs,hfv->shv', phi_key, grad_state_in, precision=high)]
    select_n x0 -> x1, other arithmetic: none -> 2.81 us  [local(): grad_scores = jnp.where(allowed[None], grad_weights * (1.0 + scores), 0.0)]
    all_to_all x2, waiting for transfers between devices: 25.7 us -> 28.2 us  [state_scan(): back = lax.all_to_all(summed, 'ctx', 0, 0, tiled=True)]
    unnamed x1 -> x0, other arithmetic: 2.43 us -> none
    reshape x1 -> x0, local copies, waits for them, and re-layouts: 2.26 us -> none  [local(): upstream = d_out.astype(jnp.float32).reshape(tok_rows, HEADS, VD)]
where the time goes in v7:
time: 164 us; the launch traced here: 161 us
  waiting for transfers between devices  49.7 us (30%)
  starting transfers between devices  35.3 us (22%)
  matrix products  31.8 us (19%)
  local copies, waits for them, and re-layouts  25.7 us (16%)
  other arithmetic  17.7 us (11%)
    all_to_all x2, waiting for transfers between devices, state_scan(): back = lax.all_to_all(summed, 'ctx', 0, 0, tiled=True)  28.2 us
    all_to_all x2, waiting for transfers between devices, state_scan(): chunks = lax.all_to_all(packed, 'ctx', 0, 0, tiled=True)  21.5 us
    all_to_all x2, starting transfers between devices, state_scan(): chunks = lax.all_to_all(packed, 'ctx', 0, 0, tiled=True)  16.6 us
    unnamed x42, local copies, waits for them, and re-layouts  13.7 us
    all_to_all x2, starting transfers between devices, state_scan(): back = lax.all_to_all(summed, 'ctx', 0, 0, tiled=True)  10.9 us
    ppermute x2, starting transfers between devices, shifted(): return lax.ppermute(block, axis, route)  7.87 us
    dot_general x1, matrix products, local(): jnp.einsum('hfs,hfv->shv', phi_key, grad_state_in, precision=high)  3.93 us
    dot_general x1, matrix products, local(): jnp.einsum('hft,hfv->thv', phi_query, state_in, precision=high)  3.61 us
  transfers between devices with their start and end apart: 6, of which 4 were waited for; matrix products, arithmetic and copies ran while one was open for 24% of the time, Pallas kernels for 0%

profile of v7, /device:TPU:32, one launch (start us, length us, event | category | flops | bytes accessed | tf_op | source)
XLA Modules:
  0.0 161.3 jit_solution(1750847612959741499)
XLA Ops:
  0.6 0.7 slice.83
  1.4 3.5 %collective-permute-start = (bf16[2,1024]{1,0:T(2,128)(2,1)S(1)}, bf16[2,1024]{1,0:T(2,128)(2,1)S(1)}, u32[]{:S(2)}, u32[]{:S(2)}) collective-permute-start(bf16[2,1024]{1,0:T(2,128)(2,1)S(1)} %slice.83), channel_id=1, source_target_pairs={{0,8},{8,16},{16,24},{24,32},{32,40},{40,48},{48,56},{56,64},{64,7... | collective-permute-start | bytes 12296 | tf_op jit(solution)/shard_map/ppermute | solution.py:23
  4.9 0.7 broadcast_add_fusion.3
  5.6 0.8 fusion.104
  6.4 0.7 copy.106
  7.6 0.7 compare_select_fusion
  8.3 0.6 fusion.106
  8.9 0.6 compare_convert_fusion.4
  9.5 0.6 fusion.105
  10.1 0.9 copy.108
  11.1 0.9 copy.105
  12.0 1.3 convolution_bitcast_fusion.1
  13.4 0.5 convolution_bitcast_fusion
  14.0 2.1 %compare_convert_fusion.1 = (f32[256]{0:T(256)S(1)}, f32[256]{0:T(256)S(1)}, f32[256]{0:T(256)S(1)}, f32[256]{0:T(256)S(1)}, f32[256]{0:T(256)S(1)}, /*index=5*/f32[256]{0:T(256)S(1)}, f32[256]{0:T(256)S(1)}) fusion(s32[256]{0:T(256)S(1)} %get-tuple-element.53, s32[258]{0:T(512)S(1)} %get-tuple-element.83, s32[]{:T(128)} %bitcast.34, s32[]{:T(128)} %bitcast.16, ...), kind=kLoop, calls=%fused_computation.138 | loop fusion | flops 3584 | bytes 12300 | tf_op jit(solution)/shard_map/convert_element_type | solution.py:230
  16.1 1.9 %multiply_reduce_fusion = (f32[8,160]{1,0:T(8,128)S(1)}, f32[8,160,256]{2,1,0:T(8,128)}, f32[8,160,256]{2,1,0:T(8,128)}) fusion(f32[256]{0:T(256)S(1)} %get-tuple-element.82, f32[160]{0:T(256)S(1)} %copy-done.14, f32[2,8,160,256]{3,2,1,0:T(8,128)S(1)} %convolution_bitcast_fusion.1, f32[160]{0:T(256)S(1)} %copy-done.15, f32[160]{0:T(256)S(1)} %copy-done.13, ...), kind=kLoop, calls=%fused_computation.48 | loop fusion | flops 3275520 | bytes 7872384 | tf_op jit(solution)/shard_map/reduce_sum | solution.py:166
  18.3 3.6 %subtract_multiply_fusion = (f32[256,1024]{1,0:T(8,128)}, bf16[256,1024]{1,0:T(8,128)(2,1)S(1)}) fusion(bf16[256,1024]{1,0:T(8,128)(2,1)} %param.23, f32[256]{0:T(256)S(1)} %get-tuple-element.80, bf16[256,1024]{1,0:T(8,128)(2,1)} %param.22, bf16[2,1024]{1,0:T(2,128)(2,1)S(1)} %collective-permute-done, f32[1024]{0:T(1024)S(1)} %bitcast.205, ...), kind=kLoop, calls=%fused_computation.76 | loop fusion | flops 6291456 | bytes 2639872 | tf_op jit(solution)/shard_map/mul | solution.py:175
  21.9 0.5 fusion.25
  22.4 0.9 copy-done.6
  23.3 11.1 %all-to-all-start = ((f32[32,40,128]{2,1,0:T(8,128)}), f32[32,40,128]{2,1,0:T(8,128)}, u32[]{:S(2)}, u32[]{:S(2)}) async-start(f32[32,40,128]{2,1,0:T(8,128)} %bitcast.185), calls=%async_computation | async-start | bytes 1310720 | tf_op jit(solution)/shard_map/all_to_all | solution.py:102
  34.7 0.7 gather_fusion.1
  35.4 0.7 gather_fusion
  36.2 0.8 fusion.59
  37.0 1.3 copy-done.7
  38.3 2.0 %convolution_bitcast_fusion.3 = f32[256,8,128]{0,2,1:T(8,128)} fusion(f32[8,256,256]{1,2,0:T(8,128)S(1)} %get-tuple-element.90, pred[256,256]{0,1:T(8,128)(4,1)S(1)} %fusion.69, bf16[256,1024]{1,0:T(8,128)(2,1)S(1)} %get-tuple-element.55), kind=kOutput, calls=%fused_computation.23 | convolution fusion | flops 405798912 | bytes 3735552 | tf_op jit(solution)/shard_map/hts,shv->thv/dot_general | solution.py:159
  40.4 13.6 %all-to-all-done = f32[32,40,128]{2,1,0:T(8,128)} async-done(((f32[32,40,128]{2,1,0:T(8,128)}), f32[32,40,128]{2,1,0:T(8,128)}, u32[]{:S(2)}, u32[]{:S(2)}) %all-to-all-start) | async-done | bytes 655392 | tf_op jit(solution)/shard_map/all_to_all | solution.py:102
  54.0 1.5 fusion.54
  55.4 1.2 copy.113
  56.7 5.5 %all-to-all-start.1 = ((f32[32,40,128]{2,1,0:T(8,128)}), f32[32,40,128]{2,1,0:T(8,128)}, u32[]{:S(2)}, u32[]{:S(2)}) async-start(f32[32,40,128]{2,1,0:T(8,128)} %copy.113), calls=%async_computation.1 | async-start | bytes 1310720 | tf_op jit(solution)/shard_map/all_to_all | solution.py:105
  62.4 0.7 gather_fusion.3
  63.1 0.7 gather_fusion.2
  63.8 2.0 %copy.114 = bf16[256,1024]{0,1:T(8,128)(2,1)} copy(bf16[256,1024]{1,0:T(8,128)(2,1)} %param.26) | data formatting | bytes 1048576 | tf_op args[6]
  65.9 2.8 %convolution_bitcast_fusion.2 = f32[8,256,256]{1,2,0:T(8,128)} fusion(bf16[256,8,128]{0,2,1:T(8,128)(2,1)} %bitcast.186, bf16[256,1024]{1,0:T(8,128)(2,1)S(1)} %get-tuple-element.55), kind=kOutput, calls=%fused_computation.16 | convolution fusion | flops 134217728 | bytes 3145728 | tf_op jit(solution)/shard_map/thv,shv->hts/dot_general | solution.py:169
  68.7 12.3 %all-to-all-done.1 = f32[32,40,128]{2,1,0:T(8,128)} async-done(((f32[32,40,128]{2,1,0:T(8,128)}), f32[32,40,128]{2,1,0:T(8,128)}, u32[]{:S(2)}, u32[]{:S(2)}) %all-to-all-start.1) | async-done | bytes 655392 | tf_op jit(solution)/shard_map/all_to_all | solution.py:105
  81.0 0.9 slice_bitcast_fusion.5
  81.9 1.7 %fusion.77 = f32[8,1,256]{2,1,0:T(1,128)S(1)} fusion(f32[8,160,256]{2,1,0:T(8,128)} %get-tuple-element.75, f32[8,160,1]{1,0,2:T(8,128)S(1)} %get-tuple-element.69), kind=kOutput, calls=%fused_computation.123 | convolution fusion | flops 1966080 | bytes 1324032 | tf_op jit(solution)/shard_map/hft,hf->th/dot_general | solution.py:183
  83.7 3.6 %fusion.49 = (f32[256,8]{0,1:T(8,128)S(1)}, bf16[256,8,128]{0,2,1:T(8,128)(2,1)}) fusion(bf16[256,1024]{0,1:T(8,128)(2,1)} %copy.114, f32[256,8]{0,1:T(8,128)S(1)} %bitcast_add_fusion, f32[256,8,128]{0,2,1:T(8,128)} %convolution_bitcast_fusion.3, f32[8,160,128]{2,1,0:T(8,128)} %bitcast.23, f32[8,160,256]{2,1,0:T(8,128)S(1)} %copy-done.1, ...), kind=kOutput, calls=%fused_computation.71 | convolution fusion | flops 253491200 | bytes 4080640 | tf_op jit(solution)/shard_map/hft,hfv->thv/dot_general | solution.py:180
  87.3 1.6 fusion.23
  88.9 0.6 fusion.21
  89.5 0.6 constant_dynamic-update-slice_fusion
  90.1 5.5 %all-to-all-start.2 = ((f32[32,40,128]{2,1,0:T(8,128)}), f32[32,40,128]{2,1,0:T(8,128)}, u32[]{:S(2)}, u32[]{:S(2)}) async-start(f32[32,40,128]{2,1,0:T(8,128)} %bitcast.190), calls=%async_computation.2 | async-start | bytes 1310720 | tf_op jit(solution)/shard_map/all_to_all | solution.py:102
  95.6 2.8 %multiply_select_fusion = f32[8,256,256]{1,2,0:T(8,128)S(1)} fusion(f32[8,256,256]{1,2,0:T(8,128)} %convolution_bitcast_fusion.2, f32[8,256,256]{1,2,0:T(8,128)} %copy-done.7, f32[8,256]{1,0:T(8,128)S(1)} %get-tuple-element.66, f32[8,256]{1,0:T(8,128)S(1)} %bitcast.200, pred[256,256]{0,1:T(8,128)(4,1)S(1)} %fusion.69), kind=kLoop, calls=%fused_computation.12 | loop fusion | flops 3145728 | bytes 6373376 | tf_op jit(solution)/shard_map/jit(_where)/select_n | solution.py:201
  98.7 2.2 %fusion.30 = (f32[8,160,256]{2,1,0:T(8,128)S(1)}, f32[8,160,256]{2,1,0:T(8,128)S(1)}) fusion(f32[2,8,160,256]{3,2,1,0:T(8,128)S(1)} %copy-done.3, f32[160]{0:T(256)S(1)} %copy-done.14, f32[160]{0:T(256)S(1)} %copy-done.15, f32[160]{0:T(256)S(1)} %copy-done.13, f32[8,256]{1,0:T(8,128)S(1)} %get-tuple-element.66, f32[8,160]{1,0:T(8,128)S(1)} %get-tuple-element.68, ...), kind=kOutput, calls=%fused_computation.54 | convolution fusion | flops 254803968 | bytes 6446976 | tf_op jit(solution)/shard_map/hfv,thv->hft/dot_general | solution.py:205
  100.9 0.7 fusion
  101.7 0.7 fusion.34
  102.3 0.5 fusion.36
  102.8 1.1 copy-done.8
  103.9 2.6 %convolution_bitcast_fusion.4 = f32[256,8,128]{0,2,1:T(8,128)} fusion(f32[8,256,256]{1,2,0:T(8,128)S(1)} %copy-done.8, pred[256,256]{0,1:T(8,128)(4,1)S(1)} %fusion.69, bf16[256,8,128]{0,2,1:T(8,128)(2,1)S(1)} %bitcast.189, f32[256,8]{0,1:T(8,128)S(1)} %bitcast_add_fusion), kind=kOutput, calls=%fused_computation.27 | convolution fusion | flops 406323200 | bytes 3743744 | tf_op jit(solution)/shard_map/hts,thv->shv/dot_general | solution.py:196
  106.5 7.9 %all-to-all-done.2 = f32[32,40,128]{2,1,0:T(8,128)} async-done(((f32[32,40,128]{2,1,0:T(8,128)}), f32[32,40,128]{2,1,0:T(8,128)}, u32[]{:S(2)}, u32[]{:S(2)}) %all-to-all-start.2) | async-done | bytes 655392 | tf_op jit(solution)/shard_map/all_to_all | solution.py:102
  114.4 1.5 fusion.52
  115.9 1.2 copy.124
  117.1 5.4 %all-to-all-start.3 = ((f32[32,40,128]{2,1,0:T(8,128)}), f32[32,40,128]{2,1,0:T(8,128)}, u32[]{:S(2)}, u32[]{:S(2)}) async-start(f32[32,40,128]{2,1,0:T(8,128)} %copy.124), calls=%async_computation.3 | async-start | bytes 1310720 | tf_op jit(solution)/shard_map/all_to_all | solution.py:105
  122.5 2.0 %copy.128 = bf16[256,1024]{1,0:T(8,128)(2,1)} copy(bf16[256,1024]{0,1:T(8,128)(2,1)} %bitcast.197) | data formatting | bytes 1048576
  124.5 0.7 copy.129
  125.3 15.9 %all-to-all-done.3 = f32[32,40,128]{2,1,0:T(8,128)} async-done(((f32[32,40,128]{2,1,0:T(8,128)}), f32[32,40,128]{2,1,0:T(8,128)}, u32[]{:S(2)}, u32[]{:S(2)}) %all-to-all-start.3) | async-done | bytes 655392 | tf_op jit(solution)/shard_map/all_to_all | solution.py:105
  141.2 0.8 slice_bitcast_fusion.4
  141.9 3.9 %fusion.13 = f32[256,8,128]{0,2,1:T(8,128)} fusion(f32[256,8,128]{0,2,1:T(8,128)} %convolution_bitcast_fusion.4, f32[8,160,128]{2,1,0:T(8,128)} %bitcast.50, f32[8,160,256]{2,1,0:T(8,128)} %get-tuple-element.57, f32[256]{0:T(256)S(1)} %get-tuple-element.52), kind=kOutput, calls=%fused_computation.26 | convolution fusion | flops 252182528 | bytes 4064256 | tf_op jit(solution)/shard_map/hfs,hfv->shv/dot_general | solution.py:212
  145.9 2.5 %copy.126 = f32[256,1024]{1,0:T(8,128)} copy(f32[256,1024]{0,1:T(8,128)} %bitcast.184) | data formatting | bytes 2097152 | tf_op jit(solution)/shard_map/reshape | solution.py:222
  148.4 2.7 %multiply_convert_fusion = (bf16[256,1024]{1,0:T(8,128)(2,1)}, f32[256,1024]{1,0:T(8,128)S(1)}) fusion(f32[256,1024]{1,0:T(8,128)} %copy.126, f32[256,1024]{1,0:T(8,128)} %get-tuple-element.24, bf16[256,1024]{1,0:T(8,128)(2,1)} %param.23), kind=kLoop, calls=%fused_computation.75 | loop fusion | flops 1835008 | bytes 4194304 | tf_op jit(solution)/shard_map/convert_element_type | solution.py:223
  151.2 1.0 copy-done.4
  152.2 2.0 %fusion.28 = (f32[8,160,256]{2,1,0:T(8,128)S(1)}, f32[8,160,256]{2,1,0:T(8,128)S(1)}) fusion(f32[2,8,160,256]{3,2,1,0:T(8,128)S(1)} %convolution_bitcast_fusion.1, f32[160]{0:T(256)S(1)} %copy-done.14, f32[160]{0:T(256)S(1)} %copy-done.15, f32[160]{0:T(256)S(1)} %copy-done.13, f32[8,160]{1,0:T(8,128)S(1)} %bitcast.207, f32[8,160,128]{2,1,0:T(8,128)} %bitcast.50, ...), kind=kOutput, calls=%fused_computation.52 | convolution fusion | flops 253952000 | bytes 6430592 | tf_op jit(solution)/shard_map/hfv,shv->hfs/dot_general | solution.py:216
  154.1 4.4 %collective-permute-start.1 = (f32[2,1024]{1,0:T(2,128)S(1)}, f32[2,1024]{1,0:T(2,128)S(1)}, u32[]{:S(2)}, u32[]{:S(2)}) collective-permute-start(f32[2,1024]{1,0:T(2,128)S(1)} %slice.124), channel_id=1, source_target_pairs={{8,0},{16,8},{24,16},{32,24},{40,32},{48,40},{56,48},{64,56},{72,6... | collective-permute-start | bytes 24584 | tf_op jit(solution)/shard_map/ppermute | solution.py:23
  158.5 0.7 fusion.40
  159.3 0.7 copy.130
  160.0 1.2 fusion.48
  (70 shorter events, 1.9 us)
Async XLA Ops:
  1.4 16.9 %collective-permute-start = (bf16[2,1024]{1,0:T(2,128)(2,1)S(1)}, bf16[2,1024]{1,0:T(2,128)(2,1)S(1)}, u32[]{:S(2)}, u32[]{:S(2)}) collective-permute-start(bf16[2,1024]{1,0:T(2,128)(2,1)S(1)} %slice.83), channel_id=1, source_target_pairs={{0,8},{8,16},{16,24},{24,32},{32,40},{40,48},{48,56},{56,64},{64,7... | collective-permute-start | bytes 12296 | tf_op jit(solution)/shard_map/ppermute | solution.py:23
  12.0 1.3 copy-start.12
  13.3 2.7 %copy-start.13 = (f32[160]{0:T(256)S(1)}, f32[160]{0:T(256)}, u32[]{:S(2)}) copy-start(f32[160]{0:T(256)} %constant.80.clone) | copy-start | bytes 1924
  13.3 2.7 %copy-start.14 = (f32[160]{0:T(256)S(1)}, f32[160]{0:T(256)}, u32[]{:S(2)}) copy-start(f32[160]{0:T(256)} %constant.79.clone) | copy-start | bytes 1924
  13.4 2.7 %copy-start.15 = (f32[160]{0:T(256)S(1)}, f32[160]{0:T(256)}, u32[]{:S(2)}) copy-start(f32[160]{0:T(256)} %constant.78.clone) | copy-start | bytes 1924
  13.9 4.1 %copy-start.2 = (f32[2,8,160,256]{3,2,1,0:T(8,128)}, f32[2,8,160,256]{3,2,1,0:T(8,128)S(1)}, u32[]{:S(2)}) copy-start(f32[2,8,160,256]{3,2,1,0:T(8,128)S(1)} %convolution_bitcast_fusion) | copy-start | bytes 7864324
  18.2 3.6 %copy-start = (f32[8,160,256]{2,1,0:T(8,128)S(1)}, f32[8,160,256]{2,1,0:T(8,128)}, u32[]{:S(2)}) copy-start(f32[8,160,256]{2,1,0:T(8,128)} %get-tuple-element.57) | copy-start | bytes 3932164
  22.4 0.9 copy-start.6
  23.3 30.7 %all-to-all-start = ((f32[32,40,128]{2,1,0:T(8,128)}), f32[32,40,128]{2,1,0:T(8,128)}, u32[]{:S(2)}, u32[]{:S(2)}) async-start(f32[32,40,128]{2,1,0:T(8,128)} %bitcast.185), calls=%async_computation | async-start | bytes 1310720 | tf_op jit(solution)/shard_map/all_to_all | solution.py:102
  37.0 1.3 copy-start.7
  56.7 24.4 %all-to-all-start.1 = ((f32[32,40,128]{2,1,0:T(8,128)}), f32[32,40,128]{2,1,0:T(8,128)}, u32[]{:S(2)}, u32[]{:S(2)}) async-start(f32[32,40,128]{2,1,0:T(8,128)} %copy.113), calls=%async_computation.1 | async-start | bytes 1310720 | tf_op jit(solution)/shard_map/all_to_all | solution.py:105
  81.0 2.6 %copy-start.1 = (f32[8,160,256]{2,1,0:T(8,128)S(1)}, f32[8,160,256]{2,1,0:T(8,128)}, u32[]{:S(2)}) copy-start(f32[8,160,256]{2,1,0:T(8,128)} %get-tuple-element.75) | copy-start | bytes 3932164
  83.7 3.6 %copy-start.9 = (bf16[256,1024]{0,1:T(8,128)(2,1)S(1)}, bf16[256,1024]{0,1:T(8,128)(2,1)}, u32[]{:S(2)}) copy-start(bf16[256,1024]{0,1:T(8,128)(2,1)} %copy.114) | copy-start | bytes 1572868
  90.1 24.3 %all-to-all-start.2 = ((f32[32,40,128]{2,1,0:T(8,128)}), f32[32,40,128]{2,1,0:T(8,128)}, u32[]{:S(2)}, u32[]{:S(2)}) async-start(f32[32,40,128]{2,1,0:T(8,128)} %bitcast.190), calls=%async_computation.2 | async-start | bytes 1310720 | tf_op jit(solution)/shard_map/all_to_all | solution.py:102
  95.6 3.0 %copy-start.3 = (f32[2,8,160,256]{3,2,1,0:T(8,128)S(1)}, f32[2,8,160,256]{3,2,1,0:T(8,128)}, u32[]{:S(2)}) copy-start(f32[2,8,160,256]{3,2,1,0:T(8,128)} %copy-done.2) | copy-start | bytes 7864324
  95.6 3.1 %copy-start.10 = (bf16[256,1024]{0,1:T(8,128)(2,1)S(1)}, bf16[256,1024]{0,1:T(8,128)(2,1)}, u32[]{:S(2)}) copy-start(bf16[256,1024]{0,1:T(8,128)(2,1)} %copy.114) | copy-start | bytes 1572868
  98.7 2.2 %copy-start.11 = (f32[320,16,1]{0,1,2:T(8,128)S(1)}, f32[320,16,1]{0,1,2:T(8,128)}, u32[]{:S(2)}) copy-start(f32[320,16,1]{0,1,2:T(8,128)} %constant.87) | copy-start | bytes 61444
  102.3 1.6 copy-start.8
  117.1 24.1 %all-to-all-start.3 = ((f32[32,40,128]{2,1,0:T(8,128)}), f32[32,40,128]{2,1,0:T(8,128)}, u32[]{:S(2)}, u32[]{:S(2)}) async-start(f32[32,40,128]{2,1,0:T(8,128)} %copy.124), calls=%async_computation.3 | async-start | bytes 1310720 | tf_op jit(solution)/shard_map/all_to_all | solution.py:105
  151.2 1.0 copy-start.4
  154.1 5.9 %collective-permute-start.1 = (f32[2,1024]{1,0:T(2,128)S(1)}, f32[2,1024]{1,0:T(2,128)S(1)}, u32[]{:S(2)}, u32[]{:S(2)}) collective-permute-start(f32[2,1024]{1,0:T(2,128)S(1)} %slice.124), channel_id=1, source_target_pairs={{8,0},{16,8},{24,16},{32,24},{40,32},{48,40},{56,48},{64,56},{72,6... | collective-permute-start | bytes 24584 | tf_op jit(solution)/shard_map/ppermute | solution.py:23
  158.5 1.5 copy-start.5

commit v8 on v7

--- a/solution.py
+++ b/solution.py
@@ -166,15 +166,9 @@
     local_norm = jnp.sum(masked_key, axis=2)
     restart_all, closes_all = block_flags(doc_lengths, lax.axis_size("ctx"), tok_rows)
     forward_mask, backward_mask = scan_masks(restart_all, closes_all)
-    upstream_values = jnp.einsum(
-        "thv,shv->hts",
-        d_out.reshape(tok_rows, HEADS, VD),
-        value_rows.reshape(tok_rows, HEADS, VD),
-        preferred_element_type=jnp.float32,
-    )
     gate_slope = convolved * opening * (1.0 - opening)
-    state_in, norm_in, (numerator, denominator), (upstream_values, gate_slope) = state_scan(
-        local_state, local_norm, forward_mask, (numerator, denominator), (upstream_values, gate_slope)
+    state_in, norm_in, (numerator, denominator), gate_slope = state_scan(
+        local_state, local_norm, forward_mask, (numerator, denominator), gate_slope
     )
     inside = (doc_ids == prev_doc).astype(jnp.float32)
     numerator = numerator + inside[:, None, None] * jnp.einsum(
@@ -195,7 +189,7 @@
     outside = (doc_ids == next_doc).astype(jnp.float32)
     grad_v = jnp.einsum("hts,thv->shv", weights, grad_num, precision=high)
     grad_weights = (
-        upstream_values / jnp.transpose(denominator, (1, 0))[:, :, None]
+        jnp.einsum("thv,shv->hts", grad_num, v_float, precision=high)
         + jnp.transpose(grad_den, (1, 0))[:, :, None]
     )
     grad_scores = jnp.where(allowed[None], grad_weights * (1.0 + scores), 0.0)

time: 164 us -> 163 us (level)
  waiting for transfers between devices: 49.7 us -> 53.3 us
  other arithmetic: 17.7 us -> 14.9 us
  matrix products: 31.8 us -> 29.9 us
    select_n x1 -> x0, other arithmetic: 2.81 us -> none  [local(): grad_scores = jnp.where(allowed[None], grad_weights * (1.0 + scores), 0.0)]
    unnamed x42 -> x47, local copies, waits for them, and re-layouts: 13.7 us -> 10.9 us
    all_to_all x2, waiting for transfers between devices: 28.2 us -> 30.7 us  [state_scan(): back = lax.all_to_all(summed, 'ctx', 0, 0, tiled=True)]
    reshape x0 -> x1, local copies, waits for them, and re-layouts: none -> 2.32 us  [local(): upstream = d_out.astype(jnp.float32).reshape(tok_rows, HEADS, VD)]
    dot_general x1, matrix products: 2.83 us -> 1.11 us  [local(): jnp.einsum('thv,shv->hts', grad_num, v_float, precision=high)]
  transfers between devices with their start and end apart: 6 -> 6, of which waited for: 4 -> 4; matrix products, arithmetic and copies ran while one was open for 24% -> 22% of each run, Pallas kernels for 0% -> 0%
where the time goes in v8:
time: 163 us; the launch traced here: 160 us
  waiting for transfers between devices  53.3 us (33%)
  starting transfers between devices  35.2 us (22%)
  matrix products  29.9 us (18%)
  local copies, waits for them, and re-layouts  25.3 us (16%)
  other arithmetic  14.9 us (9%)
    all_to_all x2, waiting for transfers between devices, state_scan(): back = lax.all_to_all(summed, 'ctx', 0, 0, tiled=True)  30.7 us
    all_to_all x2, waiting for transfers between devices, state_scan(): chunks = lax.all_to_all(packed, 'ctx', 0, 0, tiled=True)  22.6 us
    all_to_all x2, starting transfers between devices, state_scan(): chunks = lax.all_to_all(packed, 'ctx', 0, 0, tiled=True)  16.6 us
    unnamed x47, local copies, waits for them, and re-layouts  10.9 us
    all_to_all x2, starting transfers between devices, state_scan(): back = lax.all_to_all(summed, 'ctx', 0, 0, tiled=True)  10.8 us
    ppermute x2, starting transfers between devices, shifted(): return lax.ppermute(block, axis, route)  7.86 us
    dot_general x1, matrix products, local(): jnp.einsum('hft,hfv->thv', phi_query, state_in, precision=high)  3.69 us
    dot_general x1, matrix products, local(): jnp.einsum('hfs,hfv->shv', phi_key, grad_state_in, precision=high)  3.66 us
  transfers between devices with their start and end apart: 6, of which 4 were waited for; matrix products, arithmetic and copies ran while one was open for 22% of the time, Pallas kernels for 0%

profile of v8, /device:TPU:32, one launch (start us, length us, event | category | flops | bytes accessed | tf_op | source)
XLA Modules:
  0.0 159.7 jit_solution(5296357250364398543)
XLA Ops:
  0.6 0.7 slice.83
  1.4 3.5 %collective-permute-start = (bf16[2,1024]{1,0:T(2,128)(2,1)S(1)}, bf16[2,1024]{1,0:T(2,128)(2,1)S(1)}, u32[]{:S(2)}, u32[]{:S(2)}) collective-permute-start(bf16[2,1024]{1,0:T(2,128)(2,1)S(1)} %slice.83), channel_id=1, source_target_pairs={{0,8},{8,16},{16,24},{24,32},{32,40},{40,48},{48,56},{56,64},{64,7... | collective-permute-start | bytes 12296 | tf_op jit(solution)/shard_map/ppermute | solution.py:23
  4.9 0.7 broadcast_add_fusion.3
  5.6 0.8 fusion.103
  6.4 0.7 copy.109
  7.6 0.7 compare_select_fusion
  8.3 0.6 fusion.105
  8.9 0.6 compare_convert_fusion.4
  9.5 0.6 fusion.104
  10.1 0.9 copy.111
  11.1 0.9 copy.108
  12.0 1.3 convolution_bitcast_fusion.1
  13.4 0.5 convolution_bitcast_fusion
  14.0 2.1 %compare_convert_fusion.1 = (f32[256]{0:T(256)S(1)}, f32[256]{0:T(256)S(1)}, f32[256]{0:T(256)S(1)}, f32[256]{0:T(256)S(1)}, f32[256]{0:T(256)S(1)}, /*index=5*/f32[256]{0:T(256)S(1)}, f32[256]{0:T(256)S(1)}) fusion(s32[256]{0:T(256)S(1)} %get-tuple-element.51, s32[258]{0:T(512)S(1)} %get-tuple-element.81, s32[]{:T(128)} %bitcast.32, s32[]{:T(128)} %bitcast.16, ...), kind=kLoop, calls=%fused_computation.136 | loop fusion | flops 3584 | bytes 12300 | tf_op jit(solution)/shard_map/convert_element_type | solution.py:224
  16.1 1.9 %multiply_reduce_fusion = (f32[8,160]{1,0:T(8,128)S(1)}, f32[8,160,256]{2,1,0:T(8,128)}, f32[8,160,256]{2,1,0:T(8,128)}) fusion(f32[256]{0:T(256)S(1)} %get-tuple-element.80, f32[160]{0:T(256)S(1)} %copy-done.15, f32[2,8,160,256]{3,2,1,0:T(8,128)S(1)} %convolution_bitcast_fusion.1, f32[160]{0:T(256)S(1)} %copy-done.16, f32[160]{0:T(256)S(1)} %copy-done.14, ...), kind=kLoop, calls=%fused_computation.45 | loop fusion | flops 3275520 | bytes 7872384 | tf_op jit(solution)/shard_map/reduce_sum | solution.py:166
  18.2 3.6 %subtract_multiply_fusion = (f32[256,1024]{1,0:T(8,128)}, bf16[256,1024]{1,0:T(8,128)(2,1)S(1)}) fusion(bf16[256,1024]{1,0:T(8,128)(2,1)} %param.23, f32[256]{0:T(256)S(1)} %get-tuple-element.78, bf16[256,1024]{1,0:T(8,128)(2,1)} %param.22, bf16[2,1024]{1,0:T(2,128)(2,1)S(1)} %collective-permute-done, f32[1024]{0:T(1024)S(1)} %bitcast.203, ...), kind=kLoop, calls=%fused_computation.73 | loop fusion | flops 6291456 | bytes 2639872 | tf_op jit(solution)/shard_map/mul | solution.py:169
  21.8 0.5 fusion.25
  22.4 0.9 copy-done.7
  23.3 11.1 %all-to-all-start = ((f32[32,40,128]{2,1,0:T(8,128)}), f32[32,40,128]{2,1,0:T(8,128)}, u32[]{:S(2)}, u32[]{:S(2)}) async-start(f32[32,40,128]{2,1,0:T(8,128)} %bitcast.184), calls=%async_computation | async-start | bytes 1310720 | tf_op jit(solution)/shard_map/all_to_all | solution.py:102
  34.7 0.7 gather_fusion.1
  35.4 0.7 gather_fusion
  36.2 0.8 fusion.58
  37.0 1.3 copy-done.17
  38.3 2.0 %convolution_bitcast_fusion.2 = f32[256,8,128]{0,2,1:T(8,128)} fusion(f32[8,256,256]{1,2,0:T(8,128)S(1)} %get-tuple-element.88, pred[256,256]{0,1:T(8,128)(4,1)S(1)} %fusion.68, bf16[256,1024]{1,0:T(8,128)(2,1)S(1)} %get-tuple-element.53), kind=kOutput, calls=%fused_computation.22 | convolution fusion | flops 405798912 | bytes 3735552 | tf_op jit(solution)/shard_map/hts,shv->thv/dot_general | solution.py:159
  40.3 13.6 %all-to-all-done = f32[32,40,128]{2,1,0:T(8,128)} async-done(((f32[32,40,128]{2,1,0:T(8,128)}), f32[32,40,128]{2,1,0:T(8,128)}, u32[]{:S(2)}, u32[]{:S(2)}) %all-to-all-start) | async-done | bytes 655392 | tf_op jit(solution)/shard_map/all_to_all | solution.py:102
  53.9 1.5 fusion.53
  55.4 1.2 copy.116
  56.6 5.5 %all-to-all-start.1 = ((f32[32,40,128]{2,1,0:T(8,128)}), f32[32,40,128]{2,1,0:T(8,128)}, u32[]{:S(2)}, u32[]{:S(2)}) async-start(f32[32,40,128]{2,1,0:T(8,128)} %copy.116), calls=%async_computation.1 | async-start | bytes 1310720 | tf_op jit(solution)/shard_map/all_to_all | solution.py:105
  62.4 0.7 gather_fusion.3
  63.1 0.7 gather_fusion.2
  63.8 2.3 %copy.117 = f32[256,1024]{0,1:T(8,128)} copy(bf16[256,1024]{1,0:T(8,128)(2,1)} %param.26) | data formatting | bytes 1572864 | tf_op jit(solution)/shard_map/reshape | solution.py:182
  66.1 14.9 %all-to-all-done.1 = f32[32,40,128]{2,1,0:T(8,128)} async-done(((f32[32,40,128]{2,1,0:T(8,128)}), f32[32,40,128]{2,1,0:T(8,128)}, u32[]{:S(2)}, u32[]{:S(2)}) %all-to-all-start.1) | async-done | bytes 655392 | tf_op jit(solution)/shard_map/all_to_all | solution.py:105
  81.0 0.9 slice_bitcast_fusion.5
  81.9 1.7 %fusion.76 = f32[8,1,256]{2,1,0:T(1,128)S(1)} fusion(f32[8,160,256]{2,1,0:T(8,128)} %get-tuple-element.73, f32[8,160,1]{1,0,2:T(8,128)S(1)} %get-tuple-element.67), kind=kOutput, calls=%fused_computation.121 | convolution fusion | flops 1966080 | bytes 1324032 | tf_op jit(solution)/shard_map/hft,hf->th/dot_general | solution.py:177
  83.6 3.7 %multiply_reduce_fusion.1 = (f32[256,8]{0,1:T(8,128)S(1)}, bf16[256,8,128]{0,2,1:T(8,128)(2,1)}) fusion(f32[256,1024]{0,1:T(8,128)} %copy.117, f32[256,8]{0,1:T(8,128)S(1)} %bitcast_add_fusion, f32[256,8,128]{0,2,1:T(8,128)} %convolution_bitcast_fusion.2, f32[8,160,128]{2,1,0:T(8,128)} %bitcast.21, f32[8,160,256]{2,1,0:T(8,128)S(1)} %copy-done.1, ...), kind=kOutput, calls=%fused_computation.72 | convolution fusion | flops 253229056 | bytes 4604928 | tf_op jit(solution)/shard_map/hft,hfv->thv/dot_general | solution.py:174
  87.3 0.6 fusion.21
  87.9 0.6 copy-done.8
  88.5 1.6 fusion.23
  90.1 0.6 constant_dynamic-update-slice_fusion
  90.7 5.5 %all-to-all-start.2 = ((f32[32,40,128]{2,1,0:T(8,128)}), f32[32,40,128]{2,1,0:T(8,128)}, u32[]{:S(2)}, u32[]{:S(2)}) async-start(f32[32,40,128]{2,1,0:T(8,128)} %bitcast.189), calls=%async_computation.2 | async-start | bytes 1310720 | tf_op jit(solution)/shard_map/all_to_all | solution.py:102
  96.2 3.4 %fusion.30 = (f32[8,160,256]{2,1,0:T(8,128)S(1)}, f32[8,160,256]{2,1,0:T(8,128)S(1)}) fusion(f32[2,8,160,256]{3,2,1,0:T(8,128)} %copy-done.2, f32[160]{0:T(256)S(1)} %copy-done.15, f32[160]{0:T(256)S(1)} %copy-done.16, f32[160]{0:T(256)S(1)} %copy-done.14, f32[8,256]{1,0:T(8,128)S(1)} %get-tuple-element.64, f32[8,160]{1,0:T(8,128)S(1)} %get-tuple-element.66, ...), kind=kOutput, calls=%fused_computation.51 | convolution fusion | flops 254541824 | bytes 6971264 | tf_op jit(solution)/shard_map/hfv,thv->hft/dot_general | solution.py:199
  99.7 0.7 fusion
  100.5 0.4 copy-done.9
  100.9 1.1 multiply_select_fusion
  102.0 0.7 fusion.34
  102.7 0.5 fusion.36
  103.2 0.4 copy-done.13
  103.6 2.5 %convolution_bitcast_fusion.3 = f32[256,8,128]{0,2,1:T(8,128)} fusion(f32[8,256,256]{1,2,0:T(8,128)S(1)} %copy-done.18, pred[256,256]{0,1:T(8,128)(4,1)S(1)} %copy-done.13, f32[256,8,128]{0,2,1:T(8,128)S(1)} %bitcast.188, f32[256,8]{0,1:T(8,128)S(1)} %bitcast_add_fusion), kind=kOutput, calls=%fused_computation.26 | convolution fusion | flops 406061056 | bytes 4268032 | tf_op jit(solution)/shard_map/hts,thv->shv/dot_general | solution.py:190
  106.0 9.0 %all-to-all-done.2 = f32[32,40,128]{2,1,0:T(8,128)} async-done(((f32[32,40,128]{2,1,0:T(8,128)}), f32[32,40,128]{2,1,0:T(8,128)}, u32[]{:S(2)}, u32[]{:S(2)}) %all-to-all-start.2) | async-done | bytes 655392 | tf_op jit(solution)/shard_map/all_to_all | solution.py:102
  115.0 1.5 fusion.51
  116.5 1.2 copy.128
  117.7 5.3 %all-to-all-start.3 = ((f32[32,40,128]{2,1,0:T(8,128)}), f32[32,40,128]{2,1,0:T(8,128)S(1)}, u32[]{:S(2)}, u32[]{:S(2)}) async-start(f32[32,40,128]{2,1,0:T(8,128)} %copy.128), calls=%async_computation.3 | async-start | bytes 1310720 | tf_op jit(solution)/shard_map/all_to_all | solution.py:105
  123.1 2.0 %copy.132 = bf16[256,1024]{1,0:T(8,128)(2,1)} copy(bf16[256,1024]{0,1:T(8,128)(2,1)} %bitcast.196) | data formatting | bytes 1048576
  125.1 0.7 copy.133
  125.8 15.8 %all-to-all-done.3 = f32[32,40,128]{2,1,0:T(8,128)S(1)} async-done(((f32[32,40,128]{2,1,0:T(8,128)}), f32[32,40,128]{2,1,0:T(8,128)S(1)}, u32[]{:S(2)}, u32[]{:S(2)}) %all-to-all-start.3) | async-done | bytes 655392 | tf_op jit(solution)/shard_map/all_to_all | solution.py:105
  141.7 3.7 %fusion.13 = f32[256,8,128]{0,2,1:T(8,128)} fusion(f32[256,8,128]{0,2,1:T(8,128)} %convolution_bitcast_fusion.3, f32[8,160,128]{2,1,0:T(8,128)S(1)} %bitcast.181, f32[8,160,256]{2,1,0:T(8,128)} %get-tuple-element.55, f32[256]{0:T(256)S(1)} %get-tuple-element.50), kind=kOutput, calls=%fused_computation.25 | convolution fusion | flops 252182528 | bytes 4064256 | tf_op jit(solution)/shard_map/hfs,hfv->shv/dot_general | solution.py:206
  145.3 2.5 %copy.130 = f32[256,1024]{1,0:T(8,128)} copy(f32[256,1024]{0,1:T(8,128)} %bitcast.183) | data formatting | bytes 2097152 | tf_op jit(solution)/shard_map/reshape | solution.py:216
  147.9 2.8 %multiply_convert_fusion = (bf16[256,1024]{1,0:T(8,128)(2,1)}, f32[256,1024]{1,0:T(8,128)S(1)}) fusion(f32[256,1024]{1,0:T(8,128)} %copy.130, f32[256,1024]{1,0:T(8,128)} %get-tuple-element.22, bf16[256,1024]{1,0:T(8,128)(2,1)} %param.23), kind=kLoop, calls=%fused_computation.71 | loop fusion | flops 1835008 | bytes 4194304 | tf_op jit(solution)/shard_map/convert_element_type | solution.py:217
  150.7 1.0 copy-done.5
  151.7 0.9 fusion.28
  152.6 4.4 %collective-permute-start.1 = (f32[2,1024]{1,0:T(2,128)S(1)}, f32[2,1024]{1,0:T(2,128)S(1)}, u32[]{:S(2)}, u32[]{:S(2)}) collective-permute-start(f32[2,1024]{1,0:T(2,128)S(1)} %slice.124), channel_id=1, source_target_pairs={{8,0},{16,8},{24,16},{32,24},{40,32},{48,40},{56,48},{64,56},{72,6... | collective-permute-start | bytes 24584 | tf_op jit(solution)/shard_map/ppermute | solution.py:23
  157.0 0.7 fusion.40
  157.7 0.7 copy.134
  158.5 1.2 fusion.48
  (75 shorter events, 1.7 us)
Async XLA Ops:
  1.4 16.9 %collective-permute-start = (bf16[2,1024]{1,0:T(2,128)(2,1)S(1)}, bf16[2,1024]{1,0:T(2,128)(2,1)S(1)}, u32[]{:S(2)}, u32[]{:S(2)}) collective-permute-start(bf16[2,1024]{1,0:T(2,128)(2,1)S(1)} %slice.83), channel_id=1, source_target_pairs={{0,8},{8,16},{16,24},{24,32},{32,40},{40,48},{48,56},{56,64},{64,7... | collective-permute-start | bytes 12296 | tf_op jit(solution)/shard_map/ppermute | solution.py:23
  12.0 1.3 copy-start.11
  13.3 2.7 %copy-start.14 = (f32[160]{0:T(256)S(1)}, f32[160]{0:T(256)}, u32[]{:S(2)}) copy-start(f32[160]{0:T(256)} %constant.80.clone) | copy-start | bytes 1924
  13.3 2.7 %copy-start.15 = (f32[160]{0:T(256)S(1)}, f32[160]{0:T(256)}, u32[]{:S(2)}) copy-start(f32[160]{0:T(256)} %constant.79.clone) | copy-start | bytes 1924
  13.4 2.7 %copy-start.16 = (f32[160]{0:T(256)S(1)}, f32[160]{0:T(256)}, u32[]{:S(2)}) copy-start(f32[160]{0:T(256)} %constant.78.clone) | copy-start | bytes 1924
  13.9 4.1 %copy-start.2 = (f32[2,8,160,256]{3,2,1,0:T(8,128)}, f32[2,8,160,256]{3,2,1,0:T(8,128)S(1)}, u32[]{:S(2)}) copy-start(f32[2,8,160,256]{3,2,1,0:T(8,128)S(1)} %convolution_bitcast_fusion) | copy-start | bytes 7864324
  18.2 3.6 %copy-start = (f32[8,160,256]{2,1,0:T(8,128)S(1)}, f32[8,160,256]{2,1,0:T(8,128)}, u32[]{:S(2)}) copy-start(f32[8,160,256]{2,1,0:T(8,128)} %get-tuple-element.55) | copy-start | bytes 3932164
  21.8 78.6 %copy-start.3 = (bf16[256,1024]{1,0:T(8,128)(2,1)}, bf16[256,1024]{1,0:T(8,128)(2,1)S(1)}, u32[]{:S(2)}) copy-start(bf16[256,1024]{1,0:T(8,128)(2,1)S(1)} %get-tuple-element.53) | copy-start | bytes 1572868
  22.4 0.9 copy-start.7
  23.3 30.7 %all-to-all-start = ((f32[32,40,128]{2,1,0:T(8,128)}), f32[32,40,128]{2,1,0:T(8,128)}, u32[]{:S(2)}, u32[]{:S(2)}) async-start(f32[32,40,128]{2,1,0:T(8,128)} %bitcast.184), calls=%async_computation | async-start | bytes 1310720 | tf_op jit(solution)/shard_map/all_to_all | solution.py:102
  36.2 64.2 %copy-start.12 = (pred[256,256]{0,1:T(8,128)(4,1)}, pred[256,256]{0,1:T(8,128)(4,1)S(1)}, u32[]{:S(2)}) copy-start(pred[256,256]{0,1:T(8,128)(4,1)S(1)} %fusion.68) | copy-start | bytes 196612
  37.0 1.3 copy-start.17
  56.6 24.4 %all-to-all-start.1 = ((f32[32,40,128]{2,1,0:T(8,128)}), f32[32,40,128]{2,1,0:T(8,128)}, u32[]{:S(2)}, u32[]{:S(2)}) async-start(f32[32,40,128]{2,1,0:T(8,128)} %copy.116), calls=%async_computation.1 | async-start | bytes 1310720 | tf_op jit(solution)/shard_map/all_to_all | solution.py:105
  81.0 2.6 %copy-start.1 = (f32[8,160,256]{2,1,0:T(8,128)S(1)}, f32[8,160,256]{2,1,0:T(8,128)}, u32[]{:S(2)}) copy-start(f32[8,160,256]{2,1,0:T(8,128)} %get-tuple-element.73) | copy-start | bytes 3932164
  87.3 1.2 copy-start.8
  90.7 24.3 %all-to-all-start.2 = ((f32[32,40,128]{2,1,0:T(8,128)}), f32[32,40,128]{2,1,0:T(8,128)}, u32[]{:S(2)}, u32[]{:S(2)}) async-start(f32[32,40,128]{2,1,0:T(8,128)} %bitcast.189), calls=%async_computation.2 | async-start | bytes 1310720 | tf_op jit(solution)/shard_map/all_to_all | solution.py:102
  96.2 3.5 %copy-start.10 = (f32[320,16,1]{0,1,2:T(8,128)S(1)}, f32[320,16,1]{0,1,2:T(8,128)}, u32[]{:S(2)}) copy-start(f32[320,16,1]{0,1,2:T(8,128)} %constant.87) | copy-start | bytes 61444
  96.2 4.2 %copy-start.18 = (f32[8,256,256]{1,2,0:T(8,128)S(1)}, f32[8,256,256]{1,2,0:T(8,128)}, u32[]{:S(2)}) copy-start(f32[8,256,256]{1,2,0:T(8,128)} %copy-done.17) | copy-start | bytes 6291460
  99.7 1.2 copy-start.9
  102.7 0.8 copy-start.13
  117.7 24.0 %all-to-all-start.3 = ((f32[32,40,128]{2,1,0:T(8,128)}), f32[32,40,128]{2,1,0:T(8,128)S(1)}, u32[]{:S(2)}, u32[]{:S(2)}) async-start(f32[32,40,128]{2,1,0:T(8,128)} %copy.128), calls=%async_computation.3 | async-start | bytes 1310720 | tf_op jit(solution)/shard_map/all_to_all | solution.py:105
  147.9 3.8 %copy-start.4 = (bf16[256,1024]{1,0:T(8,128)(2,1)S(1)}, bf16[256,1024]{1,0:T(8,128)(2,1)}, u32[]{:S(2)}) copy-start(bf16[256,1024]{1,0:T(8,128)(2,1)} %copy-done.3) | copy-start | bytes 1572868
  150.7 1.0 copy-start.5
  152.6 5.9 %collective-permute-start.1 = (f32[2,1024]{1,0:T(2,128)S(1)}, f32[2,1024]{1,0:T(2,128)S(1)}, u32[]{:S(2)}, u32[]{:S(2)}) collective-permute-start(f32[2,1024]{1,0:T(2,128)S(1)} %slice.124), channel_id=1, source_target_pairs={{8,0},{16,8},{24,16},{32,24},{40,32},{48,40},{56,48},{64,56},{72,6... | collective-permute-start | bytes 24584 | tf_op jit(solution)/shard_map/ppermute | solution.py:23
  157.0 1.5 copy-start.6

commit v9 on v4

--- a/solution.py
+++ b/solution.py
@@ -164,9 +164,7 @@
     local_norm = jnp.sum(masked_key, axis=2)
     restart_all, closes_all = block_flags(doc_lengths, lax.axis_size("ctx"), tok_rows)
     forward_mask, backward_mask = scan_masks(restart_all, closes_all)
-    state_in, norm_in, (numerator, denominator) = state_scan(
-        local_state, local_norm, forward_mask, (numerator, denominator)
-    )
+    state_in, norm_in, _ = state_scan(local_state, local_norm, forward_mask, ())
     inside = (doc_ids == prev_doc).astype(jnp.float32)
     numerator = numerator + inside[:, None, None] * jnp.einsum(
         "hft,hfv->thv", phi_query, state_in, precision=high

time: 161 us -> 160 us (level)
    all_to_all x2, waiting for transfers between devices: 29.8 us -> 25.5 us  [state_scan(): lax.all_to_all(summed, 'ctx', 0, 0, tiled=True).reshape(heads, feats, width)]
    all_to_all x2, waiting for transfers between devices: 22.4 us -> 26.5 us  [state_scan(): chunks = lax.all_to_all(packed, 'ctx', 0, 0, tiled=True)]
    unnamed x53 -> x55, local copies, waits for them, and re-layouts: 9.89 us -> 9.89 us
where the time goes in v9:
time: 160 us; the launch traced here: 157 us
  waiting for transfers between devices  52 us (32%)
  starting transfers between devices  35.3 us (22%)
  matrix products  31.2 us (20%)
  local copies, waits for them, and re-layouts  24.5 us (15%)
  other arithmetic  13.2 us (8%)
    all_to_all x2, waiting for transfers between devices, state_scan(): chunks = lax.all_to_all(packed, 'ctx', 0, 0, tiled=True)  26.5 us
    all_to_all x2, waiting for transfers between devices, state_scan(): lax.all_to_all(summed, 'ctx', 0, 0, tiled=True).reshape(heads, feats, width)  25.5 us
    all_to_all x2, starting transfers between devices, state_scan(): chunks = lax.all_to_all(packed, 'ctx', 0, 0, tiled=True)  16.6 us
    all_to_all x2, starting transfers between devices, state_scan(): lax.all_to_all(summed, 'ctx', 0, 0, tiled=True).reshape(heads, feats, width)  10.8 us
    unnamed x55, local copies, waits for them, and re-layouts  9.89 us
    ppermute x2, starting transfers between devices, shifted(): return lax.ppermute(block, axis, route)  7.86 us
    dot_general x1, matrix products, local(): jnp.einsum('hft,hfv->thv', phi_query, state_in, precision=high)  3.69 us
    dot_general x1, matrix products, local(): jnp.einsum('hfs,hfv->shv', phi_key, grad_state_in, precision=high)  3.68 us
  transfers between devices with their start and end apart: 6, of which 4 were waited for; matrix products, arithmetic and copies ran while one was open for 23% of the time, Pallas kernels for 0%

profile of v9, /device:TPU:32, one launch (start us, length us, event | category | flops | bytes accessed | tf_op | source)
XLA Modules:
  0.0 157.3 jit_solution(2574219578787856968)
XLA Ops:
  0.6 0.7 slice.80
  1.4 3.5 %collective-permute-start = (bf16[2,1024]{1,0:T(2,128)(2,1)S(1)}, bf16[2,1024]{1,0:T(2,128)(2,1)S(1)}, u32[]{:S(2)}, u32[]{:S(2)}) collective-permute-start(bf16[2,1024]{1,0:T(2,128)(2,1)S(1)} %slice.80), channel_id=1, source_target_pairs={{0,8},{8,16},{16,24},{24,32},{32,40},{40,48},{48,56},{56,64},{64,7... | collective-permute-start | bytes 12296 | tf_op jit(solution)/shard_map/ppermute | solution.py:23
  4.9 0.7 broadcast_add_fusion.3
  5.5 0.7 copy.108
  6.5 0.2 fusion.90
  6.8 0.7 compare_select_fusion
  7.4 0.6 fusion.107
  8.0 0.6 compare_convert_fusion.4
  8.7 0.6 fusion.106
  9.2 0.9 copy.109
  10.2 0.9 copy.110
  11.2 1.3 convolution_bitcast_fusion.1
  12.5 0.5 convolution_bitcast_fusion
  13.1 2.7 %compare_convert_fusion.1 = (f32[256]{0:T(256)S(1)}, f32[256]{0:T(256)}, f32[256]{0:T(256)S(1)}, f32[256]{0:T(256)S(1)}, f32[256]{0:T(256)S(1)}, /*index=5*/f32[256]{0:T(256)S(1)}, f32[256]{0:T(256)S(1)}) fusion(s32[256]{0:T(256)S(1)} %get-tuple-element.41, s32[258]{0:T(512)S(1)} %get-tuple-element.67, s32[]{:T(128)} %bitcast.30, s32[]{:T(128)} %bitcast.17, ...), kind=kLoop, calls=%fused_computation.138 | loop fusion | flops 3584 | bytes 12300 | tf_op jit(solution)/shard_map/convert_element_type | solution.py:219
  15.8 1.9 %multiply_reduce_fusion = (f32[8,160]{1,0:T(8,128)S(1)}, f32[8,160,256]{2,1,0:T(8,128)}, f32[8,160,256]{2,1,0:T(8,128)}) fusion(f32[256]{0:T(256)S(1)} %get-tuple-element.63, f32[160]{0:T(256)S(1)} %copy-done.16, f32[2,8,160,256]{3,2,1,0:T(8,128)S(1)} %convolution_bitcast_fusion.1, f32[160]{0:T(256)S(1)} %copy-done.17, f32[160]{0:T(256)S(1)} %copy-done.15, ...), kind=kLoop, calls=%fused_computation.44 | loop fusion | flops 3275520 | bytes 7872384 | tf_op jit(solution)/shard_map/reduce_sum | solution.py:164
  17.7 2.5 %fusion.61 = bf16[32,8,8,128]{3,2,1,0:T(8,128)(2,1)S(1)} fusion(bf16[256,1024]{1,0:T(8,128)(2,1)} %param.23, f32[256]{0:T(256)S(1)} %get-tuple-element.65, bf16[256,1024]{1,0:T(8,128)(2,1)} %param.22, bf16[2,1024]{1,0:T(2,128)(2,1)S(1)} %collective-permute-done, f32[1024]{0:T(1024)S(1)} %bitcast.191, f32[256]{0:T(256)S(1)} %get-tuple-element.66, ...), kind=kLoop, calls=%fused_computation.87 | loop fusion | flops 5767168 | bytes 1591296
  20.2 0.5 fusion.25
  20.8 0.8 copy-done.5
  21.6 11.1 %all-to-all-start = ((f32[32,40,128]{2,1,0:T(8,128)}), f32[32,40,128]{2,1,0:T(8,128)}, u32[]{:S(2)}, u32[]{:S(2)}) async-start(f32[32,40,128]{2,1,0:T(8,128)} %bitcast.170), calls=%async_computation | async-start | bytes 1310720 | tf_op jit(solution)/shard_map/all_to_all | solution.py:102
  32.8 0.2 convert_reduce_fusion.2
  33.3 0.7 gather_fusion.1
  34.0 0.7 gather_fusion
  34.7 17.6 %all-to-all-done = f32[32,40,128]{2,1,0:T(8,128)} async-done(((f32[32,40,128]{2,1,0:T(8,128)}), f32[32,40,128]{2,1,0:T(8,128)}, u32[]{:S(2)}, u32[]{:S(2)}) %all-to-all-start) | async-done | bytes 655392 | tf_op jit(solution)/shard_map/all_to_all | solution.py:102
  52.3 1.5 fusion.53
  53.8 1.2 copy.116
  55.0 5.5 %all-to-all-start.1 = ((f32[32,40,128]{2,1,0:T(8,128)}), f32[32,40,128]{2,1,0:T(8,128)}, u32[]{:S(2)}, u32[]{:S(2)}) async-start(f32[32,40,128]{2,1,0:T(8,128)} %copy.116), calls=%async_computation.1 | async-start | bytes 1310720 | tf_op jit(solution)/shard_map/all_to_all | solution.py:105
  60.8 1.2 gather_fusion.3
  62.0 1.2 gather_fusion.2
  63.2 2.2 %copy.117 = f32[256,1024]{0,1:T(8,128)} copy(bf16[256,1024]{1,0:T(8,128)(2,1)} %param.26) | data formatting | bytes 1572864 | tf_op jit(solution)/shard_map/reshape | solution.py:177
  65.5 0.8 fusion.58
  66.3 1.3 copy-done.21
  67.6 2.1 %fusion.59 = f32[8,128,256]{2,1,0:T(8,128)} fusion(f32[8,256,256]{1,2,0:T(8,128)S(1)} %get-tuple-element.74, pred[256,256]{0,1:T(8,128)(4,1)S(1)} %fusion.70, bf16[32,8,8,128]{3,2,1,0:T(8,128)(2,1)S(1)} %fusion.61), kind=kOutput, calls=%fused_computation.83 | convolution fusion | flops 405798912 | bytes 3735552 | tf_op jit(solution)/shard_map/hts,shv->thv/dot_general | solution.py:157
  69.8 9.6 %all-to-all-done.1 = f32[32,40,128]{2,1,0:T(8,128)} async-done(((f32[32,40,128]{2,1,0:T(8,128)}), f32[32,40,128]{2,1,0:T(8,128)}, u32[]{:S(2)}, u32[]{:S(2)}) %all-to-all-start.1) | async-done | bytes 655392 | tf_op jit(solution)/shard_map/all_to_all | solution.py:105
  79.4 0.9 slice_bitcast_fusion.5
  80.3 1.7 %fusion.79 = f32[8,1,256]{2,1,0:T(1,128)S(1)} fusion(f32[8,160,256]{2,1,0:T(8,128)} %get-tuple-element.59, f32[8,160,1]{1,0,2:T(8,128)S(1)} %get-tuple-element.53), kind=kOutput, calls=%fused_computation.122 | convolution fusion | flops 1966080 | bytes 1324032 | tf_op jit(solution)/shard_map/hft,hf->th/dot_general | solution.py:172
  82.0 3.7 %multiply_reduce_fusion.1 = (f32[256,8]{0,1:T(8,128)S(1)}, bf16[256,8,128]{0,2,1:T(8,128)(2,1)}) fusion(f32[256,1024]{0,1:T(8,128)} %copy.117, f32[256,8]{0,1:T(8,128)S(1)} %fusion.87, f32[8,128,256]{2,1,0:T(8,128)} %fusion.59, f32[8,160,128]{2,1,0:T(8,128)} %bitcast.19, f32[8,160,256]{2,1,0:T(8,128)S(1)} %copy-done.1, f32[256]{0:T(256)S(1)} %get-tuple-element.64), kind=kOutput, calls=%fused_computation.71 | convolution fusion | flops 253229056 | bytes 4604928 | tf_op jit(solution)/shard_map/hft,hfv->thv/dot_general | solution.py:169
  85.7 0.6 fusion.21
  86.3 0.6 copy-done.8
  86.9 1.6 %fusion.23 = f32[8,160,128]{2,1,0:T(8,128)} fusion(f32[8,160,256]{2,1,0:T(8,128)S(1)} %copy-done.1, f32[256]{0:T(256)S(1)} %get-tuple-element.62, f32[256,8,128]{0,2,1:T(8,128)S(1)} %bitcast.172, f32[256,8]{0,1:T(8,128)S(1)} %fusion.87), kind=kOutput, calls=%fused_computation.42 | convolution fusion | flops 252248064 | bytes 3023872 | tf_op jit(solution)/shard_map/hft,thv->hfv/dot_general | solution.py:182
  88.5 0.6 constant_dynamic-update-slice_fusion
  89.1 5.5 %all-to-all-start.2 = ((f32[32,40,128]{2,1,0:T(8,128)}), f32[32,40,128]{2,1,0:T(8,128)}, u32[]{:S(2)}, u32[]{:S(2)}) async-start(f32[32,40,128]{2,1,0:T(8,128)} %bitcast.175), calls=%async_computation.2 | async-start | bytes 1310720 | tf_op jit(solution)/shard_map/all_to_all | solution.py:102
  94.6 3.5 %fusion.30 = (f32[8,160,256]{2,1,0:T(8,128)S(1)}, f32[8,160,256]{2,1,0:T(8,128)S(1)}) fusion(f32[2,8,160,256]{3,2,1,0:T(8,128)} %copy-done.2, f32[160]{0:T(256)S(1)} %copy-done.16, f32[160]{0:T(256)S(1)} %copy-done.17, f32[160]{0:T(256)S(1)} %copy-done.15, f32[8,256]{1,0:T(8,128)S(1)} %bitcast_divide_fusion, f32[8,160]{1,0:T(8,128)S(1)} %get-tuple-element.52, ...), kind=kOutput, calls=%fused_computation.50 | convolution fusion | flops 254541824 | bytes 6971264 | tf_op jit(solution)/shard_map/hfv,thv->hft/dot_general | solution.py:194
  98.1 0.7 fusion
  98.9 0.4 copy-done.9
  99.3 1.1 multiply_select_fusion
  100.5 0.7 fusion.34
  101.1 0.5 fusion.36
  101.6 0.4 copy-done.13
  102.0 2.5 %convolution_bitcast_fusion.2 = f32[256,8,128]{0,2,1:T(8,128)} fusion(f32[8,256,256]{1,2,0:T(8,128)S(1)} %copy-done.22, pred[256,256]{0,1:T(8,128)(4,1)S(1)} %copy-done.13, f32[256,8,128]{0,2,1:T(8,128)S(1)} %bitcast.174, f32[256,8]{0,1:T(8,128)S(1)} %fusion.87), kind=kOutput, calls=%fused_computation.25 | convolution fusion | flops 406061056 | bytes 4268032 | tf_op jit(solution)/shard_map/hts,thv->shv/dot_general | solution.py:185
  104.5 9.0 %all-to-all-done.2 = f32[32,40,128]{2,1,0:T(8,128)} async-done(((f32[32,40,128]{2,1,0:T(8,128)}), f32[32,40,128]{2,1,0:T(8,128)}, u32[]{:S(2)}, u32[]{:S(2)}) %all-to-all-start.2) | async-done | bytes 655392 | tf_op jit(solution)/shard_map/all_to_all | solution.py:102
  113.4 1.5 fusion.51
  114.9 1.2 copy.128
  116.1 5.3 %all-to-all-start.3 = ((f32[32,40,128]{2,1,0:T(8,128)}), f32[32,40,128]{2,1,0:T(8,128)S(1)}, u32[]{:S(2)}, u32[]{:S(2)}) async-start(f32[32,40,128]{2,1,0:T(8,128)} %copy.128), calls=%async_computation.3 | async-start | bytes 1310720 | tf_op jit(solution)/shard_map/all_to_all | solution.py:105
  121.5 2.0 %copy.132 = bf16[256,1024]{1,0:T(8,128)(2,1)} copy(bf16[256,1024]{0,1:T(8,128)(2,1)} %bitcast.182) | data formatting | bytes 1048576
  123.5 0.7 copy.133
  124.3 15.8 %all-to-all-done.3 = f32[32,40,128]{2,1,0:T(8,128)S(1)} async-done(((f32[32,40,128]{2,1,0:T(8,128)}), f32[32,40,128]{2,1,0:T(8,128)S(1)}, u32[]{:S(2)}, u32[]{:S(2)}) %all-to-all-start.3) | async-done | bytes 655392 | tf_op jit(solution)/shard_map/all_to_all | solution.py:105
  140.1 3.7 %fusion.13 = f32[256,8,128]{0,2,1:T(8,128)} fusion(f32[256,8,128]{0,2,1:T(8,128)} %convolution_bitcast_fusion.2, f32[8,160,128]{2,1,0:T(8,128)S(1)} %bitcast.167, f32[8,160,256]{2,1,0:T(8,128)} %get-tuple-element.43, f32[256]{0:T(256)S(1)} %get-tuple-element.40), kind=kOutput, calls=%fused_computation.24 | convolution fusion | flops 252182528 | bytes 4064256 | tf_op jit(solution)/shard_map/hfs,hfv->shv/dot_general | solution.py:201
  143.8 2.6 %copy.130 = f32[256,1024]{1,0:T(8,128)} copy(f32[256,1024]{0,1:T(8,128)} %bitcast.169) | data formatting | bytes 2097152 | tf_op jit(solution)/shard_map/reshape | solution.py:211
  146.4 2.1 %fusion.28 = (f32[8,160,256]{2,1,0:T(8,128)S(1)}, f32[8,160,256]{2,1,0:T(8,128)S(1)}) fusion(f32[2,8,160,256]{3,2,1,0:T(8,128)S(1)} %convolution_bitcast_fusion.1, f32[160]{0:T(256)S(1)} %copy-done.16, f32[160]{0:T(256)S(1)} %copy-done.17, f32[160]{0:T(256)S(1)} %copy-done.15, f32[8,160]{1,0:T(8,128)S(1)} %bitcast.194, f32[8,160,128]{2,1,0:T(8,128)S(1)} %bitcast.168, ...), kind=kOutput, calls=%fused_computation.48 | convolution fusion | flops 253952000 | bytes 6430592 | tf_op jit(solution)/shard_map/hfv,shv->hfs/dot_general | solution.py:205
  148.5 1.7 %multiply_convert_fusion = (bf16[256,1024]{1,0:T(8,128)(2,1)}, f32[256,1024]{1,0:T(8,128)S(1)}) fusion(f32[256,1024]{1,0:T(8,128)S(1)} %copy-done.4, bf16[256,1024]{1,0:T(8,128)(2,1)S(1)} %copy-done.7, f32[256]{0:T(256)S(1)} %get-tuple-element.65, bf16[256,1024]{1,0:T(8,128)(2,1)S(1)} %copy-done.6, bf16[2,1024]{1,0:T(2,128)(2,1)S(1)} %collective-permute-done, ...), kind=kLoop, calls=%fused_computation.70 | loop fusion | flops 6815744 | bytes 3688448 | tf_op jit(solution)/shard_map/convert_element_type | solution.py:212
  150.2 4.4 %collective-permute-start.1 = (f32[2,1024]{1,0:T(2,128)S(1)}, f32[2,1024]{1,0:T(2,128)S(1)}, u32[]{:S(2)}, u32[]{:S(2)}) collective-permute-start(f32[2,1024]{1,0:T(2,128)S(1)} %slice.124), channel_id=1, source_target_pairs={{8,0},{16,8},{24,16},{32,24},{40,32},{48,40},{56,48},{64,56},{72,6... | collective-permute-start | bytes 24584 | tf_op jit(solution)/shard_map/ppermute | solution.py:23
  154.6 0.7 fusion.40
  155.3 0.7 copy.134
  156.1 1.2 fusion.48
  (84 shorter events, 1.2 us)
Async XLA Ops:
  1.4 16.4 %collective-permute-start = (bf16[2,1024]{1,0:T(2,128)(2,1)S(1)}, bf16[2,1024]{1,0:T(2,128)(2,1)S(1)}, u32[]{:S(2)}, u32[]{:S(2)}) collective-permute-start(bf16[2,1024]{1,0:T(2,128)(2,1)S(1)} %slice.80), channel_id=1, source_target_pairs={{0,8},{8,16},{16,24},{24,32},{32,40},{40,48},{48,56},{56,64},{64,7... | collective-permute-start | bytes 12296 | tf_op jit(solution)/shard_map/ppermute | solution.py:23
  11.1 1.3 copy-start.11
  12.5 3.3 %copy-start.15 = (f32[160]{0:T(256)S(1)}, f32[160]{0:T(256)}, u32[]{:S(2)}) copy-start(f32[160]{0:T(256)} %constant.80.clone) | copy-start | bytes 1924
  12.5 3.3 %copy-start.16 = (f32[160]{0:T(256)S(1)}, f32[160]{0:T(256)}, u32[]{:S(2)}) copy-start(f32[160]{0:T(256)} %constant.79.clone) | copy-start | bytes 1924
  12.5 3.3 %copy-start.17 = (f32[160]{0:T(256)S(1)}, f32[160]{0:T(256)}, u32[]{:S(2)}) copy-start(f32[160]{0:T(256)} %constant.78.clone) | copy-start | bytes 1924
  13.0 4.6 %copy-start.2 = (f32[2,8,160,256]{3,2,1,0:T(8,128)}, f32[2,8,160,256]{3,2,1,0:T(8,128)S(1)}, u32[]{:S(2)}) copy-start(f32[2,8,160,256]{3,2,1,0:T(8,128)S(1)} %convolution_bitcast_fusion) | copy-start | bytes 7864324
  15.8 1.9 %copy-start.14 = (bf16[3,1024]{1,0:T(4,128)(2,1)S(1)}, bf16[3,1024]{1,0:T(4,128)(2,1)}, u32[]{:S(2)}) copy-start(bf16[3,1024]{1,0:T(4,128)(2,1)} %param.24) | copy-start | bytes 18436
  17.7 2.5 %copy-start = (f32[8,160,256]{2,1,0:T(8,128)S(1)}, f32[8,160,256]{2,1,0:T(8,128)}, u32[]{:S(2)}) copy-start(f32[8,160,256]{2,1,0:T(8,128)} %get-tuple-element.43) | copy-start | bytes 3932164
  20.2 78.7 %copy-start.3 = (bf16[32,8,8,128]{3,2,1,0:T(8,128)(2,1)}, bf16[32,8,8,128]{3,2,1,0:T(8,128)(2,1)S(1)}, u32[]{:S(2)}) copy-start(bf16[32,8,8,128]{3,2,1,0:T(8,128)(2,1)S(1)} %fusion.61) | copy-start | bytes 1572868
  20.8 0.8 copy-start.5
  21.6 30.7 %all-to-all-start = ((f32[32,40,128]{2,1,0:T(8,128)}), f32[32,40,128]{2,1,0:T(8,128)}, u32[]{:S(2)}, u32[]{:S(2)}) async-start(f32[32,40,128]{2,1,0:T(8,128)} %bitcast.170), calls=%async_computation | async-start | bytes 1310720 | tf_op jit(solution)/shard_map/all_to_all | solution.py:102
  55.0 24.4 %all-to-all-start.1 = ((f32[32,40,128]{2,1,0:T(8,128)}), f32[32,40,128]{2,1,0:T(8,128)}, u32[]{:S(2)}, u32[]{:S(2)}) async-start(f32[32,40,128]{2,1,0:T(8,128)} %copy.116), calls=%async_computation.1 | async-start | bytes 1310720 | tf_op jit(solution)/shard_map/all_to_all | solution.py:105
  65.5 33.3 %copy-start.12 = (pred[256,256]{0,1:T(8,128)(4,1)}, pred[256,256]{0,1:T(8,128)(4,1)S(1)}, u32[]{:S(2)}) copy-start(pred[256,256]{0,1:T(8,128)(4,1)S(1)} %fusion.70) | copy-start | bytes 196612
  66.3 1.3 copy-start.21
  79.4 2.6 %copy-start.1 = (f32[8,160,256]{2,1,0:T(8,128)S(1)}, f32[8,160,256]{2,1,0:T(8,128)}, u32[]{:S(2)}) copy-start(f32[8,160,256]{2,1,0:T(8,128)} %get-tuple-element.59) | copy-start | bytes 3932164
  85.7 1.2 copy-start.8
  89.1 24.3 %all-to-all-start.2 = ((f32[32,40,128]{2,1,0:T(8,128)}), f32[32,40,128]{2,1,0:T(8,128)}, u32[]{:S(2)}, u32[]{:S(2)}) async-start(f32[32,40,128]{2,1,0:T(8,128)} %bitcast.175), calls=%async_computation.2 | async-start | bytes 1310720 | tf_op jit(solution)/shard_map/all_to_all | solution.py:102
  94.6 3.5 %copy-start.10 = (f32[320,16,1]{0,1,2:T(8,128)S(1)}, f32[320,16,1]{0,1,2:T(8,128)}, u32[]{:S(2)}) copy-start(f32[320,16,1]{0,1,2:T(8,128)} %constant.87) | copy-start | bytes 61444
  94.6 4.3 %copy-start.22 = (f32[8,256,256]{1,2,0:T(8,128)S(1)}, f32[8,256,256]{1,2,0:T(8,128)}, u32[]{:S(2)}) copy-start(f32[8,256,256]{1,2,0:T(8,128)} %copy-done.21) | copy-start | bytes 6291460
  98.1 1.2 copy-start.9
  101.1 0.8 copy-start.13
  102.0 11.5 %copy-start.19 = (s32[32]{0:T(128)S(1)}, s32[32]{0:T(128)}, u32[]{:S(2)}) copy-start(s32[32]{0:T(128)} %gather_fusion.3) | copy-start | bytes 388
  102.0 11.5 %copy-start.20 = (s32[32]{0:T(128)S(1)}, s32[32]{0:T(128)}, u32[]{:S(2)}) copy-start(s32[32]{0:T(128)} %gather_fusion.2) | copy-start | bytes 388
  116.1 24.0 %all-to-all-start.3 = ((f32[32,40,128]{2,1,0:T(8,128)}), f32[32,40,128]{2,1,0:T(8,128)S(1)}, u32[]{:S(2)}, u32[]{:S(2)}) async-start(f32[32,40,128]{2,1,0:T(8,128)} %copy.128), calls=%async_computation.3 | async-start | bytes 1310720 | tf_op jit(solution)/shard_map/all_to_all | solution.py:105
  146.4 2.1 %copy-start.4 = (f32[256,1024]{1,0:T(8,128)S(1)}, f32[256,1024]{1,0:T(8,128)}, u32[]{:S(2)}) copy-start(f32[256,1024]{1,0:T(8,128)} %copy.130) | copy-start | bytes 3145732
  146.4 2.1 %copy-start.6 = (bf16[256,1024]{1,0:T(8,128)(2,1)S(1)}, bf16[256,1024]{1,0:T(8,128)(2,1)}, u32[]{:S(2)}) copy-start(bf16[256,1024]{1,0:T(8,128)(2,1)} %param.22) | copy-start | bytes 1572868
  146.4 2.1 %copy-start.7 = (bf16[256,1024]{1,0:T(8,128)(2,1)S(1)}, bf16[256,1024]{1,0:T(8,128)(2,1)}, u32[]{:S(2)}) copy-start(bf16[256,1024]{1,0:T(8,128)(2,1)} %param.23) | copy-start | bytes 1572868
  150.2 5.9 %collective-permute-start.1 = (f32[2,1024]{1,0:T(2,128)S(1)}, f32[2,1024]{1,0:T(2,128)S(1)}, u32[]{:S(2)}, u32[]{:S(2)}) collective-permute-start(f32[2,1024]{1,0:T(2,128)S(1)} %slice.124), channel_id=1, source_target_pairs={{8,0},{16,8},{24,16},{32,24},{40,32},{48,40},{56,48},{64,56},{72,6... | collective-permute-start | bytes 24584 | tf_op jit(solution)/shard_map/ppermute | solution.py:23
  154.6 1.5 copy-start.18

commit v10 on v9

--- a/solution.py
+++ b/solution.py
@@ -195,8 +195,9 @@
         + norm_in[:, :, None] * jnp.transpose(grad_den, (1, 0))[:, None, :]
     )
     grad_q = grad_q + feature_grad(grad_phi_query, spread_query)
-    grad_state_in, grad_norm_in, (grad_v, grad_q, grad_k) = state_scan(
-        back_state, back_norm, backward_mask, (grad_v, grad_q, grad_k)
+    gate_slope = convolved * opening * (1.0 - opening)
+    grad_state_in, grad_norm_in, (grad_v, grad_q, grad_k, gate_slope) = state_scan(
+        back_state, back_norm, backward_mask, (grad_v, grad_q, grad_k, gate_slope)
     )
     grad_v = grad_v + outside[:, None, None] * jnp.einsum(
         "hfs,hfv->shv", phi_key, grad_state_in, precision=high
@@ -209,7 +210,7 @@
     grad_query = grad_q.reshape(tok_rows, HEADS * KD).astype(jnp.bfloat16)
     grad_key = grad_k.reshape(tok_rows, HEADS * KD).astype(jnp.bfloat16)
     grad_core = grad_v.reshape(tok_rows, channels)
-    grad_gate = (grad_core * convolved * opening * (1.0 - opening)).astype(jnp.bfloat16)
+    grad_gate = (grad_core * gate_slope).astype(jnp.bfloat16)
     grad_conv = grad_core * opening
     later_rows = shifted(grad_conv[: CONV - 1], "ctx", -1)
     ahead = jnp.concatenate([grad_conv, later_rows], axis=0)

time: 160 us -> 162 us (1.012)
  other arithmetic: 13.2 us -> 14.9 us
    mul x0 -> x1, other arithmetic: none -> 3.6 us  [local(): gate_slope = convolved * opening * (1.0 - opening)]
    unnamed x1 -> x0, other arithmetic: 2.48 us -> none
    unnamed x55 -> x49, local copies, waits for them, and re-layouts: 9.89 us -> 10.9 us
  transfers between devices with their start and end apart: 6 -> 6, of which waited for: 4 -> 4; matrix products, arithmetic and copies ran while one was open for 23% -> 22% of each run, Pallas kernels for 0% -> 0%
where the time goes in v10:
time: 162 us; the launch traced here: 159 us
  waiting for transfers between devices  53 us (33%)
  starting transfers between devices  35.3 us (22%)
  matrix products  29.9 us (18%)
  local copies, waits for them, and re-layouts  24.4 us (15%)
  other arithmetic  14.9 us (9%)
    all_to_all x2, waiting for transfers between devices, state_scan(): chunks = lax.all_to_all(packed, 'ctx', 0, 0, tiled=True)  26.6 us
    all_to_all x2, waiting for transfers between devices, state_scan(): lax.all_to_all(summed, 'ctx', 0, 0, tiled=True).reshape(heads, feats, width)  26.5 us
    all_to_all x2, starting transfers between devices, state_scan(): chunks = lax.all_to_all(packed, 'ctx', 0, 0, tiled=True)  16.6 us
    unnamed x49, local copies, waits for them, and re-layouts  10.9 us
    all_to_all x2, starting transfers between devices, state_scan(): lax.all_to_all(summed, 'ctx', 0, 0, tiled=True).reshape(heads, feats, width)  10.8 us
    ppermute x2, starting transfers between devices, shifted(): return lax.ppermute(block, axis, route)  7.87 us
    dot_general x1, matrix products, local(): jnp.einsum('hft,hfv->thv', phi_query, state_in, precision=high)  3.69 us
    dot_general x1, matrix products, local(): jnp.einsum('hfs,hfv->shv', phi_key, grad_state_in, precision=high)  3.66 us
  transfers between devices with their start and end apart: 6, of which 4 were waited for; matrix products, arithmetic and copies ran while one was open for 22% of the time, Pallas kernels for 0%

profile of v10, /device:TPU:32, one launch (start us, length us, event | category | flops | bytes accessed | tf_op | source)
XLA Modules:
  0.0 158.6 jit_solution(17431047597064268246)
XLA Ops:
  0.6 0.7 slice.80
  1.4 3.5 %collective-permute-start = (bf16[2,1024]{1,0:T(2,128)(2,1)S(1)}, bf16[2,1024]{1,0:T(2,128)(2,1)S(1)}, u32[]{:S(2)}, u32[]{:S(2)}) collective-permute-start(bf16[2,1024]{1,0:T(2,128)(2,1)S(1)} %slice.80), channel_id=1, source_target_pairs={{0,8},{8,16},{16,24},{24,32},{32,40},{40,48},{48,56},{56,64},{64,7... | collective-permute-start | bytes 12296 | tf_op jit(solution)/shard_map/ppermute | solution.py:23
  4.9 0.7 broadcast_add_fusion.3
  5.5 0.7 copy.108
  6.8 0.7 compare_select_fusion
  7.4 0.6 fusion.106
  8.0 0.6 compare_convert_fusion.4
  8.7 0.6 fusion.105
  9.2 0.9 copy.109
  10.2 0.9 copy.110
  11.2 1.3 convolution_bitcast_fusion.1
  12.5 0.5 convolution_bitcast_fusion
  13.1 2.1 %compare_convert_fusion.1 = (f32[256]{0:T(256)S(1)}, f32[256]{0:T(256)S(1)}, f32[256]{0:T(256)S(1)}, f32[256]{0:T(256)S(1)}, f32[256]{0:T(256)S(1)}, /*index=5*/f32[256]{0:T(256)S(1)}, f32[256]{0:T(256)S(1)}) fusion(s32[256]{0:T(256)S(1)} %get-tuple-element.43, s32[258]{0:T(512)S(1)} %get-tuple-element.71, s32[]{:T(128)} %bitcast.30, s32[]{:T(128)} %bitcast.17, ...), kind=kLoop, calls=%fused_computation.138 | loop fusion | flops 3584 | bytes 12300 | tf_op jit(solution)/shard_map/convert_element_type | solution.py:220
  15.2 1.9 %multiply_reduce_fusion = (f32[8,160]{1,0:T(8,128)S(1)}, f32[8,160,256]{2,1,0:T(8,128)}, f32[8,160,256]{2,1,0:T(8,128)}) fusion(f32[256]{0:T(256)S(1)} %get-tuple-element.67, f32[160]{0:T(256)S(1)} %copy-done.16, f32[2,8,160,256]{3,2,1,0:T(8,128)S(1)} %convolution_bitcast_fusion.1, f32[160]{0:T(256)S(1)} %copy-done.17, f32[160]{0:T(256)S(1)} %copy-done.15, ...), kind=kLoop, calls=%fused_computation.44 | loop fusion | flops 3275520 | bytes 7872384 | tf_op jit(solution)/shard_map/reduce_sum | solution.py:164
  17.2 3.6 %subtract_multiply_fusion = (f32[256,1024]{1,0:T(8,128)}, bf16[256,1024]{1,0:T(8,128)(2,1)S(1)}) fusion(bf16[256,1024]{1,0:T(8,128)(2,1)} %param.23, f32[256]{0:T(256)S(1)} %get-tuple-element.69, bf16[256,1024]{1,0:T(8,128)(2,1)} %param.22, bf16[2,1024]{1,0:T(2,128)(2,1)S(1)} %collective-permute-done, f32[1024]{0:T(1024)S(1)} %bitcast.202, ...), kind=kLoop, calls=%fused_computation.71 | loop fusion | flops 6291456 | bytes 2639872 | tf_op jit(solution)/shard_map/mul | solution.py:198
  20.8 0.5 fusion.25
  21.3 0.8 copy-done.7
  22.2 11.1 %all-to-all-start = ((f32[32,40,128]{2,1,0:T(8,128)}), f32[32,40,128]{2,1,0:T(8,128)}, u32[]{:S(2)}, u32[]{:S(2)}) async-start(f32[32,40,128]{2,1,0:T(8,128)} %bitcast.183), calls=%async_computation | async-start | bytes 1310720 | tf_op jit(solution)/shard_map/all_to_all | solution.py:102
  33.3 0.2 convert_reduce_fusion.2
  33.8 0.7 gather_fusion.1
  34.6 0.7 gather_fusion
  35.3 17.6 %all-to-all-done = f32[32,40,128]{2,1,0:T(8,128)} async-done(((f32[32,40,128]{2,1,0:T(8,128)}), f32[32,40,128]{2,1,0:T(8,128)}, u32[]{:S(2)}, u32[]{:S(2)}) %all-to-all-start) | async-done | bytes 655392 | tf_op jit(solution)/shard_map/all_to_all | solution.py:102
  52.8 1.5 fusion.53
  54.3 1.2 copy.116
  55.5 5.5 %all-to-all-start.1 = ((f32[32,40,128]{2,1,0:T(8,128)}), f32[32,40,128]{2,1,0:T(8,128)}, u32[]{:S(2)}, u32[]{:S(2)}) async-start(f32[32,40,128]{2,1,0:T(8,128)} %copy.116), calls=%async_computation.1 | async-start | bytes 1310720 | tf_op jit(solution)/shard_map/all_to_all | solution.py:105
  61.3 0.7 gather_fusion.3
  62.0 0.7 gather_fusion.2
  62.7 2.3 %copy.117 = f32[256,1024]{0,1:T(8,128)} copy(bf16[256,1024]{1,0:T(8,128)(2,1)} %param.26) | data formatting | bytes 1572864 | tf_op jit(solution)/shard_map/reshape | solution.py:177
  65.1 0.8 fusion.58
  65.9 1.3 copy-done.18
  67.2 2.0 %fusion.59 = f32[8,128,256]{2,1,0:T(8,128)} fusion(f32[8,256,256]{1,2,0:T(8,128)S(1)} %get-tuple-element.78, pred[256,256]{0,1:T(8,128)(4,1)S(1)} %fusion.69, bf16[256,1024]{1,0:T(8,128)(2,1)S(1)} %get-tuple-element.45), kind=kOutput, calls=%fused_computation.83 | convolution fusion | flops 405798912 | bytes 3735552 | tf_op jit(solution)/shard_map/hts,shv->thv/dot_general | solution.py:157
  69.3 10.6 %all-to-all-done.1 = f32[32,40,128]{2,1,0:T(8,128)} async-done(((f32[32,40,128]{2,1,0:T(8,128)}), f32[32,40,128]{2,1,0:T(8,128)}, u32[]{:S(2)}, u32[]{:S(2)}) %all-to-all-start.1) | async-done | bytes 655392 | tf_op jit(solution)/shard_map/all_to_all | solution.py:105
  79.9 0.9 slice_bitcast_fusion.5
  80.8 1.7 %fusion.78 = f32[8,1,256]{2,1,0:T(1,128)S(1)} fusion(f32[8,160,256]{2,1,0:T(8,128)} %get-tuple-element.63, f32[8,160,1]{1,0,2:T(8,128)S(1)} %get-tuple-element.57), kind=kOutput, calls=%fused_computation.122 | convolution fusion | flops 1966080 | bytes 1324032 | tf_op jit(solution)/shard_map/hft,hf->th/dot_general | solution.py:172
  82.5 3.7 %multiply_reduce_fusion.1 = (f32[256,8]{0,1:T(8,128)S(1)}, bf16[256,8,128]{0,2,1:T(8,128)(2,1)}) fusion(f32[256,1024]{0,1:T(8,128)} %copy.117, f32[256,8]{0,1:T(8,128)S(1)} %fusion.86, f32[8,128,256]{2,1,0:T(8,128)} %fusion.59, f32[8,160,128]{2,1,0:T(8,128)} %bitcast.19, f32[8,160,256]{2,1,0:T(8,128)S(1)} %copy-done.1, f32[256]{0:T(256)S(1)} %get-tuple-element.68), kind=kOutput, calls=%fused_computation.72 | convolution fusion | flops 253229056 | bytes 4604928 | tf_op jit(solution)/shard_map/hft,hfv->thv/dot_general | solution.py:169
  86.2 0.6 fusion.21
  86.9 0.6 copy-done.8
  87.4 1.6 fusion.23
  89.0 0.6 constant_dynamic-update-slice_fusion
  89.7 5.5 %all-to-all-start.2 = ((f32[32,40,128]{2,1,0:T(8,128)}), f32[32,40,128]{2,1,0:T(8,128)}, u32[]{:S(2)}, u32[]{:S(2)}) async-start(f32[32,40,128]{2,1,0:T(8,128)} %bitcast.188), calls=%async_computation.2 | async-start | bytes 1310720 | tf_op jit(solution)/shard_map/all_to_all | solution.py:102
  95.2 3.5 %fusion.30 = (f32[8,160,256]{2,1,0:T(8,128)S(1)}, f32[8,160,256]{2,1,0:T(8,128)S(1)}) fusion(f32[2,8,160,256]{3,2,1,0:T(8,128)} %copy-done.2, f32[160]{0:T(256)S(1)} %copy-done.16, f32[160]{0:T(256)S(1)} %copy-done.17, f32[160]{0:T(256)S(1)} %copy-done.15, f32[8,256]{1,0:T(8,128)S(1)} %bitcast_divide_fusion, f32[8,160]{1,0:T(8,128)S(1)} %get-tuple-element.56, ...), kind=kOutput, calls=%fused_computation.50 | convolution fusion | flops 254541824 | bytes 6971264 | tf_op jit(solution)/shard_map/hfv,thv->hft/dot_general | solution.py:194
  98.6 0.7 fusion
  99.4 0.4 copy-done.9
  99.8 1.1 multiply_select_fusion
  101.0 0.7 fusion.34
  101.6 0.5 fusion.36
  102.1 0.4 copy-done.13
  102.5 2.5 %convolution_bitcast_fusion.2 = f32[256,8,128]{0,2,1:T(8,128)} fusion(f32[8,256,256]{1,2,0:T(8,128)S(1)} %copy-done.19, pred[256,256]{0,1:T(8,128)(4,1)S(1)} %copy-done.13, f32[256,8,128]{0,2,1:T(8,128)S(1)} %bitcast.187, f32[256,8]{0,1:T(8,128)S(1)} %fusion.86), kind=kOutput, calls=%fused_computation.25 | convolution fusion | flops 406061056 | bytes 4268032 | tf_op jit(solution)/shard_map/hts,thv->shv/dot_general | solution.py:185
  104.9 9.0 %all-to-all-done.2 = f32[32,40,128]{2,1,0:T(8,128)} async-done(((f32[32,40,128]{2,1,0:T(8,128)}), f32[32,40,128]{2,1,0:T(8,128)}, u32[]{:S(2)}, u32[]{:S(2)}) %all-to-all-start.2) | async-done | bytes 655392 | tf_op jit(solution)/shard_map/all_to_all | solution.py:102
  113.9 1.5 fusion.51
  115.4 1.2 copy.128
  116.6 5.4 %all-to-all-start.3 = ((f32[32,40,128]{2,1,0:T(8,128)}), f32[32,40,128]{2,1,0:T(8,128)S(1)}, u32[]{:S(2)}, u32[]{:S(2)}) async-start(f32[32,40,128]{2,1,0:T(8,128)} %copy.128), calls=%async_computation.3 | async-start | bytes 1310720 | tf_op jit(solution)/shard_map/all_to_all | solution.py:105
  122.0 2.0 %copy.132 = bf16[256,1024]{1,0:T(8,128)(2,1)} copy(bf16[256,1024]{0,1:T(8,128)(2,1)} %bitcast.195) | data formatting | bytes 1048576
  124.0 0.7 copy.133
  124.8 15.8 %all-to-all-done.3 = f32[32,40,128]{2,1,0:T(8,128)S(1)} async-done(((f32[32,40,128]{2,1,0:T(8,128)}), f32[32,40,128]{2,1,0:T(8,128)S(1)}, u32[]{:S(2)}, u32[]{:S(2)}) %all-to-all-start.3) | async-done | bytes 655392 | tf_op jit(solution)/shard_map/all_to_all | solution.py:105
  140.6 3.7 %fusion.13 = f32[256,8,128]{0,2,1:T(8,128)} fusion(f32[256,8,128]{0,2,1:T(8,128)} %convolution_bitcast_fusion.2, f32[8,160,128]{2,1,0:T(8,128)S(1)} %bitcast.180, f32[8,160,256]{2,1,0:T(8,128)} %get-tuple-element.47, f32[256]{0:T(256)S(1)} %get-tuple-element.42), kind=kOutput, calls=%fused_computation.24 | convolution fusion | flops 252182528 | bytes 4064256 | tf_op jit(solution)/shard_map/hfs,hfv->shv/dot_general | solution.py:202
  144.3 2.5 %copy.130 = f32[256,1024]{1,0:T(8,128)} copy(f32[256,1024]{0,1:T(8,128)} %bitcast.182) | data formatting | bytes 2097152 | tf_op jit(solution)/shard_map/reshape | solution.py:212
  146.8 2.8 %multiply_convert_fusion = (bf16[256,1024]{1,0:T(8,128)(2,1)}, f32[256,1024]{1,0:T(8,128)S(1)}) fusion(f32[256,1024]{1,0:T(8,128)} %copy.130, f32[256,1024]{1,0:T(8,128)} %get-tuple-element.14, bf16[256,1024]{1,0:T(8,128)(2,1)} %param.23), kind=kLoop, calls=%fused_computation.70 | loop fusion | flops 1835008 | bytes 4194304 | tf_op jit(solution)/shard_map/convert_element_type | solution.py:213
  149.6 1.0 copy-done.5
  150.6 0.9 fusion.28
  151.5 4.4 %collective-permute-start.1 = (f32[2,1024]{1,0:T(2,128)S(1)}, f32[2,1024]{1,0:T(2,128)S(1)}, u32[]{:S(2)}, u32[]{:S(2)}) collective-permute-start(f32[2,1024]{1,0:T(2,128)S(1)} %slice.124), channel_id=1, source_target_pairs={{8,0},{16,8},{24,16},{32,24},{40,32},{48,40},{56,48},{64,56},{72,6... | collective-permute-start | bytes 24584 | tf_op jit(solution)/shard_map/ppermute | solution.py:23
  155.9 0.7 fusion.40
  156.7 0.7 copy.134
  157.4 1.2 fusion.48
  (78 shorter events, 1.5 us)
Async XLA Ops:
  1.4 15.8 %collective-permute-start = (bf16[2,1024]{1,0:T(2,128)(2,1)S(1)}, bf16[2,1024]{1,0:T(2,128)(2,1)S(1)}, u32[]{:S(2)}, u32[]{:S(2)}) collective-permute-start(bf16[2,1024]{1,0:T(2,128)(2,1)S(1)} %slice.80), channel_id=1, source_target_pairs={{0,8},{8,16},{16,24},{24,32},{32,40},{40,48},{48,56},{56,64},{64,7... | collective-permute-start | bytes 12296 | tf_op jit(solution)/shard_map/ppermute | solution.py:23
  11.1 1.3 copy-start.11
  12.5 2.7 %copy-start.15 = (f32[160]{0:T(256)S(1)}, f32[160]{0:T(256)}, u32[]{:S(2)}) copy-start(f32[160]{0:T(256)} %constant.80.clone) | copy-start | bytes 1924
  12.5 2.7 %copy-start.16 = (f32[160]{0:T(256)S(1)}, f32[160]{0:T(256)}, u32[]{:S(2)}) copy-start(f32[160]{0:T(256)} %constant.79.clone) | copy-start | bytes 1924
  12.5 2.7 %copy-start.17 = (f32[160]{0:T(256)S(1)}, f32[160]{0:T(256)}, u32[]{:S(2)}) copy-start(f32[160]{0:T(256)} %constant.78.clone) | copy-start | bytes 1924
  13.0 4.1 %copy-start.2 = (f32[2,8,160,256]{3,2,1,0:T(8,128)}, f32[2,8,160,256]{3,2,1,0:T(8,128)S(1)}, u32[]{:S(2)}) copy-start(f32[2,8,160,256]{3,2,1,0:T(8,128)S(1)} %convolution_bitcast_fusion) | copy-start | bytes 7864324
  15.2 1.9 %copy-start.14 = (bf16[3,1024]{1,0:T(4,128)(2,1)S(1)}, bf16[3,1024]{1,0:T(4,128)(2,1)}, u32[]{:S(2)}) copy-start(bf16[3,1024]{1,0:T(4,128)(2,1)} %param.24) | copy-start | bytes 18436
  17.2 3.6 %copy-start = (f32[8,160,256]{2,1,0:T(8,128)S(1)}, f32[8,160,256]{2,1,0:T(8,128)}, u32[]{:S(2)}) copy-start(f32[8,160,256]{2,1,0:T(8,128)} %get-tuple-element.47) | copy-start | bytes 3932164
  20.8 78.6 %copy-start.3 = (bf16[256,1024]{1,0:T(8,128)(2,1)}, bf16[256,1024]{1,0:T(8,128)(2,1)S(1)}, u32[]{:S(2)}) copy-start(bf16[256,1024]{1,0:T(8,128)(2,1)S(1)} %get-tuple-element.45) | copy-start | bytes 1572868
  21.3 0.8 copy-start.7
  22.2 30.7 %all-to-all-start = ((f32[32,40,128]{2,1,0:T(8,128)}), f32[32,40,128]{2,1,0:T(8,128)}, u32[]{:S(2)}, u32[]{:S(2)}) async-start(f32[32,40,128]{2,1,0:T(8,128)} %bitcast.183), calls=%async_computation | async-start | bytes 1310720 | tf_op jit(solution)/shard_map/all_to_all | solution.py:102
  55.5 24.4 %all-to-all-start.1 = ((f32[32,40,128]{2,1,0:T(8,128)}), f32[32,40,128]{2,1,0:T(8,128)}, u32[]{:S(2)}, u32[]{:S(2)}) async-start(f32[32,40,128]{2,1,0:T(8,128)} %copy.116), calls=%async_computation.1 | async-start | bytes 1310720 | tf_op jit(solution)/shard_map/all_to_all | solution.py:105
  65.1 34.3 %copy-start.12 = (pred[256,256]{0,1:T(8,128)(4,1)}, pred[256,256]{0,1:T(8,128)(4,1)S(1)}, u32[]{:S(2)}) copy-start(pred[256,256]{0,1:T(8,128)(4,1)S(1)} %fusion.69) | copy-start | bytes 196612
  65.9 1.3 copy-start.18
  79.9 2.6 %copy-start.1 = (f32[8,160,256]{2,1,0:T(8,128)S(1)}, f32[8,160,256]{2,1,0:T(8,128)}, u32[]{:S(2)}) copy-start(f32[8,160,256]{2,1,0:T(8,128)} %get-tuple-element.63) | copy-start | bytes 3932164
  86.2 1.2 copy-start.8
  89.7 24.3 %all-to-all-start.2 = ((f32[32,40,128]{2,1,0:T(8,128)}), f32[32,40,128]{2,1,0:T(8,128)}, u32[]{:S(2)}, u32[]{:S(2)}) async-start(f32[32,40,128]{2,1,0:T(8,128)} %bitcast.188), calls=%async_computation.2 | async-start | bytes 1310720 | tf_op jit(solution)/shard_map/all_to_all | solution.py:102
  95.1 3.5 %copy-start.10 = (f32[320,16,1]{0,1,2:T(8,128)S(1)}, f32[320,16,1]{0,1,2:T(8,128)}, u32[]{:S(2)}) copy-start(f32[320,16,1]{0,1,2:T(8,128)} %constant.87) | copy-start | bytes 61444
  95.1 4.3 %copy-start.19 = (f32[8,256,256]{1,2,0:T(8,128)S(1)}, f32[8,256,256]{1,2,0:T(8,128)}, u32[]{:S(2)}) copy-start(f32[8,256,256]{1,2,0:T(8,128)} %copy-done.18) | copy-start | bytes 6291460
  98.6 1.2 copy-start.9
  101.6 0.8 copy-start.13
  116.6 24.0 %all-to-all-start.3 = ((f32[32,40,128]{2,1,0:T(8,128)}), f32[32,40,128]{2,1,0:T(8,128)S(1)}, u32[]{:S(2)}, u32[]{:S(2)}) async-start(f32[32,40,128]{2,1,0:T(8,128)} %copy.128), calls=%async_computation.3 | async-start | bytes 1310720 | tf_op jit(solution)/shard_map/all_to_all | solution.py:105
  146.8 3.8 %copy-start.4 = (bf16[256,1024]{1,0:T(8,128)(2,1)S(1)}, bf16[256,1024]{1,0:T(8,128)(2,1)}, u32[]{:S(2)}) copy-start(bf16[256,1024]{1,0:T(8,128)(2,1)} %copy-done.3) | copy-start | bytes 1572868
  149.6 1.0 copy-start.5
  151.5 5.9 %collective-permute-start.1 = (f32[2,1024]{1,0:T(2,128)S(1)}, f32[2,1024]{1,0:T(2,128)S(1)}, u32[]{:S(2)}, u32[]{:S(2)}) collective-permute-start(f32[2,1024]{1,0:T(2,128)S(1)} %slice.124), channel_id=1, source_target_pairs={{8,0},{16,8},{24,16},{32,24},{40,32},{48,40},{56,48},{64,56},{72,6... | collective-permute-start | bytes 24584 | tf_op jit(solution)/shard_map/ppermute | solution.py:23
  155.9 1.5 copy-start.6

commit v11 on v9

--- a/solution.py
+++ b/solution.py
@@ -164,7 +164,7 @@
     local_norm = jnp.sum(masked_key, axis=2)
     restart_all, closes_all = block_flags(doc_lengths, lax.axis_size("ctx"), tok_rows)
     forward_mask, backward_mask = scan_masks(restart_all, closes_all)
-    state_in, norm_in, _ = state_scan(local_state, local_norm, forward_mask, ())
+    state_in, norm_in, denominator = state_scan(local_state, local_norm, forward_mask, denominator)
     inside = (doc_ids == prev_doc).astype(jnp.float32)
     numerator = numerator + inside[:, None, None] * jnp.einsum(
         "hft,hfv->thv", phi_query, state_in, precision=high

time: 160 us -> 161 us (level)
  matrix products: 31.2 us -> 34.1 us
    all_to_all x2, waiting for transfers between devices: 26.5 us -> 24.4 us  [state_scan(): chunks = lax.all_to_all(packed, 'ctx', 0, 0, tiled=True)]
    unnamed x55 -> x51, local copies, waits for them, and re-layouts: 9.89 us -> 8.65 us
  transfers between devices with their start and end apart: 6 -> 6, of which waited for: 4 -> 4; matrix products, arithmetic and copies ran while one was open for 23% -> 25% of each run, Pallas kernels for 0% -> 0%
where the time goes in v11:
time: 161 us; the launch traced here: 158 us
  waiting for transfers between devices  50.5 us (31%)
  starting transfers between devices  35.2 us (22%)
  matrix products  34.1 us (21%)
  local copies, waits for them, and re-layouts  24 us (15%)
  other arithmetic  13.2 us (8%)
    all_to_all x2, waiting for transfers between devices, state_scan(): lax.all_to_all(summed, 'ctx', 0, 0, tiled=True).reshape(heads, feats, width)  26.1 us
    all_to_all x2, waiting for transfers between devices, state_scan(): chunks = lax.all_to_all(packed, 'ctx', 0, 0, tiled=True)  24.4 us
    all_to_all x2, starting transfers between devices, state_scan(): chunks = lax.all_to_all(packed, 'ctx', 0, 0, tiled=True)  16.6 us
    all_to_all x2, starting transfers between devices, state_scan(): lax.all_to_all(summed, 'ctx', 0, 0, tiled=True).reshape(heads, feats, width)  10.8 us
    unnamed x51, local copies, waits for them, and re-layouts  8.65 us
    ppermute x2, starting transfers between devices, shifted(): return lax.ppermute(block, axis, route)  7.85 us
    dot_general x1, matrix products, local(): numerator = jnp.einsum('hts,shv->thv', weights, v_float, precision=high)  3.7 us
    dot_general x1, matrix products, local(): jnp.einsum('hft,hfv->thv', phi_query, state_in, precision=high)  3.69 us
  transfers between devices with their start and end apart: 6, of which 4 were waited for; matrix products, arithmetic and copies ran while one was open for 25% of the time, Pallas kernels for 0%

profile of v11, /device:TPU:32, one launch (start us, length us, event | category | flops | bytes accessed | tf_op | source)
XLA Modules:
  0.0 158.2 jit_solution(11028056498021341090)
XLA Ops:
  0.6 0.7 slice.80
  1.4 3.5 %collective-permute-start = (bf16[2,1024]{1,0:T(2,128)(2,1)S(1)}, bf16[2,1024]{1,0:T(2,128)(2,1)S(1)}, u32[]{:S(2)}, u32[]{:S(2)}) collective-permute-start(bf16[2,1024]{1,0:T(2,128)(2,1)S(1)} %slice.80), channel_id=1, source_target_pairs={{0,8},{8,16},{16,24},{24,32},{32,40},{40,48},{48,56},{56,64},{64,7... | collective-permute-start | bytes 12296 | tf_op jit(solution)/shard_map/ppermute | solution.py:23
  4.9 0.7 broadcast_add_fusion.3
  5.6 0.8 fusion.105
  6.4 0.7 copy.108
  7.4 0.2 fusion.88
  7.6 0.7 compare_select_fusion
  8.3 0.6 fusion.107
  8.9 0.6 compare_convert_fusion.4
  9.5 0.6 fusion.106
  10.1 0.9 copy.109
  11.0 0.9 copy.110
  12.0 1.3 convolution_bitcast_fusion.1
  13.4 0.5 convolution_bitcast_fusion
  14.0 2.7 %compare_convert_fusion.1 = (f32[256]{0:T(256)S(1)}, f32[256]{0:T(256)}, f32[256]{0:T(256)S(1)}, f32[256]{0:T(256)S(1)}, f32[256]{0:T(256)S(1)}, /*index=5*/f32[256]{0:T(256)S(1)}, f32[256]{0:T(256)S(1)}) fusion(s32[256]{0:T(256)S(1)} %get-tuple-element.45, s32[258]{0:T(512)S(1)} %get-tuple-element.73, s32[]{:T(128)} %bitcast.31, s32[]{:T(128)} %bitcast.17, ...), kind=kLoop, calls=%fused_computation.136 | loop fusion | flops 3584 | bytes 12300 | tf_op jit(solution)/shard_map/convert_element_type | solution.py:219
  16.6 1.9 %multiply_reduce_fusion = (f32[8,160]{1,0:T(8,128)S(1)}, f32[8,160,256]{2,1,0:T(8,128)}, f32[8,160,256]{2,1,0:T(8,128)}) fusion(f32[256]{0:T(256)S(1)} %get-tuple-element.69, f32[160]{0:T(256)S(1)} %copy-done.15, f32[2,8,160,256]{3,2,1,0:T(8,128)S(1)} %convolution_bitcast_fusion.1, f32[160]{0:T(256)S(1)} %copy-done.16, f32[160]{0:T(256)S(1)} %copy-done.14, ...), kind=kLoop, calls=%fused_computation.44 | loop fusion | flops 3275520 | bytes 7872384 | tf_op jit(solution)/shard_map/reduce_sum | solution.py:164
  18.5 2.5 %fusion.61 = bf16[32,8,8,128]{3,2,1,0:T(8,128)(2,1)S(1)} fusion(bf16[256,1024]{1,0:T(8,128)(2,1)} %param.23, f32[256]{0:T(256)S(1)} %get-tuple-element.71, bf16[256,1024]{1,0:T(8,128)(2,1)} %param.22, bf16[2,1024]{1,0:T(2,128)(2,1)S(1)} %collective-permute-done, f32[1024]{0:T(1024)S(1)} %bitcast.188, f32[256]{0:T(256)S(1)} %get-tuple-element.72, ...), kind=kLoop, calls=%fused_computation.87 | loop fusion | flops 5767168 | bytes 1591296
  21.1 0.5 fusion.25
  21.6 0.9 copy-done.5
  22.5 11.1 %all-to-all-start = ((f32[32,40,128]{2,1,0:T(8,128)}), f32[32,40,128]{2,1,0:T(8,128)}, u32[]{:S(2)}, u32[]{:S(2)}) async-start(f32[32,40,128]{2,1,0:T(8,128)} %bitcast.167), calls=%async_computation | async-start | bytes 1310720 | tf_op jit(solution)/shard_map/all_to_all | solution.py:102
  33.6 0.2 convert_reduce_fusion.2
  34.2 0.7 gather_fusion.1
  34.9 0.7 gather_fusion
  35.7 2.0 %fusion.58 = (f32[8,256]{1,0:T(8,128)S(1)}, f32[8,256,256]{1,2,0:T(8,128)}) fusion(pred[256,256]{0,1:T(8,128)(4,1)S(1)} %fusion.70, bf16[256,8,16]{0,2,1:T(8,128)(2,1)S(1)} %bitcast.177, bf16[256,8,16]{0,2,1:T(8,128)(2,1)S(1)} %bitcast.174), kind=kOutput, calls=%fused_computation.82 | convolution fusion | flops 20445184 | bytes 2301952 | tf_op jit(solution)/shard_map/thd,shd->hts/dot_general | solution.py:146
  37.7 15.5 %all-to-all-done = f32[32,40,128]{2,1,0:T(8,128)} async-done(((f32[32,40,128]{2,1,0:T(8,128)}), f32[32,40,128]{2,1,0:T(8,128)}, u32[]{:S(2)}, u32[]{:S(2)}) %all-to-all-start) | async-done | bytes 655392 | tf_op jit(solution)/shard_map/all_to_all | solution.py:102
  53.2 1.5 fusion.53
  54.7 1.2 copy.116
  55.9 5.5 %all-to-all-start.1 = ((f32[32,40,128]{2,1,0:T(8,128)}), f32[32,40,128]{2,1,0:T(8,128)}, u32[]{:S(2)}, u32[]{:S(2)}) async-start(f32[32,40,128]{2,1,0:T(8,128)} %copy.116), calls=%async_computation.1 | async-start | bytes 1310720 | tf_op jit(solution)/shard_map/all_to_all | solution.py:105
  61.6 1.2 gather_fusion.3
  62.9 1.2 gather_fusion.2
  64.1 2.2 %copy.117 = f32[256,1024]{0,1:T(8,128)} copy(bf16[256,1024]{1,0:T(8,128)(2,1)} %param.26) | data formatting | bytes 1572864 | tf_op jit(solution)/shard_map/reshape | solution.py:177
  66.3 3.7 %fusion.59 = f32[8,128,256]{2,1,0:T(8,128)} fusion(f32[8,256,256]{1,2,0:T(8,128)} %get-tuple-element.80, pred[256,256]{0,1:T(8,128)(4,1)S(1)} %fusion.70, bf16[32,8,8,128]{3,2,1,0:T(8,128)(2,1)S(1)} %fusion.61), kind=kOutput, calls=%fused_computation.83 | convolution fusion | flops 405798912 | bytes 3735552 | tf_op jit(solution)/shard_map/hts,shv->thv/dot_general | solution.py:157
  70.0 10.3 %all-to-all-done.1 = f32[32,40,128]{2,1,0:T(8,128)} async-done(((f32[32,40,128]{2,1,0:T(8,128)}), f32[32,40,128]{2,1,0:T(8,128)}, u32[]{:S(2)}, u32[]{:S(2)}) %all-to-all-start.1) | async-done | bytes 655392 | tf_op jit(solution)/shard_map/all_to_all | solution.py:105
  80.2 0.9 slice_bitcast_fusion.5
  81.1 1.7 %fusion.78 = f32[8,1,256]{2,1,0:T(1,128)S(1)} fusion(f32[8,160,256]{2,1,0:T(8,128)} %get-tuple-element.65, f32[8,160,1]{1,0,2:T(8,128)S(1)} %get-tuple-element.59), kind=kOutput, calls=%fused_computation.121 | convolution fusion | flops 1966080 | bytes 1324032 | tf_op jit(solution)/shard_map/hft,hf->th/dot_general | solution.py:172
  82.9 3.7 %multiply_reduce_fusion.1 = (f32[256,8]{0,1:T(8,128)S(1)}, bf16[256,8,128]{0,2,1:T(8,128)(2,1)}) fusion(f32[256,1024]{0,1:T(8,128)} %copy.117, f32[256,8]{0,1:T(8,128)S(1)} %bitcast_add_fusion, f32[8,128,256]{2,1,0:T(8,128)} %fusion.59, f32[8,160,128]{2,1,0:T(8,128)} %bitcast.20, f32[8,160,256]{2,1,0:T(8,128)S(1)} %copy-done.1, f32[256]{0:T(256)S(1)} %get-tuple-element.70), kind=kOutput, calls=%fused_computation.71 | convolution fusion | flops 253229056 | bytes 4604928 | tf_op jit(solution)/shard_map/hft,hfv->thv/dot_general | solution.py:169
  86.6 0.6 fusion.21
  87.2 0.6 copy-done.8
  87.8 1.6 %fusion.23 = f32[8,160,128]{2,1,0:T(8,128)} fusion(f32[8,160,256]{2,1,0:T(8,128)S(1)} %copy-done.1, f32[256]{0:T(256)S(1)} %get-tuple-element.68, f32[256,8,128]{0,2,1:T(8,128)S(1)} %bitcast.169, f32[256,8]{0,1:T(8,128)S(1)} %bitcast_add_fusion), kind=kOutput, calls=%fused_computation.42 | convolution fusion | flops 252248064 | bytes 3023872 | tf_op jit(solution)/shard_map/hft,thv->hfv/dot_general | solution.py:182
  89.4 0.6 constant_dynamic-update-slice_fusion
  90.0 5.5 %all-to-all-start.2 = ((f32[32,40,128]{2,1,0:T(8,128)}), f32[32,40,128]{2,1,0:T(8,128)}, u32[]{:S(2)}, u32[]{:S(2)}) async-start(f32[32,40,128]{2,1,0:T(8,128)} %bitcast.172), calls=%async_computation.2 | async-start | bytes 1310720 | tf_op jit(solution)/shard_map/all_to_all | solution.py:102
  95.5 3.4 %fusion.30 = (f32[8,160,256]{2,1,0:T(8,128)S(1)}, f32[8,160,256]{2,1,0:T(8,128)S(1)}) fusion(f32[2,8,160,256]{3,2,1,0:T(8,128)} %copy-done.2, f32[160]{0:T(256)S(1)} %copy-done.15, f32[160]{0:T(256)S(1)} %copy-done.16, f32[160]{0:T(256)S(1)} %copy-done.14, f32[8,256]{1,0:T(8,128)S(1)} %get-tuple-element.56, f32[8,160]{1,0:T(8,128)S(1)} %get-tuple-element.58, ...), kind=kOutput, calls=%fused_computation.50 | convolution fusion | flops 254541824 | bytes 6971264 | tf_op jit(solution)/shard_map/hfv,thv->hft/dot_general | solution.py:194
  99.0 0.7 fusion
  99.8 0.4 copy-done.9
  100.2 1.1 multiply_select_fusion
  101.3 0.7 fusion.34
  102.0 0.5 fusion.36
  102.5 0.4 copy-done.13
  102.8 2.5 %convolution_bitcast_fusion.2 = f32[256,8,128]{0,2,1:T(8,128)} fusion(f32[8,256,256]{1,2,0:T(8,128)S(1)} %copy-done.20, pred[256,256]{0,1:T(8,128)(4,1)S(1)} %copy-done.13, f32[256,8,128]{0,2,1:T(8,128)S(1)} %bitcast.171, f32[256,8]{0,1:T(8,128)S(1)} %bitcast_add_fusion), kind=kOutput, calls=%fused_computation.25 | convolution fusion | flops 406061056 | bytes 4268032 | tf_op jit(solution)/shard_map/hts,thv->shv/dot_general | solution.py:185
  105.3 9.0 %all-to-all-done.2 = f32[32,40,128]{2,1,0:T(8,128)} async-done(((f32[32,40,128]{2,1,0:T(8,128)}), f32[32,40,128]{2,1,0:T(8,128)}, u32[]{:S(2)}, u32[]{:S(2)}) %all-to-all-start.2) | async-done | bytes 655392 | tf_op jit(solution)/shard_map/all_to_all | solution.py:102
  114.3 1.5 fusion.51
  115.8 1.2 copy.128
  117.0 5.4 %all-to-all-start.3 = ((f32[32,40,128]{2,1,0:T(8,128)}), f32[32,40,128]{2,1,0:T(8,128)S(1)}, u32[]{:S(2)}, u32[]{:S(2)}) async-start(f32[32,40,128]{2,1,0:T(8,128)} %copy.128), calls=%async_computation.3 | async-start | bytes 1310720 | tf_op jit(solution)/shard_map/all_to_all | solution.py:105
  122.4 2.0 %copy.132 = bf16[256,1024]{1,0:T(8,128)(2,1)} copy(bf16[256,1024]{0,1:T(8,128)(2,1)} %bitcast.179) | data formatting | bytes 1048576
  124.4 0.7 copy.133
  125.1 15.8 %all-to-all-done.3 = f32[32,40,128]{2,1,0:T(8,128)S(1)} async-done(((f32[32,40,128]{2,1,0:T(8,128)}), f32[32,40,128]{2,1,0:T(8,128)S(1)}, u32[]{:S(2)}, u32[]{:S(2)}) %all-to-all-start.3) | async-done | bytes 655392 | tf_op jit(solution)/shard_map/all_to_all | solution.py:105
  141.0 3.7 %fusion.13 = f32[256,8,128]{0,2,1:T(8,128)} fusion(f32[256,8,128]{0,2,1:T(8,128)} %convolution_bitcast_fusion.2, f32[8,160,128]{2,1,0:T(8,128)S(1)} %bitcast.164, f32[8,160,256]{2,1,0:T(8,128)} %get-tuple-element.47, f32[256]{0:T(256)S(1)} %get-tuple-element.44), kind=kOutput, calls=%fused_computation.24 | convolution fusion | flops 252182528 | bytes 4064256 | tf_op jit(solution)/shard_map/hfs,hfv->shv/dot_general | solution.py:201
  144.7 2.6 %copy.130 = f32[256,1024]{1,0:T(8,128)} copy(f32[256,1024]{0,1:T(8,128)} %bitcast.166) | data formatting | bytes 2097152 | tf_op jit(solution)/shard_map/reshape | solution.py:211
  147.3 2.1 %fusion.28 = (f32[8,160,256]{2,1,0:T(8,128)S(1)}, f32[8,160,256]{2,1,0:T(8,128)S(1)}) fusion(f32[2,8,160,256]{3,2,1,0:T(8,128)S(1)} %convolution_bitcast_fusion.1, f32[160]{0:T(256)S(1)} %copy-done.15, f32[160]{0:T(256)S(1)} %copy-done.16, f32[160]{0:T(256)S(1)} %copy-done.14, f32[8,160]{1,0:T(8,128)S(1)} %bitcast.191, f32[8,160,128]{2,1,0:T(8,128)S(1)} %bitcast.165, ...), kind=kOutput, calls=%fused_computation.48 | convolution fusion | flops 253952000 | bytes 6430592 | tf_op jit(solution)/shard_map/hfv,shv->hfs/dot_general | solution.py:205
  149.4 1.7 %multiply_convert_fusion = (bf16[256,1024]{1,0:T(8,128)(2,1)}, f32[256,1024]{1,0:T(8,128)S(1)}) fusion(f32[256,1024]{1,0:T(8,128)S(1)} %copy-done.4, bf16[256,1024]{1,0:T(8,128)(2,1)S(1)} %copy-done.7, f32[256]{0:T(256)S(1)} %get-tuple-element.71, bf16[256,1024]{1,0:T(8,128)(2,1)S(1)} %copy-done.6, bf16[2,1024]{1,0:T(2,128)(2,1)S(1)} %collective-permute-done, ...), kind=kLoop, calls=%fused_computation.70 | loop fusion | flops 6815744 | bytes 3688448 | tf_op jit(solution)/shard_map/convert_element_type | solution.py:212
  151.1 4.4 %collective-permute-start.1 = (f32[2,1024]{1,0:T(2,128)S(1)}, f32[2,1024]{1,0:T(2,128)S(1)}, u32[]{:S(2)}, u32[]{:S(2)}) collective-permute-start(f32[2,1024]{1,0:T(2,128)S(1)} %slice.124), channel_id=1, source_target_pairs={{8,0},{16,8},{24,16},{32,24},{40,32},{48,40},{56,48},{64,56},{72,6... | collective-permute-start | bytes 24584 | tf_op jit(solution)/shard_map/ppermute | solution.py:23
  155.5 0.7 fusion.40
  156.2 0.7 copy.134
  156.9 1.2 fusion.48
  (79 shorter events, 1.2 us)
Async XLA Ops:
  1.4 17.2 %collective-permute-start = (bf16[2,1024]{1,0:T(2,128)(2,1)S(1)}, bf16[2,1024]{1,0:T(2,128)(2,1)S(1)}, u32[]{:S(2)}, u32[]{:S(2)}) collective-permute-start(bf16[2,1024]{1,0:T(2,128)(2,1)S(1)} %slice.80), channel_id=1, source_target_pairs={{0,8},{8,16},{16,24},{24,32},{32,40},{40,48},{48,56},{56,64},{64,7... | collective-permute-start | bytes 12296 | tf_op jit(solution)/shard_map/ppermute | solution.py:23
  12.0 1.3 copy-start.11
  13.3 3.3 %copy-start.14 = (f32[160]{0:T(256)S(1)}, f32[160]{0:T(256)}, u32[]{:S(2)}) copy-start(f32[160]{0:T(256)} %constant.80.clone) | copy-start | bytes 1924
  13.3 3.3 %copy-start.15 = (f32[160]{0:T(256)S(1)}, f32[160]{0:T(256)}, u32[]{:S(2)}) copy-start(f32[160]{0:T(256)} %constant.79.clone) | copy-start | bytes 1924
  13.3 3.3 %copy-start.16 = (f32[160]{0:T(256)S(1)}, f32[160]{0:T(256)}, u32[]{:S(2)}) copy-start(f32[160]{0:T(256)} %constant.78.clone) | copy-start | bytes 1924
  13.9 4.6 %copy-start.2 = (f32[2,8,160,256]{3,2,1,0:T(8,128)}, f32[2,8,160,256]{3,2,1,0:T(8,128)S(1)}, u32[]{:S(2)}) copy-start(f32[2,8,160,256]{3,2,1,0:T(8,128)S(1)} %convolution_bitcast_fusion) | copy-start | bytes 7864324
  18.5 2.5 %copy-start = (f32[8,160,256]{2,1,0:T(8,128)S(1)}, f32[8,160,256]{2,1,0:T(8,128)}, u32[]{:S(2)}) copy-start(f32[8,160,256]{2,1,0:T(8,128)} %get-tuple-element.47) | copy-start | bytes 3932164
  21.0 78.7 %copy-start.3 = (bf16[32,8,8,128]{3,2,1,0:T(8,128)(2,1)}, bf16[32,8,8,128]{3,2,1,0:T(8,128)(2,1)S(1)}, u32[]{:S(2)}) copy-start(bf16[32,8,8,128]{3,2,1,0:T(8,128)(2,1)S(1)} %fusion.61) | copy-start | bytes 1572868
  21.6 0.9 copy-start.5
  22.5 30.7 %all-to-all-start = ((f32[32,40,128]{2,1,0:T(8,128)}), f32[32,40,128]{2,1,0:T(8,128)}, u32[]{:S(2)}, u32[]{:S(2)}) async-start(f32[32,40,128]{2,1,0:T(8,128)} %bitcast.167), calls=%async_computation | async-start | bytes 1310720 | tf_op jit(solution)/shard_map/all_to_all | solution.py:102
  35.7 64.0 %copy-start.12 = (pred[256,256]{0,1:T(8,128)(4,1)}, pred[256,256]{0,1:T(8,128)(4,1)S(1)}, u32[]{:S(2)}) copy-start(pred[256,256]{0,1:T(8,128)(4,1)S(1)} %fusion.70) | copy-start | bytes 196612
  55.9 24.4 %all-to-all-start.1 = ((f32[32,40,128]{2,1,0:T(8,128)}), f32[32,40,128]{2,1,0:T(8,128)}, u32[]{:S(2)}, u32[]{:S(2)}) async-start(f32[32,40,128]{2,1,0:T(8,128)} %copy.116), calls=%async_computation.1 | async-start | bytes 1310720 | tf_op jit(solution)/shard_map/all_to_all | solution.py:105
  80.2 2.6 %copy-start.1 = (f32[8,160,256]{2,1,0:T(8,128)S(1)}, f32[8,160,256]{2,1,0:T(8,128)}, u32[]{:S(2)}) copy-start(f32[8,160,256]{2,1,0:T(8,128)} %get-tuple-element.65) | copy-start | bytes 3932164
  86.6 1.2 copy-start.8
  90.0 24.3 %all-to-all-start.2 = ((f32[32,40,128]{2,1,0:T(8,128)}), f32[32,40,128]{2,1,0:T(8,128)}, u32[]{:S(2)}, u32[]{:S(2)}) async-start(f32[32,40,128]{2,1,0:T(8,128)} %bitcast.172), calls=%async_computation.2 | async-start | bytes 1310720 | tf_op jit(solution)/shard_map/all_to_all | solution.py:102
  95.5 3.5 %copy-start.10 = (f32[320,16,1]{0,1,2:T(8,128)S(1)}, f32[320,16,1]{0,1,2:T(8,128)}, u32[]{:S(2)}) copy-start(f32[320,16,1]{0,1,2:T(8,128)} %constant.87) | copy-start | bytes 61444
  95.5 4.3 %copy-start.20 = (f32[8,256,256]{1,2,0:T(8,128)S(1)}, f32[8,256,256]{1,2,0:T(8,128)}, u32[]{:S(2)}) copy-start(f32[8,256,256]{1,2,0:T(8,128)} %get-tuple-element.80) | copy-start | bytes 6291460
  99.0 1.2 copy-start.9
  102.0 0.8 copy-start.13
  102.8 11.4 %copy-start.18 = (s32[32]{0:T(128)S(1)}, s32[32]{0:T(128)}, u32[]{:S(2)}) copy-start(s32[32]{0:T(128)} %gather_fusion.3) | copy-start | bytes 388
  102.8 11.4 %copy-start.19 = (s32[32]{0:T(128)S(1)}, s32[32]{0:T(128)}, u32[]{:S(2)}) copy-start(s32[32]{0:T(128)} %gather_fusion.2) | copy-start | bytes 388
  117.0 24.0 %all-to-all-start.3 = ((f32[32,40,128]{2,1,0:T(8,128)}), f32[32,40,128]{2,1,0:T(8,128)S(1)}, u32[]{:S(2)}, u32[]{:S(2)}) async-start(f32[32,40,128]{2,1,0:T(8,128)} %copy.128), calls=%async_computation.3 | async-start | bytes 1310720 | tf_op jit(solution)/shard_map/all_to_all | solution.py:105
  147.3 2.1 %copy-start.4 = (f32[256,1024]{1,0:T(8,128)S(1)}, f32[256,1024]{1,0:T(8,128)}, u32[]{:S(2)}) copy-start(f32[256,1024]{1,0:T(8,128)} %copy.130) | copy-start | bytes 3145732
  147.3 2.1 %copy-start.6 = (bf16[256,1024]{1,0:T(8,128)(2,1)S(1)}, bf16[256,1024]{1,0:T(8,128)(2,1)}, u32[]{:S(2)}) copy-start(bf16[256,1024]{1,0:T(8,128)(2,1)} %param.22) | copy-start | bytes 1572868
  147.3 2.1 %copy-start.7 = (bf16[256,1024]{1,0:T(8,128)(2,1)S(1)}, bf16[256,1024]{1,0:T(8,128)(2,1)}, u32[]{:S(2)}) copy-start(bf16[256,1024]{1,0:T(8,128)(2,1)} %param.23) | copy-start | bytes 1572868
  151.1 5.9 %collective-permute-start.1 = (f32[2,1024]{1,0:T(2,128)S(1)}, f32[2,1024]{1,0:T(2,128)S(1)}, u32[]{:S(2)}, u32[]{:S(2)}) collective-permute-start(f32[2,1024]{1,0:T(2,128)S(1)} %slice.124), channel_id=1, source_target_pairs={{8,0},{16,8},{24,16},{32,24},{40,32},{48,40},{56,48},{64,56},{72,6... | collective-permute-start | bytes 24584 | tf_op jit(solution)/shard_map/ppermute | solution.py:23
  155.4 1.5 copy-start.17
